TPU v7x, 768 devices: a whole 4x8x12 slice. The times are simulated.
768 devices in a mesh: vert: 24 (over z, core), feat: 32 (over y, x).
Axes of the slice: x: 4, y: 8, z: 12, core: 2. Of those that a mesh axis runs over, the one named last changes fastest.
Arguments:
- states: bfloat16 [4, 256, 98304], P(None, 'feat', 'vert'), may hold values from -6 to 6
- depth_weight: float32 [4, 256], P(None, 'feat'), may hold values from -1 to 1
- tile_values: bfloat16 [24, 256, 128, 128], P('vert'), may hold values from -0.1875 to 0.1875
- tile_dst: int32 [24, 256], P('vert'), may hold values from 0 to 31
- tile_src: int32 [24, 256], P('vert'), may hold values from 0 to 43
- tile_count: int32 [24], P('vert'), may hold values from 64 to 256, as said below
- send_rows: int32 [24, 24, 64], P('vert'), may hold values from 0 to 4095
- weight: bfloat16 [256, 256], replicated, may hold values from -0.375 to 0.375
- bias_vec: float32 [256], P('feat'), may hold values from -3 to 3
- cotangent: bfloat16 [256, 98304], P('feat', 'vert'), may hold values from -6 to 6
Outputs:
- layer_out: bfloat16 [256, 98304], P('feat', 'vert')
- grad_states: bfloat16 [4, 256, 98304], P(None, 'feat', 'vert')
- grad_weight: float32 [256, 256], P('feat')
- grad_bias: float32 [256], P('feat')
- grad_depth: float32 [4, 256], P(None, 'feat')
Inputs may be any that keep to these rules, and one draw needn't show every extreme that they name: `tile_count`: at least 64 tiles in every partition, and exactly 256 in some partition.
All inputs are finite; a program needn't handle non-finite values.
Results may differ from a plain program's by a relative error of at most 0.024.
Values may be sent and summed in bfloat16 or wider, within the bound.
No kernel may reach another device: no remote copies, remote signals or barrier semaphores. Data moves between devices by JAX's collectives and lax.ppermute only.
A program may use at most 64 MiB of HBM per device.

v0:
```python
import math

import jax
import jax.numpy as jnp
from jax import lax
from jax.sharding import PartitionSpec as P


def tile_forward(extended, tile_grp, dst_grp, src_grp, live_mask, row_blocks):
    picked = jnp.take(extended, src_grp, axis=1)
    products = jnp.einsum("dtc,trc->dtr", picked, tile_grp, preferred_element_type=jnp.float32)
    onehot = (
        (dst_grp[:, None] == jnp.arange(row_blocks, dtype=jnp.int32)[None, :]) & live_mask[:, None]
    ).astype(jnp.float32)
    return jnp.einsum("dtr,tn->dnr", products, onehot)


def tile_backward(grad_blocks, tile_grp, dst_grp, src_grp, live_mask, src_blocks):
    picked = jnp.take(grad_blocks, dst_grp, axis=1)
    products = jnp.einsum("dtr,trc->dtc", picked, tile_grp, preferred_element_type=jnp.float32)
    onehot = (
        (src_grp[:, None] == jnp.arange(src_blocks, dtype=jnp.int32)[None, :]) & live_mask[:, None]
    ).astype(jnp.float32)
    return jnp.einsum("dtc,ts->dsc", products, onehot)


def over_tiles(kernel, source, tile_values, tile_dst, tile_src, tile_total, out_blocks):
    capacity = tile_values.shape[0]
    live_mask = jnp.arange(capacity, dtype=jnp.int32) < tile_total
    return kernel(source, tile_values, tile_dst, tile_src, live_mask, out_blocks)


def local(
    states,
    depth_weight,
    tile_values,
    tile_dst,
    tile_src,
    tile_count,
    send_rows,
    weight,
    bias_vec,
    cotangent,
):
    channels = states.shape[1]
    row_count = states.shape[2]
    block_size = tile_values.shape[2]
    row_blocks = row_count // block_size
    my_tiles = tile_values[0]
    my_dst = tile_dst[0]
    my_src = tile_src[0]
    tile_total = tile_count[0]
    my_send = send_rows[0]
    section_count = my_send.shape[0]
    halo_width = my_send.shape[1]
    vert_count = lax.axis_size("vert")
    panel_start = lax.axis_index("feat") * channels
    src_blocks = (row_count + section_count * halo_width) // block_size
    norm_scale = 1.0 / math.sqrt(vert_count * row_count)
    weight_rows = lax.dynamic_slice_in_dim(weight, panel_start, channels, 0)
    mixed_state = jnp.sum(depth_weight[:, :, None] * states, axis=0).astype(jnp.bfloat16)
    outgoing = mixed_state[:, my_send]
    incoming = lax.all_to_all(outgoing, "vert", split_axis=1, concat_axis=1, tiled=True)
    extended = jnp.concatenate([mixed_state, incoming.reshape(channels, -1)], axis=1)
    extended = extended.reshape(channels, src_blocks, block_size)
    aggregated = over_tiles(
        tile_forward, extended, my_tiles, my_dst, my_src, tile_total, row_blocks
    )
    aggregated = aggregated.reshape(channels, row_count).astype(jnp.bfloat16)
    pre_act = lax.psum_scatter(
        lax.dot_general(
            weight_rows, aggregated, (((0,), (0,)), ((), ())), preferred_element_type=jnp.float32
        ).astype(jnp.bfloat16),
        "feat",
        scatter_dimension=0,
        tiled=True,
    ).astype(jnp.float32)
    pre_act = pre_act + bias_vec[:, None]
    sigmoid_pre = jax.nn.sigmoid(pre_act)
    layer_out = (pre_act * sigmoid_pre).astype(jnp.bfloat16)
    grad_pre = (
        cotangent.astype(jnp.float32) * sigmoid_pre * (1.0 + pre_act * (1.0 - sigmoid_pre))
    ).astype(jnp.bfloat16)
    piece = lax.all_gather(grad_pre, "feat", axis=0, tiled=True)
    agg_total = jnp.dot(weight_rows, piece, preferred_element_type=jnp.float32)
    terms_now = lax.dot_general(
        aggregated, piece, (((1,), (1,)), ((), ())), preferred_element_type=jnp.float32
    )
    grad_agg = agg_total.astype(jnp.bfloat16)
    grad_blocks = grad_agg.reshape(channels, row_blocks, block_size)
    spread_out = over_tiles(
        tile_backward, grad_blocks, my_tiles, my_dst, my_src, tile_total, src_blocks
    )
    spread_out = spread_out.reshape(channels, src_blocks * block_size)
    halo_terms = (
        spread_out[:, row_count:].astype(jnp.bfloat16).reshape(channels, section_count, halo_width)
    )
    returned = lax.all_to_all(halo_terms, "vert", split_axis=1, concat_axis=1, tiled=True)
    grad_mixed = spread_out[:, :row_count].at[:, my_send].add(returned.astype(jnp.float32))
    grad_states = (depth_weight[:, :, None] * grad_mixed[None]).astype(jnp.bfloat16)
    bias_terms = jnp.sum(grad_pre.astype(jnp.float32), axis=1)
    depth_terms = jnp.sum(states * grad_mixed[None], axis=2)
    weight_sum, bias_sum, depth_sum = lax.psum((terms_now, bias_terms, depth_terms), "vert")
    return (
        layer_out,
        grad_states,
        weight_sum * norm_scale,
        bias_sum * norm_scale,
        depth_sum * norm_scale,
    )


def solution(mesh):
    placed = (
        P(None, "feat", "vert"),
        P(None, "feat"),
        P("vert", None, None, None),
        P("vert", None),
        P("vert", None),
        P("vert"),
        P("vert", None, None),
        P(),
        P("feat"),
        P("feat", "vert"),
    )
    return jax.shard_map(
        local,
        mesh=mesh,
        in_specs=placed,
        out_specs=(
            P("feat", "vert"),
            P(None, "feat", "vert"),
            P("feat", None),
            P("feat"),
            P(None, "feat"),
        ),
        check_vma=False,
    )
```

profile of v0, /device:TPU:1, one launch (start us, length us, event | category | flops | bytes accessed | tf_op | source)
XLA Modules:
  0.0 480.8 jit_solution(12318239589021220795)
XLA Ops:
  7.2 0.0 copy-start
  7.2 0.8 compare_select_fusion
  7.9 0.1 reshape.139
  8.0 1.1 fusion.14
  9.1 0.5 copy.41
  9.6 3.2 gather_fusion
  12.8 0.2 copy.42
  13.0 0.7 reshape.173
  13.7 16.7 %all-to-all-start = ((bf16[24,2,256]{2,1,0:T(2,128)(2,1)}), bf16[24,2,256]{2,1,0:T(2,128)(2,1)S(1)}, u32[]{:S(2)}, u32[]{:S(2)}) async-start(bf16[24,2,256]{2,1,0:T(2,128)(2,1)} %reshape.173), calls=%async_computation | async-start | bytes 49152 | tf_op jit(solution)/shard_map/all_to_all | solution.py:63
  30.4 0.0 reduce-scatter.2.cloned.1.call-start
  31.2 9.0 %all-to-all-done = bf16[24,2,256]{2,1,0:T(2,128)(2,1)S(1)} async-done(((bf16[24,2,256]{2,1,0:T(2,128)(2,1)}), bf16[24,2,256]{2,1,0:T(2,128)(2,1)S(1)}, u32[]{:S(2)}, u32[]{:S(2)}) %all-to-all-start) | async-done | bytes 24608 | tf_op jit(solution)/shard_map/all_to_all | solution.py:63
  40.2 0.1 reshape.174
  40.3 0.1 reshape.132
  40.4 0.8 gather_fusion.1
  41.2 0.0 copy-start.5
  41.3 7.8 %fusion.4 = bf16[8,256,128]{2,0,1:T(8,128)(2,1)S(1)} fusion(bf16[1,256,128,128]{3,2,1,0:T(8,128)(2,1)} %param.12, bf16[256,8,128]{2,1,0:T(8,128)(2,1)S(1)} %gather_fusion.1, pred[256]{0:T(512)(128)(4,1)S(1)} %compare_and_fusion.1), kind=kOutput, calls=%fused_computation.10 | convolution fusion | flops 67371008 | bytes 9437440 | tf_op jit(solution)/shard_map/dtc,trc->dtr/dot_general | solution.py:11
  49.1 0.2 fusion.10
  49.3 0.0 copy-start.3
  49.3 0.0 copy-start.7
  49.3 2.1 convolution_convert_fusion
  51.4 0.0 reduce-scatter.2.cloned.1.call-update
  51.5 0.0 all-gather.2.cloned.1.call-start
  51.5 216.0 %reduce-scatter.2.cloned.1.call-done = bf16[8,4096]{1,0:T(8,128)(2,1)} async-done(((bf16[256,4096]{1,0:T(8,128)(2,1)}), bf16[8,4096]{1,0:T(8,128)(2,1)}) %reduce-scatter.2.cloned.1.call-update) | async-done | bytes 65552 | tf_op jit(solution)/shard_map/reduce_scatter | solution.py:70
  267.5 1.7 convert_reduce_fusion
  269.2 0.0 all-gather.2.cloned.1.call-update
  269.3 92.0 %all-gather.2.cloned.1.call-done = bf16[256,4096]{1,0:T(8,128)(2,1)} async-done(((bf16[8,4096]{1,0:T(8,128)(2,1)}), bf16[256,4096]{1,0:T(8,128)(2,1)}) %all-gather.2.cloned.1.call-update) | async-done | bytes 2097168 | tf_op jit(solution)/shard_map/all_gather | solution.py:84
  361.3 2.0 fusion.11
  363.3 0.8 gather_fusion.2
  364.1 5.9 %fusion.7 = bf16[8,256,128]{2,0,1:T(8,128)(2,1)S(1)} fusion(bf16[1,256,128,128]{3,2,1,0:T(8,128)(2,1)} %param.12, bf16[256,8,128]{2,1,0:T(8,128)(2,1)S(1)} %gather_fusion.2, pred[256]{0:T(512)(128)(4,1)S(1)} %compare_and_fusion), kind=kOutput, calls=%fused_computation.11 | convolution fusion | flops 67371008 | bytes 9437440 | tf_op jit(solution)/shard_map/dtr,trc->dtc/dot_general | solution.py:20
  370.0 0.2 convolution_bitcast_fusion
  370.2 0.1 copy.70
  370.2 0.1 reshape.136
  370.4 0.7 reshape.175
  371.1 14.7 %all-to-all-start.1 = ((bf16[24,2,256]{2,1,0:T(2,128)(2,1)}), bf16[24,2,256]{2,1,0:T(2,128)(2,1)S(1)}, u32[]{:S(2)}, u32[]{:S(2)}) async-start(bf16[24,2,256]{2,1,0:T(2,128)(2,1)} %reshape.175), calls=%async_computation.2 | async-start | bytes 49152 | tf_op jit(solution)/shard_map/all_to_all | solution.py:98
  385.7 0.6 fusion.24
  386.4 0.6 copy.53
  387.0 8.5 %all-to-all-done.1 = bf16[24,2,256]{2,1,0:T(2,128)(2,1)S(1)} async-done(((bf16[24,2,256]{2,1,0:T(2,128)(2,1)}), bf16[24,2,256]{2,1,0:T(2,128)(2,1)S(1)}, u32[]{:S(2)}, u32[]{:S(2)}) %all-to-all-start.1) | async-done | bytes 24608 | tf_op jit(solution)/shard_map/all_to_all | solution.py:98
  395.5 0.1 reshape.176
  395.6 0.3 copy.51
  395.9 0.0 copy-start.2
  395.9 0.0 copy-start.4
  395.9 9.5 %scatter_fusion = f32[8,4096]{0,1:T(8,128)S(1)} fusion(f32[8,4096]{0,1:T(8,128)S(1)} %copy.53, s32[1536]{0:T(1024)S(1)} %reshape.139, f32[1536,8]{1,0:T(8,128)S(1)} %bitcast.73), kind=kCustom, calls=%fused_computation.3 | custom fusion | flops 12288 | bytes 153600 | tf_op jit(solution)/shard_map/scatter-add | solution.py:99
  405.5 0.6 copy.50
  406.0 0.9 fusion.15
  406.9 65.4 %all-reduce = (f32[8,256]{1,0:T(8,128)S(1)}, f32[8]{0:T(128)S(1)}, f32[4,8]{1,0:T(4,128)S(1)}) all-reduce(f32[8,256]{1,0:T(8,128)S(1)} %fusion.24, f32[8]{0:T(128)S(1)} %get-tuple-element.8, f32[4,8]{1,0:T(4,128)S(1)} %get-tuple-element.10), channel_id=1, replica_groups=mesh['vert'=24,'feat'=32] {'vert'}, use_global_device_ids=true, to_apply=%region_3.4 | all-reduce | flops 2088 | bytes 16704 | tf_op jit(solution)/shard_map/psum | solution.py:103
  472.3 0.6 broadcast_multiply_fusion
  472.9 0.5 broadcast_multiply_fusion.2
  473.4 0.6 broadcast_multiply_fusion.1
  (25 shorter events, 0.1 us)
Async XLA Ops:
  7.2 42.1 %copy-start = (bf16[256,256]{1,0:T(8,128)(2,1)S(1)}, bf16[256,256]{1,0:T(8,128)(2,1)}, u32[]{:S(2)}) copy-start(bf16[256,256]{1,0:T(8,128)(2,1)} %param.17) | copy-start | bytes 393220
  7.2 23.9 %copy-start.6 = (s32[1,256]{1,0:T(1,128)S(1)}, s32[1,256]{1,0:T(1,128)}, u32[]{:S(2)}) copy-start(s32[1,256]{1,0:T(1,128)} %param.14) | copy-start | bytes 3076
  13.7 26.5 %all-to-all-start = ((bf16[24,2,256]{2,1,0:T(2,128)(2,1)}), bf16[24,2,256]{2,1,0:T(2,128)(2,1)S(1)}, u32[]{:S(2)}, u32[]{:S(2)}) async-start(bf16[24,2,256]{2,1,0:T(2,128)(2,1)} %reshape.173), calls=%async_computation | async-start | bytes 49152 | tf_op jit(solution)/shard_map/all_to_all | solution.py:63
  30.4 237.1 %reduce-scatter.2.cloned.1.call-start = ((), (), s32[]{:S(2)}) async-start(), calls=%async_computation.3 | async-start | bytes 2162688 | tf_op jit(solution)/shard_map/reduce_scatter | solution.py:70
  41.2 7.9 %copy-start.5 = (s32[1,256]{1,0:T(1,128)S(1)}, s32[1,256]{1,0:T(1,128)}, u32[]{:S(2)}) copy-start(s32[1,256]{1,0:T(1,128)} %param.13) | copy-start | bytes 3076
  49.3 218.1 %copy-start.3 = (bf16[8,4096]{1,0:T(8,128)(2,1)S(1)}, bf16[8,4096]{1,0:T(8,128)(2,1)}, u32[]{:S(2)}) copy-start(bf16[8,4096]{1,0:T(8,128)(2,1)} %param.19) | copy-start | bytes 196612
  49.3 218.1 %copy-start.7 = (f32[8]{0:T(128)S(1)}, f32[8]{0:T(128)}, u32[]{:S(2)}) copy-start(f32[8]{0:T(128)} %param.18) | copy-start | bytes 100
  51.5 309.8 %all-gather.2.cloned.1.call-start = ((), (), s32[]{:S(2)}) async-start(), calls=%async_computation.4 | async-start | bytes 2162688 | tf_op jit(solution)/shard_map/all_gather | solution.py:84
  364.1 21.7 %copy-start.1 = (bf16[256,4096]{1,0:T(8,128)(2,1)S(1)}, bf16[256,4096]{1,0:T(8,128)(2,1)}, u32[]{:S(2)}) copy-start(bf16[256,4096]{1,0:T(8,128)(2,1)} %all-gather.2.cloned.1.call-done) | copy-start | bytes 6291460
  371.1 24.4 %all-to-all-start.1 = ((bf16[24,2,256]{2,1,0:T(2,128)(2,1)}), bf16[24,2,256]{2,1,0:T(2,128)(2,1)S(1)}, u32[]{:S(2)}, u32[]{:S(2)}) async-start(bf16[24,2,256]{2,1,0:T(2,128)(2,1)} %reshape.175), calls=%async_computation.2 | async-start | bytes 49152 | tf_op jit(solution)/shard_map/all_to_all | solution.py:98
  395.9 10.1 %copy-start.2 = (bf16[4,8,4096]{2,1,0:T(8,128)(2,1)S(1)}, bf16[4,8,4096]{2,1,0:T(8,128)(2,1)}, u32[]{:S(2)}) copy-start(bf16[4,8,4096]{2,1,0:T(8,128)(2,1)} %param.10) | copy-start | bytes 786436
  395.9 10.1 %copy-start.4 = (f32[4,8]{1,0:T(4,128)S(1)}, f32[4,8]{1,0:T(4,128)}, u32[]{:S(2)}) copy-start(f32[4,8]{1,0:T(4,128)} %param.11) | copy-start | bytes 388
Sparse Core Ops, SparseCore 0:
  51.6 215.8 reduce-scatter.1
  272.4 88.8 all-gather.1
where the time goes:
time: 483 us; the launch traced here: 481 us
  waiting for transfers between devices  325 us (67%)
  blocking collectives  65.4 us (14%)
  starting transfers between devices  31.4 us (7%)
  matrix products  18.8 us (4%)
  other arithmetic  15.7 us (3%)
  between operations  15 us (3%)
  local copies, waits for them, and re-layouts  9.02 us (2%)
    reduce_scatter x1, waiting for transfers between devices, local(): lax.psum_scatter(lax.dot_general(weight_rows, aggregated, (((0,), (0,)),...  216 us
    all_gather x1, waiting for transfers between devices, local(): piece = lax.all_gather(grad_pre, 'feat', axis=0, tiled=True)  92 us
    psum x1, blocking collectives, local(): lax.psum((terms_now, bias_terms, depth_terms), 'vert')  65.4 us
    all_to_all x1, starting transfers between devices, local(): lax.all_to_all(outgoing, 'vert', split_axis=1, concat_axis=1, tiled=True)  16.7 us
    all_to_all x1, starting transfers between devices, local(): lax.all_to_all(halo_terms, 'vert', split_axis=1, concat_axis=1, tiled=True)  14.7 us
  transfers between devices with their start and end apart: 4, of which 4 were waited for; matrix products, arithmetic and copies ran while one was open for 0% of the time, Pallas kernels for 0%

commit v1 on v0

--- a/solution.py
+++ b/solution.py
@@ -30,6 +30,14 @@
     return kernel(source, tile_values, tile_dst, tile_src, live_mask, out_blocks)
 
 
+def to_vertex_split(panel):
+    return lax.all_to_all(panel, "feat", split_axis=1, concat_axis=0, tiled=True)
+
+
+def to_channel_split(block):
+    return lax.all_to_all(block, "feat", split_axis=0, concat_axis=1, tiled=True)
+
+
 def local(
     states,
     depth_weight,
@@ -54,10 +62,17 @@
     section_count = my_send.shape[0]
     halo_width = my_send.shape[1]
     vert_count = lax.axis_size("vert")
-    panel_start = lax.axis_index("feat") * channels
     src_blocks = (row_count + section_count * halo_width) // block_size
     norm_scale = 1.0 / math.sqrt(vert_count * row_count)
-    weight_rows = lax.dynamic_slice_in_dim(weight, panel_start, channels, 0)
+    cot_block = to_vertex_split(cotangent)
+    feat_count = lax.axis_size("feat")
+    bias_full = lax.all_to_all(
+        jnp.broadcast_to(bias_vec[None, :], (feat_count, channels)),
+        "feat",
+        split_axis=0,
+        concat_axis=0,
+        tiled=True,
+    ).reshape(-1)
     mixed_state = jnp.sum(depth_weight[:, :, None] * states, axis=0).astype(jnp.bfloat16)
     outgoing = mixed_state[:, my_send]
     incoming = lax.all_to_all(outgoing, "vert", split_axis=1, concat_axis=1, tiled=True)
@@ -67,26 +82,25 @@
         tile_forward, extended, my_tiles, my_dst, my_src, tile_total, row_blocks
     )
     aggregated = aggregated.reshape(channels, row_count).astype(jnp.bfloat16)
-    pre_act = lax.psum_scatter(
-        lax.dot_general(
-            weight_rows, aggregated, (((0,), (0,)), ((), ())), preferred_element_type=jnp.float32
-        ).astype(jnp.bfloat16),
-        "feat",
-        scatter_dimension=0,
-        tiled=True,
-    ).astype(jnp.float32)
-    pre_act = pre_act + bias_vec[:, None]
+    agg_block = to_vertex_split(aggregated)
+    pre_act = lax.dot_general(
+        weight, agg_block, (((0,), (0,)), ((), ())), preferred_element_type=jnp.float32
+    )
+    pre_act = pre_act + bias_full[:, None]
     sigmoid_pre = jax.nn.sigmoid(pre_act)
-    layer_out = (pre_act * sigmoid_pre).astype(jnp.bfloat16)
+    out_block = (pre_act * sigmoid_pre).astype(jnp.bfloat16)
     grad_pre = (
-        cotangent.astype(jnp.float32) * sigmoid_pre * (1.0 + pre_act * (1.0 - sigmoid_pre))
+        cot_block.astype(jnp.float32) * sigmoid_pre * (1.0 + pre_act * (1.0 - sigmoid_pre))
     ).astype(jnp.bfloat16)
-    piece = lax.all_gather(grad_pre, "feat", axis=0, tiled=True)
-    agg_total = jnp.dot(weight_rows, piece, preferred_element_type=jnp.float32)
-    terms_now = lax.dot_general(
-        aggregated, piece, (((1,), (1,)), ((), ())), preferred_element_type=jnp.float32
+    grad_agg_block = jnp.dot(weight, grad_pre, preferred_element_type=jnp.float32).astype(
+        jnp.bfloat16
     )
-    grad_agg = agg_total.astype(jnp.bfloat16)
+    weight_terms = lax.dot_general(
+        agg_block, grad_pre, (((1,), (1,)), ((), ())), preferred_element_type=jnp.float32
+    )
+    bias_terms = jnp.sum(grad_pre.astype(jnp.float32), axis=1)
+    layer_out = to_channel_split(out_block)
+    grad_agg = to_channel_split(grad_agg_block)
     grad_blocks = grad_agg.reshape(channels, row_blocks, block_size)
     spread_out = over_tiles(
         tile_backward, grad_blocks, my_tiles, my_dst, my_src, tile_total, src_blocks
@@ -98,14 +112,25 @@
     returned = lax.all_to_all(halo_terms, "vert", split_axis=1, concat_axis=1, tiled=True)
     grad_mixed = spread_out[:, :row_count].at[:, my_send].add(returned.astype(jnp.float32))
     grad_states = (depth_weight[:, :, None] * grad_mixed[None]).astype(jnp.bfloat16)
-    bias_terms = jnp.sum(grad_pre.astype(jnp.float32), axis=1)
     depth_terms = jnp.sum(states * grad_mixed[None], axis=2)
-    weight_sum, bias_sum, depth_sum = lax.psum((terms_now, bias_terms, depth_terms), "vert")
+    packed = jnp.concatenate([weight_terms, bias_terms[:, None]], axis=1)
+    packed = lax.psum_scatter(packed, "feat", scatter_dimension=0, tiled=True)
+    flat = jnp.concatenate([packed.reshape(-1), depth_terms.reshape(-1)])
+    flat = lax.all_to_all(
+        jnp.broadcast_to(flat[None, :], (vert_count, flat.shape[0])),
+        "vert",
+        split_axis=0,
+        concat_axis=0,
+        tiled=True,
+    ).sum(axis=0)
+    width = weight.shape[1]
+    packed_sum = flat[: packed.size].reshape(packed.shape)
+    depth_sum = flat[packed.size :].reshape(depth_terms.shape)
     return (
         layer_out,
         grad_states,
-        weight_sum * norm_scale,
-        bias_sum * norm_scale,
+        packed_sum[:, :width] * norm_scale,
+        packed_sum[:, width] * norm_scale,
         depth_sum * norm_scale,
     )
 

time: 483 us -> 326 us (0.67)
  waiting for transfers between devices: 325 us -> 183 us
  blocking collectives: 65.4 us -> 0 us
  starting transfers between devices: 31.4 us -> 75.6 us
  local copies, waits for them, and re-layouts: 9.02 us -> 17.8 us
    reduce_scatter x1 -> x0, waiting for transfers between devices: 216 us -> none  [local(): lax.psum_scatter(lax.dot_general(weight_rows, aggregated, (((0,), (0,)),...]
    unnamed x2, waiting for transfers between devices: 0.04 us -> 135 us
    all_gather x1 -> x0, waiting for transfers between devices: 92 us -> none  [local(): piece = lax.all_gather(grad_pre, 'feat', axis=0, tiled=True)]
    psum x1 -> x0, blocking collectives: 65.4 us -> none  [local(): lax.psum((terms_now, bias_terms, depth_terms), 'vert')]
    all_to_all x0 -> x6, starting transfers between devices: none -> 52.4 us  [the longest x2 18.7 us: to_vertex_split(): lax.all_to_all(panel, 'feat', split_axis=1, concat_axis=0, tiled=True)]
    all_to_all x0 -> x6, waiting for transfers between devices: none -> 31.4 us  [the longest x1 14 us: local(): lax.all_to_all(jnp.broadcast_to(flat[None, :], (vert_count, flat.shape[0]...]
    all_to_all x1, starting transfers between devices: 14.7 us -> 7.04 us  [local(): lax.all_to_all(halo_terms, 'vert', split_axis=1, concat_axis=1, tiled=True)]
  transfers between devices with their start and end apart: 4 -> 9, of which waited for: 4 -> 6; matrix products, arithmetic and copies ran while one was open for 0% -> 11% of each run, Pallas kernels for 0% -> 0%
where the time goes in v1:
time: 326 us; the launch traced here: 325 us
  waiting for transfers between devices  183 us (56%)
  starting transfers between devices  75.6 us (23%)
  other arithmetic  17.9 us (5%)
  local copies, waits for them, and re-layouts  17.8 us (5%)
  between operations  15.7 us (5%)
  matrix products  14.6 us (4%)
    unnamed x2, waiting for transfers between devices  135 us
    all_to_all x2, starting transfers between devices, to_vertex_split(): lax.all_to_all(panel, 'feat', split_axis=1, concat_axis=0, tiled=True)  18.7 us
    all_to_all x1, starting transfers between devices, local(): lax.all_to_all(outgoing, 'vert', split_axis=1, concat_axis=1, tiled=True)  16.2 us
    all_to_all x1, starting transfers between devices, local(): lax.all_to_all(jnp.broadcast_to(flat[None, :], (vert_count, flat.shape[0]...  15.5 us
    all_to_all x1, waiting for transfers between devices, local(): lax.all_to_all(jnp.broadcast_to(flat[None, :], (vert_count, flat.shape[0]...  14 us
    all_to_all x1, starting transfers between devices, local(): lax.all_to_all(jnp.broadcast_to(bias_vec[None, :], (feat_count, channels)...  10.5 us
    scatter-add x1, other arithmetic, local(): spread_out[:, :row_count].at[:, my_send].add(returned.astype(jnp.float32))  9.52 us
    all_to_all x2, waiting for transfers between devices, to_vertex_split(): lax.all_to_all(panel, 'feat', split_axis=1, concat_axis=0, tiled=True)  8.72 us
  transfers between devices with their start and end apart: 9, of which 6 were waited for; matrix products, arithmetic and copies ran while one was open for 11% of the time, Pallas kernels for 0%

profile of v1, /device:TPU:1, one launch (start us, length us, event | category | flops | bytes accessed | tf_op | source)
XLA Modules:
  0.0 324.7 jit_solution(8860005678462092389)
XLA Ops:
  7.2 1.3 broadcast_in_dim.26
  8.5 10.5 %all-to-all-start.2 = ((f32[32,1,8]{2,1,0:T(1,128)}), f32[32,1,8]{2,1,0:T(1,128)S(1)}, u32[]{:S(2)}, u32[]{:S(2)}) async-start(f32[32,1,8]{2,1,0:T(1,128)} %broadcast_in_dim.26), calls=%async_computation.2 | async-start | bytes 32768 | tf_op jit(solution)/shard_map/all_to_all | solution.py:69
  19.0 0.7 compare_select_fusion.1
  19.7 0.7 compare_and_fusion
  20.4 0.7 compare_select_fusion.2
  21.1 0.7 compare_and_fusion.1
  21.8 0.7 compare_select_fusion
  22.5 1.1 fusion.15
  23.6 0.5 copy.91
  24.1 3.2 gather_fusion
  28.2 0.7 reshape.236
  28.9 1.3 dynamic-slice
  30.8 16.2 %all-to-all-start = ((bf16[24,2,256]{2,1,0:T(2,128)(2,1)}), bf16[24,2,256]{2,1,0:T(2,128)(2,1)S(1)}, u32[]{:S(2)}, u32[]{:S(2)}) async-start(bf16[24,2,256]{2,1,0:T(2,128)(2,1)} %reshape.236), calls=%async_computation | async-start | bytes 49152 | tf_op jit(solution)/shard_map/all_to_all | solution.py:78
  47.0 0.5 broadcast.137
  47.5 0.7 reduce.6
  48.3 8.5 %all-to-all-done = bf16[24,2,256]{2,1,0:T(2,128)(2,1)S(1)} async-done(((bf16[24,2,256]{2,1,0:T(2,128)(2,1)}), bf16[24,2,256]{2,1,0:T(2,128)(2,1)S(1)}, u32[]{:S(2)}, u32[]{:S(2)}) %all-to-all-start) | async-done | bytes 24608 | tf_op jit(solution)/shard_map/all_to_all | solution.py:78
  56.8 9.5 %all-to-all-start.4 = ((bf16[8,32,128]{2,0,1:T(8,128)(2,1)}), bf16[8,32,128]{2,0,1:T(8,128)(2,1)S(1)}, u32[]{:S(2)}, u32[]{:S(2)}) async-start(bf16[8,32,128]{2,0,1:T(8,128)(2,1)} %bitcast.104), calls=%async_computation.4 | async-start | bytes 131072 | tf_op jit(solution)/shard_map/all_to_all | solution.py:34
  66.5 0.8 gather_fusion.1
  67.3 7.8 %fusion.4 = bf16[8,256,128]{2,0,1:T(8,128)(2,1)S(1)} fusion(bf16[1,256,128,128]{3,2,1,0:T(8,128)(2,1)} %param.12, bf16[256,8,128]{2,1,0:T(8,128)(2,1)S(1)} %gather_fusion.1, pred[256]{0:T(512)(128)(4,1)S(1)} %compare_and_fusion.1), kind=kOutput, calls=%fused_computation.8 | convolution fusion | flops 67371008 | bytes 9437440 | tf_op jit(solution)/shard_map/dtc,trc->dtr/dot_general | solution.py:11
  75.4 0.7 copy.95
  76.0 9.2 %all-to-all-start.1 = ((bf16[8,32,128]{2,0,1:T(8,128)(2,1)}), bf16[8,32,128]{2,0,1:T(8,128)(2,1)S(1)}, u32[]{:S(2)}, u32[]{:S(2)}) async-start(bf16[8,32,128]{2,0,1:T(8,128)(2,1)} %copy.95), calls=%async_computation.1 | async-start | bytes 131072 | tf_op jit(solution)/shard_map/all_to_all | solution.py:34
  85.4 8.7 %all-to-all-done.1 = bf16[8,32,128]{2,0,1:T(8,128)(2,1)S(1)} async-done(((bf16[8,32,128]{2,0,1:T(8,128)(2,1)}), bf16[8,32,128]{2,0,1:T(8,128)(2,1)S(1)}, u32[]{:S(2)}, u32[]{:S(2)}) %all-to-all-start.1) | async-done | bytes 65568 | tf_op jit(solution)/shard_map/all_to_all | solution.py:34
  94.1 0.3 convert_reduce_fusion
  94.4 0.7 copy.96
  95.3 0.7 copy.98
  96.0 3.9 %all-to-all-start.5 = ((bf16[32,8,128]{2,1,0:T(8,128)(2,1)}), bf16[32,8,128]{2,1,0:T(8,128)(2,1)S(1)}, u32[]{:S(2)}, u32[]{:S(2)}) async-start(bf16[32,8,128]{2,1,0:T(8,128)(2,1)} %bitcast.25), calls=%async_computation.5 | async-start | bytes 131072 | tf_op jit(solution)/shard_map/all_to_all | solution.py:38
  100.1 8.6 %all-to-all-done.5 = bf16[32,8,128]{2,1,0:T(8,128)(2,1)S(1)} async-done(((bf16[32,8,128]{2,1,0:T(8,128)(2,1)}), bf16[32,8,128]{2,1,0:T(8,128)(2,1)S(1)}, u32[]{:S(2)}, u32[]{:S(2)}) %all-to-all-start.5) | async-done | bytes 65568 | tf_op jit(solution)/shard_map/all_to_all | solution.py:38
  108.8 0.8 gather_fusion.2
  109.6 5.8 %fusion.7 = bf16[8,256,128]{2,0,1:T(8,128)(2,1)S(1)} fusion(bf16[1,256,128,128]{3,2,1,0:T(8,128)(2,1)} %param.12, bf16[256,8,128]{2,1,0:T(8,128)(2,1)S(1)} %gather_fusion.2, pred[256]{0:T(512)(128)(4,1)S(1)} %compare_and_fusion), kind=kOutput, calls=%fused_computation.9 | convolution fusion | flops 67371008 | bytes 9437440 | tf_op jit(solution)/shard_map/dtr,trc->dtc/dot_general | solution.py:20
  115.8 0.7 reshape.238
  116.5 7.0 %all-to-all-start.6 = ((bf16[24,2,256]{2,1,0:T(2,128)(2,1)}), bf16[24,2,256]{2,1,0:T(2,128)(2,1)S(1)}, u32[]{:S(2)}, u32[]{:S(2)}) async-start(bf16[24,2,256]{2,1,0:T(2,128)(2,1)} %reshape.238), calls=%async_computation.6 | async-start | bytes 49152 | tf_op jit(solution)/shard_map/all_to_all | solution.py:112
  123.6 0.7 pad_maximum_fusion
  124.4 0.6 copy.112
  125.0 8.4 %all-to-all-done.6 = bf16[24,2,256]{2,1,0:T(2,128)(2,1)S(1)} async-done(((bf16[24,2,256]{2,1,0:T(2,128)(2,1)}), bf16[24,2,256]{2,1,0:T(2,128)(2,1)S(1)}, u32[]{:S(2)}, u32[]{:S(2)}) %all-to-all-start.6) | async-done | bytes 24608 | tf_op jit(solution)/shard_map/all_to_all | solution.py:112
  133.3 3.9 %all-to-all-start.3 = ((bf16[32,8,128]{2,1,0:T(8,128)(2,1)}), bf16[32,8,128]{2,1,0:T(8,128)(2,1)S(1)}, u32[]{:S(2)}, u32[]{:S(2)}) async-start(bf16[32,8,128]{2,1,0:T(8,128)(2,1)} %bitcast.17), calls=%async_computation.3 | async-start | bytes 131072 | tf_op jit(solution)/shard_map/all_to_all | solution.py:38
  137.3 0.3 copy.107
  137.6 9.5 %scatter_fusion = f32[8,4096]{0,1:T(8,128)S(1)} fusion(f32[8,4096]{0,1:T(8,128)S(1)} %copy.112, s32[1536]{0:T(1024)S(1)} %reshape.189, f32[1536,8]{1,0:T(8,128)S(1)} %bitcast.97), kind=kCustom, calls=%fused_computation.3 | custom fusion | flops 12288 | bytes 153600 | tf_op jit(solution)/shard_map/scatter-add | solution.py:113
  147.1 0.6 copy.104
  147.7 0.9 fusion.16
  148.7 134.8 %all-reduce.3.cloned.1.call-done = f32[256,257]{0,1:T(8,128)} async-done(((f32[256,257]{0,1:T(8,128)}), f32[256,257]{0,1:T(8,128)}) %all-reduce.3.cloned.1.call-update) | async-done | bytes 263184
  283.5 1.0 constant_dynamic-slice_fusion
  284.8 0.8 broadcast_in_dim.29
  285.5 15.5 %all-to-all-start.7 = ((f32[24,1,2088]{2,1,0:T(1,128)}), f32[24,1,2088]{2,1,0:T(1,128)S(1)}, u32[]{:S(2)}, u32[]{:S(2)}) async-start(f32[24,1,2088]{2,1,0:T(1,128)} %broadcast_in_dim.29), calls=%async_computation.7 | async-start | bytes 417792 | tf_op jit(solution)/shard_map/all_to_all | solution.py:119
  301.0 14.0 %all-to-all-done.7 = f32[24,1,2088]{2,1,0:T(1,128)S(1)} async-done(((f32[24,1,2088]{2,1,0:T(1,128)}), f32[24,1,2088]{2,1,0:T(1,128)S(1)}, u32[]{:S(2)}, u32[]{:S(2)}) %all-to-all-start.7) | async-done | bytes 200480 | tf_op jit(solution)/shard_map/all_to_all | solution.py:119
  315.3 0.6 fusion.38
  315.9 0.6 slice_multiply_fusion
  316.5 0.7 mul.73
  317.2 0.6 copy.128
  (47 shorter events, 2.5 us)
Async XLA Ops:
  7.2 86.9 %copy-start = (bf16[256,256]{1,0:T(8,128)(2,1)S(1)}, bf16[256,256]{1,0:T(8,128)(2,1)}, u32[]{:S(2)}) copy-start(bf16[256,256]{1,0:T(8,128)(2,1)} %param.17) | copy-start | bytes 393220
  7.2 68.0 %copy-start.3 = (s32[1,256]{1,0:T(1,128)S(1)}, s32[1,256]{1,0:T(1,128)}, u32[]{:S(2)}) copy-start(s32[1,256]{1,0:T(1,128)} %param.13) | copy-start | bytes 3076
  8.5 22.3 %all-to-all-start.2 = ((f32[32,1,8]{2,1,0:T(1,128)}), f32[32,1,8]{2,1,0:T(1,128)S(1)}, u32[]{:S(2)}, u32[]{:S(2)}) async-start(f32[32,1,8]{2,1,0:T(1,128)} %broadcast_in_dim.26), calls=%async_computation.2 | async-start | bytes 32768 | tf_op jit(solution)/shard_map/all_to_all | solution.py:69
  30.8 25.9 %all-to-all-start = ((bf16[24,2,256]{2,1,0:T(2,128)(2,1)}), bf16[24,2,256]{2,1,0:T(2,128)(2,1)S(1)}, u32[]{:S(2)}, u32[]{:S(2)}) async-start(bf16[24,2,256]{2,1,0:T(2,128)(2,1)} %reshape.236), calls=%async_computation | async-start | bytes 49152 | tf_op jit(solution)/shard_map/all_to_all | solution.py:78
  56.8 19.3 %all-to-all-start.4 = ((bf16[8,32,128]{2,0,1:T(8,128)(2,1)}), bf16[8,32,128]{2,0,1:T(8,128)(2,1)S(1)}, u32[]{:S(2)}, u32[]{:S(2)}) async-start(bf16[8,32,128]{2,0,1:T(8,128)(2,1)} %bitcast.104), calls=%async_computation.4 | async-start | bytes 131072 | tf_op jit(solution)/shard_map/all_to_all | solution.py:34
  75.2 40.2 %copy-start.4 = (s32[1,256]{1,0:T(1,128)S(1)}, s32[1,256]{1,0:T(1,128)}, u32[]{:S(2)}) copy-start(s32[1,256]{1,0:T(1,128)} %param.14) | copy-start | bytes 3076
  76.0 18.1 %all-to-all-start.1 = ((bf16[8,32,128]{2,0,1:T(8,128)(2,1)}), bf16[8,32,128]{2,0,1:T(8,128)(2,1)S(1)}, u32[]{:S(2)}, u32[]{:S(2)}) async-start(bf16[8,32,128]{2,0,1:T(8,128)(2,1)} %copy.95), calls=%async_computation.1 | async-start | bytes 131072 | tf_op jit(solution)/shard_map/all_to_all | solution.py:34
  96.0 12.7 %all-to-all-start.5 = ((bf16[32,8,128]{2,1,0:T(8,128)(2,1)}), bf16[32,8,128]{2,1,0:T(8,128)(2,1)S(1)}, u32[]{:S(2)}, u32[]{:S(2)}) async-start(bf16[32,8,128]{2,1,0:T(8,128)(2,1)} %bitcast.25), calls=%async_computation.5 | async-start | bytes 131072 | tf_op jit(solution)/shard_map/all_to_all | solution.py:38
  109.6 38.1 %copy-start.1 = (bf16[4,8,4096]{2,1,0:T(8,128)(2,1)S(1)}, bf16[4,8,4096]{2,1,0:T(8,128)(2,1)}, u32[]{:S(2)}) copy-start(bf16[4,8,4096]{2,1,0:T(8,128)(2,1)} %param.10) | copy-start | bytes 786436
  109.6 38.1 %copy-start.2 = (f32[4,8]{1,0:T(4,128)S(1)}, f32[4,8]{1,0:T(4,128)}, u32[]{:S(2)}) copy-start(f32[4,8]{1,0:T(4,128)} %param.11) | copy-start | bytes 388
  116.5 16.9 %all-to-all-start.6 = ((bf16[24,2,256]{2,1,0:T(2,128)(2,1)}), bf16[24,2,256]{2,1,0:T(2,128)(2,1)S(1)}, u32[]{:S(2)}, u32[]{:S(2)}) async-start(bf16[24,2,256]{2,1,0:T(2,128)(2,1)} %reshape.238), calls=%async_computation.6 | async-start | bytes 49152 | tf_op jit(solution)/shard_map/all_to_all | solution.py:112
  123.5 159.9 %all-reduce.3.cloned.1.call-start = ((), (), s32[]{:S(2)}) async-start(), calls=%async_computation.8 | async-start | bytes 540672
  133.3 151.4 %all-to-all-start.3 = ((bf16[32,8,128]{2,1,0:T(8,128)(2,1)}), bf16[32,8,128]{2,1,0:T(8,128)(2,1)S(1)}, u32[]{:S(2)}, u32[]{:S(2)}) async-start(bf16[32,8,128]{2,1,0:T(8,128)(2,1)} %bitcast.17), calls=%async_computation.3 | async-start | bytes 131072 | tf_op jit(solution)/shard_map/all_to_all | solution.py:38
  285.5 29.5 %all-to-all-start.7 = ((f32[24,1,2088]{2,1,0:T(1,128)}), f32[24,1,2088]{2,1,0:T(1,128)S(1)}, u32[]{:S(2)}, u32[]{:S(2)}) async-start(f32[24,1,2088]{2,1,0:T(1,128)} %broadcast_in_dim.29), calls=%async_computation.7 | async-start | bytes 417792 | tf_op jit(solution)/shard_map/all_to_all | solution.py:119
Sparse Core Ops, SparseCore 0:
  127.8 155.5 all-reduce.2

commit v2 on v1

--- a/solution.py
+++ b/solution.py
@@ -114,7 +114,8 @@
     grad_states = (depth_weight[:, :, None] * grad_mixed[None]).astype(jnp.bfloat16)
     depth_terms = jnp.sum(states * grad_mixed[None], axis=2)
     packed = jnp.concatenate([weight_terms, bias_terms[:, None]], axis=1)
-    packed = lax.psum_scatter(packed, "feat", scatter_dimension=0, tiled=True)
+    packed = packed.reshape(feat_count, channels, packed.shape[1])
+    packed = lax.all_to_all(packed, "feat", split_axis=0, concat_axis=0, tiled=True).sum(axis=0)
     flat = jnp.concatenate([packed.reshape(-1), depth_terms.reshape(-1)])
     flat = lax.all_to_all(
         jnp.broadcast_to(flat[None, :], (vert_count, flat.shape[0])),

time: 326 us -> 183 us (0.56)
  waiting for transfers between devices: 183 us -> 57.8 us
  between operations: 15.7 us -> 1.63 us
    unnamed x2 -> x0, waiting for transfers between devices: 135 us -> none
    all_to_all x1, starting transfers between devices: 15.5 us -> 5.64 us  [local(): lax.all_to_all(jnp.broadcast_to(flat[None, :], (vert_count, flat.shape[0]...]
    all_to_all x2, waiting for transfers between devices: 8.64 us -> 16.1 us  [to_channel_split(): lax.all_to_all(block, 'feat', split_axis=0, concat_axis=1, tiled=True)]
    all_to_all x2, starting transfers between devices: 7.71 us -> 11.8 us  [to_channel_split(): lax.all_to_all(block, 'feat', split_axis=0, concat_axis=1, tiled=True)]
    all_to_all x0 -> x1, starting transfers between devices: none -> 3.88 us  [local(): lax.all_to_all(packed, 'feat', split_axis=0, concat_axis=0, tiled=True)]
  transfers between devices with their start and end apart: 9 -> 9, of which waited for: 6 -> 7; matrix products, arithmetic and copies ran while one was open for 11% -> 20% of each run, Pallas kernels for 0% -> 0%
where the time goes in v2:
time: 183 us
  starting transfers between devices  73.7 us (40%)
  waiting for transfers between devices  57.8 us (32%)
  other arithmetic  18.3 us (10%)
  local copies, waits for them, and re-layouts  16.5 us (9%)
  matrix products  14.6 us (8%)
    all_to_all x2, starting transfers between devices, to_vertex_split(): lax.all_to_all(panel, 'feat', split_axis=1, concat_axis=0, tiled=True)  18.7 us
    all_to_all x1, starting transfers between devices, local(): lax.all_to_all(outgoing, 'vert', split_axis=1, concat_axis=1, tiled=True)  16.1 us
    all_to_all x2, waiting for transfers between devices, to_channel_split(): lax.all_to_all(block, 'feat', split_axis=0, concat_axis=1, tiled=True)  16.1 us
    all_to_all x1, waiting for transfers between devices, local(): lax.all_to_all(jnp.broadcast_to(flat[None, :], (vert_count, flat.shape[0]...  14.1 us
    all_to_all x2, starting transfers between devices, to_channel_split(): lax.all_to_all(block, 'feat', split_axis=0, concat_axis=1, tiled=True)  11.8 us
    all_to_all x1, starting transfers between devices, local(): lax.all_to_all(jnp.broadcast_to(bias_vec[None, :], (feat_count, channels)...  10.5 us
    scatter-add x1, other arithmetic, local(): spread_out[:, :row_count].at[:, my_send].add(returned.astype(jnp.float32))  9.89 us
    all_to_all x1, waiting for transfers between devices, local(): lax.all_to_all(halo_terms, 'vert', split_axis=1, concat_axis=1, tiled=True)  9.04 us
  transfers between devices with their start and end apart: 9, of which 7 were waited for; matrix products, arithmetic and copies ran while one was open for 20% of the time, Pallas kernels for 0%

profile of v2, /device:TPU:1, one launch (start us, length us, event | category | flops | bytes accessed | tf_op | source)
XLA Modules:
  0.0 182.6 jit_solution(6391922962890425423)
XLA Ops:
  0.7 1.3 broadcast_in_dim.24
  2.0 10.5 %all-to-all-start.2 = ((f32[32,1,8]{2,1,0:T(1,128)}), f32[32,1,8]{2,1,0:T(1,128)S(1)}, u32[]{:S(2)}, u32[]{:S(2)}) async-start(f32[32,1,8]{2,1,0:T(1,128)} %broadcast_in_dim.24), calls=%async_computation.2 | async-start | bytes 32768 | tf_op jit(solution)/shard_map/all_to_all | solution.py:69
  12.5 0.7 compare_select_fusion.1
  13.2 0.7 compare_and_fusion
  13.8 0.7 compare_select_fusion.2
  14.5 0.7 compare_and_fusion.1
  15.2 0.7 compare_select_fusion
  16.0 1.1 fusion.15
  17.1 0.5 copy.99
  17.6 3.2 %gather_fusion = bf16[1536,8]{1,0:T(8,128)(2,1)S(1)} fusion(bf16[8,4096]{0,1:T(8,128)(2,1)S(1)} %copy.99, s32[2048]{0:T(1024)S(1)} %pad_clamp_fusion), kind=kCustom, calls=%fused_computation | custom fusion | bytes 55296 | tf_op jit(solution)/shard_map/gather | solution.py:77
  21.6 0.7 reshape.240
  22.3 16.1 %all-to-all-start = ((bf16[24,2,256]{2,1,0:T(2,128)(2,1)}), bf16[24,2,256]{2,1,0:T(2,128)(2,1)S(1)}, u32[]{:S(2)}, u32[]{:S(2)}) async-start(bf16[24,2,256]{2,1,0:T(2,128)(2,1)} %reshape.240), calls=%async_computation | async-start | bytes 49152 | tf_op jit(solution)/shard_map/all_to_all | solution.py:78
  38.5 0.5 broadcast.137
  39.0 0.7 reduce.6
  39.8 8.5 %all-to-all-done = bf16[24,2,256]{2,1,0:T(2,128)(2,1)S(1)} async-done(((bf16[24,2,256]{2,1,0:T(2,128)(2,1)}), bf16[24,2,256]{2,1,0:T(2,128)(2,1)S(1)}, u32[]{:S(2)}, u32[]{:S(2)}) %all-to-all-start) | async-done | bytes 24608 | tf_op jit(solution)/shard_map/all_to_all | solution.py:78
  48.3 9.5 %all-to-all-start.4 = ((bf16[8,32,128]{2,0,1:T(8,128)(2,1)}), bf16[8,32,128]{2,0,1:T(8,128)(2,1)S(1)}, u32[]{:S(2)}, u32[]{:S(2)}) async-start(bf16[8,32,128]{2,0,1:T(8,128)(2,1)} %bitcast.102), calls=%async_computation.4 | async-start | bytes 131072 | tf_op jit(solution)/shard_map/all_to_all | solution.py:34
  58.0 0.8 gather_fusion.1
  58.8 7.8 %fusion.4 = bf16[8,256,128]{2,0,1:T(8,128)(2,1)S(1)} fusion(bf16[1,256,128,128]{3,2,1,0:T(8,128)(2,1)} %param.12, bf16[256,8,128]{2,1,0:T(8,128)(2,1)S(1)} %gather_fusion.1, pred[256]{0:T(512)(128)(4,1)S(1)} %compare_and_fusion.1), kind=kOutput, calls=%fused_computation.8 | convolution fusion | flops 67371008 | bytes 9437440 | tf_op jit(solution)/shard_map/dtc,trc->dtr/dot_general | solution.py:11
  66.9 0.7 copy.103
  67.6 9.2 %all-to-all-start.1 = ((bf16[8,32,128]{2,0,1:T(8,128)(2,1)}), bf16[8,32,128]{2,0,1:T(8,128)(2,1)S(1)}, u32[]{:S(2)}, u32[]{:S(2)}) async-start(bf16[8,32,128]{2,0,1:T(8,128)(2,1)} %copy.103), calls=%async_computation.1 | async-start | bytes 131072 | tf_op jit(solution)/shard_map/all_to_all | solution.py:34
  76.9 8.7 %all-to-all-done.1 = bf16[8,32,128]{2,0,1:T(8,128)(2,1)S(1)} async-done(((bf16[8,32,128]{2,0,1:T(8,128)(2,1)}), bf16[8,32,128]{2,0,1:T(8,128)(2,1)S(1)}, u32[]{:S(2)}, u32[]{:S(2)}) %all-to-all-start.1) | async-done | bytes 65568 | tf_op jit(solution)/shard_map/all_to_all | solution.py:34
  85.6 0.3 convert_reduce_fusion
  86.1 0.7 copy.106
  86.8 3.9 %all-to-all-start.5 = ((bf16[32,8,128]{2,1,0:T(8,128)(2,1)}), bf16[32,8,128]{2,1,0:T(8,128)(2,1)S(1)}, u32[]{:S(2)}, u32[]{:S(2)}) async-start(bf16[32,8,128]{2,1,0:T(8,128)(2,1)} %bitcast.25), calls=%async_computation.5 | async-start | bytes 131072 | tf_op jit(solution)/shard_map/all_to_all | solution.py:38
  91.1 8.5 %all-to-all-done.5 = bf16[32,8,128]{2,1,0:T(8,128)(2,1)S(1)} async-done(((bf16[32,8,128]{2,1,0:T(8,128)(2,1)}), bf16[32,8,128]{2,1,0:T(8,128)(2,1)S(1)}, u32[]{:S(2)}, u32[]{:S(2)}) %all-to-all-start.5) | async-done | bytes 65568 | tf_op jit(solution)/shard_map/all_to_all | solution.py:38
  99.6 0.8 gather_fusion.2
  100.4 5.8 %fusion.7 = bf16[8,256,128]{2,0,1:T(8,128)(2,1)S(1)} fusion(bf16[1,256,128,128]{3,2,1,0:T(8,128)(2,1)} %param.12, bf16[256,8,128]{2,1,0:T(8,128)(2,1)S(1)} %gather_fusion.2, pred[256]{0:T(512)(128)(4,1)S(1)} %compare_and_fusion), kind=kOutput, calls=%fused_computation.9 | convolution fusion | flops 67371008 | bytes 9437440 | tf_op jit(solution)/shard_map/dtr,trc->dtc/dot_general | solution.py:20
  106.6 0.7 reshape.242
  107.3 7.0 %all-to-all-start.6 = ((bf16[24,2,256]{2,1,0:T(2,128)(2,1)}), bf16[24,2,256]{2,1,0:T(2,128)(2,1)S(1)}, u32[]{:S(2)}, u32[]{:S(2)}) async-start(bf16[24,2,256]{2,1,0:T(2,128)(2,1)} %reshape.242), calls=%async_computation.6 | async-start | bytes 49152 | tf_op jit(solution)/shard_map/all_to_all | solution.py:112
  114.3 0.8 pad_maximum_fusion
  115.1 9.0 %all-to-all-done.6 = bf16[24,2,256]{2,1,0:T(2,128)(2,1)S(1)} async-done(((bf16[24,2,256]{2,1,0:T(2,128)(2,1)}), bf16[24,2,256]{2,1,0:T(2,128)(2,1)S(1)}, u32[]{:S(2)}, u32[]{:S(2)}) %all-to-all-start.6) | async-done | bytes 24608 | tf_op jit(solution)/shard_map/all_to_all | solution.py:112
  124.1 3.9 %all-to-all-start.7 = ((f32[32,8,257]{2,1,0:T(8,128)}), f32[32,8,257]{2,1,0:T(8,128)S(1)}, u32[]{:S(2)}, u32[]{:S(2)}) async-start(f32[32,8,257]{2,1,0:T(8,128)} %pad_maximum_fusion), calls=%async_computation.7 | async-start | bytes 786432 | tf_op jit(solution)/shard_map/all_to_all | solution.py:118
  128.0 0.7 copy.104
  128.8 0.6 copy.121
  129.5 1.2 copy.117
  130.7 9.9 %scatter_fusion = f32[8,4096]{0,1:T(8,128)S(1)} fusion(f32[8,4096]{0,1:T(8,128)S(1)} %copy.121, s32[1536]{0:T(1024)S(1)} %reshape.195, f32[1536,8]{1,0:T(8,128)} %bitcast.95), kind=kCustom, calls=%fused_computation.3 | custom fusion | flops 12288 | bytes 153600 | tf_op jit(solution)/shard_map/scatter-add | solution.py:113
  140.6 0.6 copy.112
  141.1 1.3 all-to-all-done.7
  142.5 7.9 %all-to-all-start.3 = ((bf16[32,8,128]{2,1,0:T(8,128)(2,1)}), bf16[32,8,128]{2,1,0:T(8,128)(2,1)S(1)}, u32[]{:S(2)}, u32[]{:S(2)}) async-start(bf16[32,8,128]{2,1,0:T(8,128)(2,1)} %bitcast.17), calls=%async_computation.3 | async-start | bytes 131072 | tf_op jit(solution)/shard_map/all_to_all | solution.py:38
  150.4 0.9 fusion.16
  151.5 7.6 %all-to-all-done.3 = bf16[32,8,128]{2,1,0:T(8,128)(2,1)S(1)} async-done(((bf16[32,8,128]{2,1,0:T(8,128)(2,1)}), bf16[32,8,128]{2,1,0:T(8,128)(2,1)S(1)}, u32[]{:S(2)}, u32[]{:S(2)}) %all-to-all-start.3) | async-done | bytes 65568 | tf_op jit(solution)/shard_map/all_to_all | solution.py:38
  159.2 0.8 broadcast_in_dim.26
  160.0 5.6 %all-to-all-start.8 = ((f32[24,1,2088]{2,1,0:T(1,128)}), f32[24,1,2088]{2,1,0:T(1,128)S(1)}, u32[]{:S(2)}, u32[]{:S(2)}) async-start(f32[24,1,2088]{2,1,0:T(1,128)} %broadcast_in_dim.26), calls=%async_computation.8 | async-start | bytes 417792 | tf_op jit(solution)/shard_map/all_to_all | solution.py:120
  165.6 14.1 %all-to-all-done.8 = f32[24,1,2088]{2,1,0:T(1,128)S(1)} async-done(((f32[24,1,2088]{2,1,0:T(1,128)}), f32[24,1,2088]{2,1,0:T(1,128)S(1)}, u32[]{:S(2)}, u32[]{:S(2)}) %all-to-all-start.8) | async-done | bytes 200480 | tf_op jit(solution)/shard_map/all_to_all | solution.py:120
  180.0 0.6 fusion.39
  180.7 0.6 slice_multiply_fusion
  181.3 0.7 mul.73
  181.9 0.6 copy.136
  (45 shorter events, 2.6 us)
Async XLA Ops:
  0.6 85.0 %copy-start = (bf16[256,256]{1,0:T(8,128)(2,1)S(1)}, bf16[256,256]{1,0:T(8,128)(2,1)}, u32[]{:S(2)}) copy-start(bf16[256,256]{1,0:T(8,128)(2,1)} %param.17) | copy-start | bytes 393220
  0.6 66.0 %copy-start.3 = (s32[1,256]{1,0:T(1,128)S(1)}, s32[1,256]{1,0:T(1,128)}, u32[]{:S(2)}) copy-start(s32[1,256]{1,0:T(1,128)} %param.13) | copy-start | bytes 3076
  2.0 20.4 %all-to-all-start.2 = ((f32[32,1,8]{2,1,0:T(1,128)}), f32[32,1,8]{2,1,0:T(1,128)S(1)}, u32[]{:S(2)}, u32[]{:S(2)}) async-start(f32[32,1,8]{2,1,0:T(1,128)} %broadcast_in_dim.24), calls=%async_computation.2 | async-start | bytes 32768 | tf_op jit(solution)/shard_map/all_to_all | solution.py:69
  22.3 25.9 %all-to-all-start = ((bf16[24,2,256]{2,1,0:T(2,128)(2,1)}), bf16[24,2,256]{2,1,0:T(2,128)(2,1)S(1)}, u32[]{:S(2)}, u32[]{:S(2)}) async-start(bf16[24,2,256]{2,1,0:T(2,128)(2,1)} %reshape.240), calls=%async_computation | async-start | bytes 49152 | tf_op jit(solution)/shard_map/all_to_all | solution.py:78
  48.3 19.3 %all-to-all-start.4 = ((bf16[8,32,128]{2,0,1:T(8,128)(2,1)}), bf16[8,32,128]{2,0,1:T(8,128)(2,1)S(1)}, u32[]{:S(2)}, u32[]{:S(2)}) async-start(bf16[8,32,128]{2,0,1:T(8,128)(2,1)} %bitcast.102), calls=%async_computation.4 | async-start | bytes 131072 | tf_op jit(solution)/shard_map/all_to_all | solution.py:34
  66.7 39.5 %copy-start.4 = (s32[1,256]{1,0:T(1,128)S(1)}, s32[1,256]{1,0:T(1,128)}, u32[]{:S(2)}) copy-start(s32[1,256]{1,0:T(1,128)} %param.14) | copy-start | bytes 3076
  67.6 18.1 %all-to-all-start.1 = ((bf16[8,32,128]{2,0,1:T(8,128)(2,1)}), bf16[8,32,128]{2,0,1:T(8,128)(2,1)S(1)}, u32[]{:S(2)}, u32[]{:S(2)}) async-start(bf16[8,32,128]{2,0,1:T(8,128)(2,1)} %copy.103), calls=%async_computation.1 | async-start | bytes 131072 | tf_op jit(solution)/shard_map/all_to_all | solution.py:34
  86.8 12.7 %all-to-all-start.5 = ((bf16[32,8,128]{2,1,0:T(8,128)(2,1)}), bf16[32,8,128]{2,1,0:T(8,128)(2,1)S(1)}, u32[]{:S(2)}, u32[]{:S(2)}) async-start(bf16[32,8,128]{2,1,0:T(8,128)(2,1)} %bitcast.25), calls=%async_computation.5 | async-start | bytes 131072 | tf_op jit(solution)/shard_map/all_to_all | solution.py:38
  100.4 50.0 %copy-start.1 = (bf16[4,8,4096]{2,1,0:T(8,128)(2,1)S(1)}, bf16[4,8,4096]{2,1,0:T(8,128)(2,1)}, u32[]{:S(2)}) copy-start(bf16[4,8,4096]{2,1,0:T(8,128)(2,1)} %param.10) | copy-start | bytes 786436
  100.4 50.0 %copy-start.2 = (f32[4,8]{1,0:T(4,128)S(1)}, f32[4,8]{1,0:T(4,128)}, u32[]{:S(2)}) copy-start(f32[4,8]{1,0:T(4,128)} %param.11) | copy-start | bytes 388
  107.3 16.9 %all-to-all-start.6 = ((bf16[24,2,256]{2,1,0:T(2,128)(2,1)}), bf16[24,2,256]{2,1,0:T(2,128)(2,1)S(1)}, u32[]{:S(2)}, u32[]{:S(2)}) async-start(bf16[24,2,256]{2,1,0:T(2,128)(2,1)} %reshape.242), calls=%async_computation.6 | async-start | bytes 49152 | tf_op jit(solution)/shard_map/all_to_all | solution.py:112
  124.1 18.3 %all-to-all-start.7 = ((f32[32,8,257]{2,1,0:T(8,128)}), f32[32,8,257]{2,1,0:T(8,128)S(1)}, u32[]{:S(2)}, u32[]{:S(2)}) async-start(f32[32,8,257]{2,1,0:T(8,128)} %pad_maximum_fusion), calls=%async_computation.7 | async-start | bytes 786432 | tf_op jit(solution)/shard_map/all_to_all | solution.py:118
  142.5 16.7 %all-to-all-start.3 = ((bf16[32,8,128]{2,1,0:T(8,128)(2,1)}), bf16[32,8,128]{2,1,0:T(8,128)(2,1)S(1)}, u32[]{:S(2)}, u32[]{:S(2)}) async-start(bf16[32,8,128]{2,1,0:T(8,128)(2,1)} %bitcast.17), calls=%async_computation.3 | async-start | bytes 131072 | tf_op jit(solution)/shard_map/all_to_all | solution.py:38
  160.0 19.8 %all-to-all-start.8 = ((f32[24,1,2088]{2,1,0:T(1,128)}), f32[24,1,2088]{2,1,0:T(1,128)S(1)}, u32[]{:S(2)}, u32[]{:S(2)}) async-start(f32[24,1,2088]{2,1,0:T(1,128)} %broadcast_in_dim.26), calls=%async_computation.8 | async-start | bytes 417792 | tf_op jit(solution)/shard_map/all_to_all | solution.py:120

commit v3 on v0

v3 whole, which is shorter than its diff:
```python
import math

import jax
import jax.numpy as jnp
from jax import lax
from jax.sharding import PartitionSpec as P


def tile_forward(extended, tile_grp, dst_grp, src_grp, live_mask, row_blocks):
    picked = jnp.take(extended, src_grp, axis=1)
    products = jnp.einsum("dtc,trc->dtr", picked, tile_grp, preferred_element_type=jnp.float32)
    onehot = (
        (dst_grp[:, None] == jnp.arange(row_blocks, dtype=jnp.int32)[None, :]) & live_mask[:, None]
    ).astype(jnp.float32)
    return jnp.einsum("dtr,tn->dnr", products, onehot)


def tile_backward(grad_blocks, tile_grp, dst_grp, src_grp, live_mask, src_blocks):
    picked = jnp.take(grad_blocks, dst_grp, axis=1)
    products = jnp.einsum("dtr,trc->dtc", picked, tile_grp, preferred_element_type=jnp.float32)
    onehot = (
        (src_grp[:, None] == jnp.arange(src_blocks, dtype=jnp.int32)[None, :]) & live_mask[:, None]
    ).astype(jnp.float32)
    return jnp.einsum("dtc,ts->dsc", products, onehot)


def over_tiles(kernel, source, tile_values, tile_dst, tile_src, tile_total, out_blocks):
    capacity = tile_values.shape[0]
    live_mask = jnp.arange(capacity, dtype=jnp.int32) < tile_total
    return kernel(source, tile_values, tile_dst, tile_src, live_mask, out_blocks)


def local(
    states,
    depth_weight,
    tile_values,
    tile_dst,
    tile_src,
    tile_count,
    send_rows,
    weight,
    bias_vec,
    cotangent,
):
    f32 = jnp.float32
    bf16 = jnp.bfloat16
    channels = states.shape[1]
    row_count = states.shape[2]
    block_size = tile_values.shape[2]
    row_blocks = row_count // block_size
    my_tiles = tile_values[0]
    my_dst = tile_dst[0]
    my_src = tile_src[0]
    tile_total = tile_count[0]
    my_send = send_rows[0]
    section_count = my_send.shape[0]
    halo_width = my_send.shape[1]
    vert_count = lax.axis_size("vert")
    feat_count = lax.axis_size("feat")
    col_width = row_count // feat_count
    width = weight.shape[1]
    src_blocks = (row_count + section_count * halo_width) // block_size
    norm_scale = 1.0 / math.sqrt(vert_count * row_count)

    def to_blocks(x):
        return x.reshape(channels, feat_count, col_width).transpose(1, 0, 2)

    def from_blocks(x):
        return x.transpose(1, 0, 2).reshape(channels, row_count)

    halo_states = lax.all_to_all(
        states[:, :, my_send], "vert", split_axis=2, concat_axis=2, tiled=True
    )
    mixed_state = jnp.sum(depth_weight[:, :, None] * states, axis=0).astype(bf16)
    mixed_halo = jnp.sum(depth_weight[:, :, None, None] * halo_states, axis=0).astype(bf16)
    extended = jnp.concatenate([mixed_state, mixed_halo.reshape(channels, -1)], axis=1)
    extended = extended.reshape(channels, src_blocks, block_size)
    aggregated = over_tiles(
        tile_forward, extended, my_tiles, my_dst, my_src, tile_total, row_blocks
    )
    aggregated = aggregated.reshape(channels, row_count).astype(bf16)

    bias_cols = jnp.broadcast_to(bias_vec[None, :, None], (feat_count, channels, 1))
    first_send = jnp.concatenate(
        [to_blocks(aggregated).astype(f32), to_blocks(cotangent).astype(f32), bias_cols], axis=2
    )
    first_recv = lax.all_to_all(first_send, "feat", split_axis=0, concat_axis=0, tiled=True)
    first_recv = first_recv.reshape(feat_count * channels, -1)
    agg_block = first_recv[:, :col_width].astype(bf16)
    cot_block = first_recv[:, col_width : 2 * col_width]
    bias_full = first_recv[:, 2 * col_width]

    pre_act = lax.dot_general(
        weight, agg_block, (((0,), (0,)), ((), ())), preferred_element_type=f32
    )
    pre_act = pre_act + bias_full[:, None]
    sigmoid_pre = jax.nn.sigmoid(pre_act)
    out_block = (pre_act * sigmoid_pre).astype(bf16)
    grad_pre = (cot_block * sigmoid_pre * (1.0 + pre_act * (1.0 - sigmoid_pre))).astype(bf16)
    grad_agg_block = jnp.dot(weight, grad_pre, preferred_element_type=f32).astype(bf16)
    weight_terms = lax.dot_general(
        agg_block, grad_pre, (((1,), (1,)), ((), ())), preferred_element_type=f32
    )
    bias_terms = jnp.sum(grad_pre.astype(f32), axis=1)

    second_send = jnp.concatenate(
        [
            out_block.astype(f32).reshape(feat_count, channels, col_width),
            grad_agg_block.astype(f32).reshape(feat_count, channels, col_width),
            weight_terms.reshape(feat_count, channels, width),
            bias_terms.reshape(feat_count, channels, 1),
        ],
        axis=2,
    )
    second_recv = lax.all_to_all(second_send, "feat", split_axis=0, concat_axis=0, tiled=True)
    layer_out = from_blocks(second_recv[:, :, :col_width]).astype(bf16)
    grad_agg = from_blocks(second_recv[:, :, col_width : 2 * col_width]).astype(bf16)
    panel_terms = jnp.sum(second_recv[:, :, 2 * col_width :], axis=0)

    grad_blocks = grad_agg.reshape(channels, row_blocks, block_size)
    spread_out = over_tiles(
        tile_backward, grad_blocks, my_tiles, my_dst, my_src, tile_total, src_blocks
    )
    spread_out = spread_out.reshape(channels, src_blocks * block_size)
    own_grad = spread_out[:, :row_count]
    halo_terms = (
        spread_out[:, row_count:]
        .astype(bf16)
        .astype(f32)
        .reshape(channels, section_count, halo_width)
    )
    depth_terms = jnp.sum(states * own_grad[None], axis=2) + jnp.sum(
        halo_states * halo_terms[None], axis=(2, 3)
    )
    totals = jnp.concatenate([panel_terms.reshape(-1), depth_terms.reshape(-1)])
    last_send = jnp.concatenate(
        [
            halo_terms.transpose(1, 0, 2).reshape(section_count, channels * halo_width),
            jnp.broadcast_to(totals[None, :], (vert_count, totals.shape[0])),
        ],
        axis=1,
    )
    last_recv = lax.all_to_all(last_send, "vert", split_axis=0, concat_axis=0, tiled=True)
    returned = (
        last_recv[:, : channels * halo_width]
        .reshape(section_count, channels, halo_width)
        .transpose(1, 0, 2)
    )
    totals = jnp.sum(last_recv[:, channels * halo_width :], axis=0)
    grad_mixed = own_grad.at[:, my_send].add(returned)
    grad_states = (depth_weight[:, :, None] * grad_mixed[None]).astype(bf16)
    panel_sum = totals[: panel_terms.size].reshape(panel_terms.shape)
    depth_sum = totals[panel_terms.size :].reshape(depth_terms.shape)
    return (
        layer_out,
        grad_states,
        panel_sum[:, :width] * norm_scale,
        panel_sum[:, width] * norm_scale,
        depth_sum * norm_scale,
    )


def solution(mesh):
    placed = (
        P(None, "feat", "vert"),
        P(None, "feat"),
        P("vert", None, None, None),
        P("vert", None),
        P("vert", None),
        P("vert"),
        P("vert", None, None),
        P(),
        P("feat"),
        P("feat", "vert"),
    )
    return jax.shard_map(
        local,
        mesh=mesh,
        in_specs=placed,
        out_specs=(
            P("feat", "vert"),
            P(None, "feat", "vert"),
            P("feat", None),
            P("feat"),
            P(None, "feat"),
        ),
        check_vma=False,
    )
```

time: 483 us -> 146 us (0.30)
  waiting for transfers between devices: 325 us -> 42.3 us
  blocking collectives: 65.4 us -> 23.3 us
  between operations: 15 us -> 1.73 us
  local copies, waits for them, and re-layouts: 9.02 us -> 20.2 us
    reduce_scatter x1 -> x0, waiting for transfers between devices: 216 us -> none  [local(): lax.psum_scatter(lax.dot_general(weight_rows, aggregated, (((0,), (0,)),...]
    all_gather x1 -> x0, waiting for transfers between devices: 92 us -> none  [local(): piece = lax.all_gather(grad_pre, 'feat', axis=0, tiled=True)]
    psum x1 -> x0, blocking collectives: 65.4 us -> none  [local(): lax.psum((terms_now, bias_terms, depth_terms), 'vert')]
    all_to_all x2 -> x3, waiting for transfers between devices: 17.5 us -> 42.3 us  [the longest x1 17.5 us: local(): lax.all_to_all(second_send, 'feat', split_axis=0, concat_axis=0, tiled=True)]
    all_to_all x0 -> x1, blocking collectives: none -> 23.3 us  [local(): lax.all_to_all(first_send, 'feat', split_axis=0, concat_axis=0, tiled=True)]
    unnamed x23 -> x24, local copies, waits for them, and re-layouts: 2.36 us -> 7.65 us
    all_to_all x2 -> x3, starting transfers between devices: 31.3 us -> 29 us  [the longest x1 16.7 us: local(): lax.all_to_all(states[:, :, my_send], 'vert', split_axis=2, concat_axis=2...]
  transfers between devices with their start and end apart: 4 -> 3, of which waited for: 4 -> 3; matrix products, arithmetic and copies ran while one was open for 0% -> 1% of each run, Pallas kernels for 0% -> 0%
where the time goes in v3:
time: 146 us; the launch traced here: 145 us
  waiting for transfers between devices  42.3 us (29%)
  starting transfers between devices  29 us (20%)
  blocking collectives  23.3 us (16%)
  local copies, waits for them, and re-layouts  20.2 us (14%)
  matrix products  14.6 us (10%)
  other arithmetic  14.1 us (10%)
  between operations  1.73 us (1%)
    all_to_all x1, blocking collectives, local(): lax.all_to_all(first_send, 'feat', split_axis=0, concat_axis=0, tiled=True)  23.3 us
    all_to_all x1, waiting for transfers between devices, local(): lax.all_to_all(second_send, 'feat', split_axis=0, concat_axis=0, tiled=True)  17.5 us
    all_to_all x1, starting transfers between devices, local(): lax.all_to_all(states[:, :, my_send], 'vert', split_axis=2, concat_axis=2...  16.7 us
    all_to_all x1, waiting for transfers between devices, local(): lax.all_to_all(last_send, 'vert', split_axis=0, concat_axis=0, tiled=True)  14.7 us
    all_to_all x1, waiting for transfers between devices, local(): lax.all_to_all(states[:, :, my_send], 'vert', split_axis=2, concat_axis=2...  10.1 us
    scatter-add x1, other arithmetic, local(): grad_mixed = own_grad.at[:, my_send].add(returned)  9.52 us
    dot_general x1, matrix products, tile_forward(): jnp.einsum('dtc,trc->dtr', picked, tile_grp, preferred_element_type=jnp.f...  7.84 us
    unnamed x24, local copies, waits for them, and re-layouts  7.65 us
  transfers between devices with their start and end apart: 3, of which 3 were waited for; matrix products, arithmetic and copies ran while one was open for 1% of the time, Pallas kernels for 0%

profile of v3, /device:TPU:1, one launch (start us, length us, event | category | flops | bytes accessed | tf_op | source)
XLA Modules:
  0.0 145.2 jit_solution(15868895290498655778)
XLA Ops:
  0.7 0.8 compare_select_fusion
  1.5 5.6 %copy.46 = bf16[4,8,4096]{1,0,2:T(4,128)(2,1)} copy(bf16[4,8,4096]{2,1,0:T(8,128)(2,1)} %param.10) | data formatting | bytes 524288 | tf_op args[0]
  7.1 5.6 %gather_fusion = bf16[1536,4,8]{2,1,0:T(4,128)(2,1)S(1)} fusion(bf16[4,8,4096]{1,0,2:T(4,128)(2,1)} %copy.46, s32[2048]{0:T(1024)S(1)} %pad_clamp_fusion), kind=kCustom, calls=%fused_computation | custom fusion | bytes 202752 | tf_op jit(solution)/shard_map/gather | solution.py:72
  12.7 0.7 copy.47
  13.5 0.8 reshape.265
  14.3 16.7 %all-to-all-start = ((bf16[24,2,1024]{2,1,0:T(2,128)(2,1)}), bf16[24,2,1024]{2,1,0:T(2,128)(2,1)S(1)}, u32[]{:S(2)}, u32[]{:S(2)}) async-start(bf16[24,2,1024]{2,1,0:T(2,128)(2,1)} %reshape.265), calls=%async_computation | async-start | bytes 196608 | tf_op jit(solution)/shard_map/all_to_all | solution.py:71
  31.0 0.1 fusion.16
  31.9 10.1 %all-to-all-done = bf16[24,2,1024]{2,1,0:T(2,128)(2,1)S(1)} async-done(((bf16[24,2,1024]{2,1,0:T(2,128)(2,1)}), bf16[24,2,1024]{2,1,0:T(2,128)(2,1)S(1)}, u32[]{:S(2)}, u32[]{:S(2)}) %all-to-all-start) | async-done | bytes 98336 | tf_op jit(solution)/shard_map/all_to_all | solution.py:71
  42.1 0.2 reshape.266
  42.2 0.1 fusion.24
  42.4 0.2 copy.67
  42.6 0.1 copy.49
  42.7 0.8 gather_fusion.1
  43.6 7.8 %fusion.4 = bf16[8,256,128]{2,0,1:T(8,128)(2,1)S(1)} fusion(bf16[1,256,128,128]{3,2,1,0:T(8,128)(2,1)} %param.12, bf16[256,8,128]{2,1,0:T(8,128)(2,1)S(1)} %gather_fusion.1, pred[256]{0:T(512)(128)(4,1)S(1)} %compare_and_fusion.1), kind=kOutput, calls=%fused_computation.8 | convolution fusion | flops 67371008 | bytes 9437440 | tf_op jit(solution)/shard_map/dtc,trc->dtr/dot_general | solution.py:11
  51.4 0.2 fusion.11
  51.8 0.2 copy.51
  52.0 23.3 %all_to_all.27 = f32[32,8,257]{2,1,0:T(8,128)S(1)} all-to-all(f32[32,8,257]{2,1,0:T(8,128)S(1)} %copy.51), channel_id=1, replica_groups=mesh['vert'=24,'feat'=32] {'feat'}, dimensions={0} | all-to-all | bytes 526336 | tf_op jit(solution)/shard_map/all_to_all | solution.py:87
  75.3 0.1 slice_reduce_fusion.2
  75.4 0.1 copy.68
  75.5 0.3 convert_reduce_fusion
  75.8 0.2 convolution_bitcast_fusion
  76.0 0.2 fusion.13
  76.2 0.1 copy.54
  76.3 0.1 copy.52
  76.4 0.2 reshape.256
  76.6 0.9 pad_maximum_fusion
  77.5 5.0 %all-to-all-start.2 = ((f32[32,8,513]{2,1,0:T(8,128)}), f32[32,8,513]{2,1,0:T(8,128)S(1)}, u32[]{:S(2)}, u32[]{:S(2)}) async-start(f32[32,8,513]{2,1,0:T(8,128)} %pad_maximum_fusion), calls=%async_computation.2 | async-start | bytes 1310720 | tf_op jit(solution)/shard_map/all_to_all | solution.py:115
  82.5 17.5 %all-to-all-done.2 = f32[32,8,513]{2,1,0:T(8,128)S(1)} async-done(((f32[32,8,513]{2,1,0:T(8,128)}), f32[32,8,513]{2,1,0:T(8,128)S(1)}, u32[]{:S(2)}, u32[]{:S(2)}) %all-to-all-start.2) | async-done | bytes 525344 | tf_op jit(solution)/shard_map/all_to_all | solution.py:115
  100.0 0.6 slice_bitcast_fusion
  100.7 0.8 gather_fusion.2
  101.5 5.7 %fusion.7 = bf16[8,256,128]{2,0,1:T(8,128)(2,1)S(1)} fusion(bf16[1,256,128,128]{3,2,1,0:T(8,128)(2,1)} %param.12, bf16[256,8,128]{2,1,0:T(8,128)(2,1)S(1)} %gather_fusion.2, pred[256]{0:T(512)(128)(4,1)S(1)} %compare_and_fusion), kind=kOutput, calls=%fused_computation.9 | convolution fusion | flops 67371008 | bytes 9437440 | tf_op jit(solution)/shard_map/dtr,trc->dtc/dot_general | solution.py:20
  107.2 0.2 convolution_bitcast_fusion.1
  107.5 0.1 reshape.217
  107.6 0.1 fusion.25
  107.8 0.2 fusion.17
  107.9 0.1 add.97
  108.1 0.1 reshape.208
  108.3 0.9 all_to_all.20
  109.2 7.3 %all-to-all-start.3 = ((f32[24,1,2600]{2,1,0:T(1,128)}), f32[24,1,2600]{2,1,0:T(1,128)S(1)}, u32[]{:S(2)}, u32[]{:S(2)}) async-start(f32[24,1,2600]{2,1,0:T(1,128)} %all_to_all.20), calls=%async_computation.3 | async-start | bytes 516096 | tf_op jit(solution)/shard_map/all_to_all | solution.py:143
  116.5 0.6 copy.69
  117.1 14.7 %all-to-all-done.3 = f32[24,1,2600]{2,1,0:T(1,128)S(1)} async-done(((f32[24,1,2600]{2,1,0:T(1,128)}), f32[24,1,2600]{2,1,0:T(1,128)S(1)}, u32[]{:S(2)}, u32[]{:S(2)}) %all-to-all-start.3) | async-done | bytes 249632 | tf_op jit(solution)/shard_map/all_to_all | solution.py:143
  132.0 0.6 slice_multiply_fusion
  132.6 0.6 fusion.40
  133.3 0.3 copy.64
  133.6 9.5 %scatter_fusion = f32[8,4096]{0,1:T(8,128)S(1)} fusion(f32[8,4096]{0,1:T(8,128)S(1)} %copy.69, s32[1536]{0:T(1024)S(1)} %reshape.222, f32[1536,8]{1,0:T(8,128)S(1)} %bitcast.99), kind=kCustom, calls=%fused_computation.3 | custom fusion | flops 12288 | bytes 153600 | tf_op jit(solution)/shard_map/scatter-add | solution.py:150
  143.2 0.6 copy.63
  143.7 0.8 multiply_convert_fusion
  144.5 0.7 mul.96
  (46 shorter events, 1.0 us)
Async XLA Ops:
  0.6 74.9 %copy-start = (bf16[256,256]{1,0:T(8,128)(2,1)S(1)}, bf16[256,256]{1,0:T(8,128)(2,1)}, u32[]{:S(2)}) copy-start(bf16[256,256]{1,0:T(8,128)(2,1)} %param.17) | copy-start | bytes 393220
  0.6 30.4 %copy-start.1 = (bf16[4,8,4096]{2,1,0:T(8,128)(2,1)S(1)}, bf16[4,8,4096]{2,1,0:T(8,128)(2,1)}, u32[]{:S(2)}) copy-start(bf16[4,8,4096]{2,1,0:T(8,128)(2,1)} %param.10) | copy-start | bytes 786436
  0.7 30.4 %copy-start.3 = (f32[4,8]{1,0:T(4,128)S(1)}, f32[4,8]{1,0:T(4,128)}, u32[]{:S(2)}) copy-start(f32[4,8]{1,0:T(4,128)} %param.11) | copy-start | bytes 388
  0.7 30.5 %copy-start.5 = (s32[1,256]{1,0:T(1,128)S(1)}, s32[1,256]{1,0:T(1,128)}, u32[]{:S(2)}) copy-start(s32[1,256]{1,0:T(1,128)} %param.14) | copy-start | bytes 3076
  0.7 31.1 %copy-start.2 = (bf16[8,4096]{1,0:T(8,128)(2,1)S(1)}, bf16[8,4096]{1,0:T(8,128)(2,1)}, u32[]{:S(2)}) copy-start(bf16[8,4096]{1,0:T(8,128)(2,1)} %param.19) | copy-start | bytes 196612
  14.3 27.8 %all-to-all-start = ((bf16[24,2,1024]{2,1,0:T(2,128)(2,1)}), bf16[24,2,1024]{2,1,0:T(2,128)(2,1)S(1)}, u32[]{:S(2)}, u32[]{:S(2)}) async-start(bf16[24,2,1024]{2,1,0:T(2,128)(2,1)} %reshape.265), calls=%async_computation | async-start | bytes 196608 | tf_op jit(solution)/shard_map/all_to_all | solution.py:71
  43.6 7.9 %copy-start.4 = (s32[1,256]{1,0:T(1,128)S(1)}, s32[1,256]{1,0:T(1,128)}, u32[]{:S(2)}) copy-start(s32[1,256]{1,0:T(1,128)} %param.13) | copy-start | bytes 3076
  43.6 8.1 %copy-start.6 = (f32[8]{0:T(128)S(1)}, f32[8]{0:T(128)}, u32[]{:S(2)}) copy-start(f32[8]{0:T(128)} %param.18) | copy-start | bytes 100
  77.5 22.5 %all-to-all-start.2 = ((f32[32,8,513]{2,1,0:T(8,128)}), f32[32,8,513]{2,1,0:T(8,128)S(1)}, u32[]{:S(2)}, u32[]{:S(2)}) async-start(f32[32,8,513]{2,1,0:T(8,128)} %pad_maximum_fusion), calls=%async_computation.2 | async-start | bytes 1310720 | tf_op jit(solution)/shard_map/all_to_all | solution.py:115
  109.2 22.6 %all-to-all-start.3 = ((f32[24,1,2600]{2,1,0:T(1,128)}), f32[24,1,2600]{2,1,0:T(1,128)S(1)}, u32[]{:S(2)}, u32[]{:S(2)}) async-start(f32[24,1,2600]{2,1,0:T(1,128)} %all_to_all.20), calls=%async_computation.3 | async-start | bytes 516096 | tf_op jit(solution)/shard_map/all_to_all | solution.py:143

commit v4 on v3

--- a/solution.py
+++ b/solution.py
@@ -68,8 +68,14 @@
     def from_blocks(x):
         return x.transpose(1, 0, 2).reshape(channels, row_count)
 
+    state_count = states.shape[0]
+    listed = jnp.take(states.reshape(state_count * channels, row_count), my_send.reshape(-1), axis=1)
     halo_states = lax.all_to_all(
-        states[:, :, my_send], "vert", split_axis=2, concat_axis=2, tiled=True
+        listed.reshape(state_count, channels, section_count, halo_width),
+        "vert",
+        split_axis=2,
+        concat_axis=2,
+        tiled=True,
     )
     mixed_state = jnp.sum(depth_weight[:, :, None] * states, axis=0).astype(bf16)
     mixed_halo = jnp.sum(depth_weight[:, :, None, None] * halo_states, axis=0).astype(bf16)

time: 146 us -> 140 us (0.959)
  local copies, waits for them, and re-layouts: 20.2 us -> 13.8 us
  other arithmetic: 14.1 us -> 18 us
  waiting for transfers between devices: 42.3 us -> 39.1 us
    unnamed x24 -> x21, local copies, waits for them, and re-layouts: 7.65 us -> 1.82 us
    all_to_all x1, waiting for transfers between devices: 10.1 us -> 7.04 us  [local(): lax.all_to_all(listed.reshape(state_count, channels, section_count, halo_...]
    gather x2 -> x3, local copies, waits for them, and re-layouts: 6.34 us -> 3.52 us  [local(): jnp.take(states.reshape(state_count * channels, row_count), my_send.resha...]
  transfers between devices with their start and end apart: 3 -> 3, of which waited for: 3 -> 3; matrix products, arithmetic and copies ran while one was open for 1% -> 3% of each run, Pallas kernels for 0% -> 0%
where the time goes in v4:
time: 140 us; the launch traced here: 139 us
  waiting for transfers between devices  39.1 us (28%)
  starting transfers between devices  29 us (21%)
  blocking collectives  23.3 us (17%)
  other arithmetic  18 us (13%)
  matrix products  14.6 us (10%)
  local copies, waits for them, and re-layouts  13.8 us (10%)
  between operations  1.72 us (1%)
    all_to_all x1, blocking collectives, local(): lax.all_to_all(first_send, 'feat', split_axis=0, concat_axis=0, tiled=True)  23.3 us
    all_to_all x1, waiting for transfers between devices, local(): lax.all_to_all(second_send, 'feat', split_axis=0, concat_axis=0, tiled=True)  17.5 us
    all_to_all x1, starting transfers between devices, local(): lax.all_to_all(listed.reshape(state_count, channels, section_count, halo_...  16.7 us
    all_to_all x1, waiting for transfers between devices, local(): lax.all_to_all(last_send, 'vert', split_axis=0, concat_axis=0, tiled=True)  14.6 us
    scatter-add x1, other arithmetic, local(): grad_mixed = own_grad.at[:, my_send].add(returned)  9.52 us
    dot_general x1, matrix products, tile_forward(): jnp.einsum('dtc,trc->dtr', picked, tile_grp, preferred_element_type=jnp.f...  7.83 us
    all_to_all x1, starting transfers between devices, local(): lax.all_to_all(last_send, 'vert', split_axis=0, concat_axis=0, tiled=True)  7.27 us
    all_to_all x1, waiting for transfers between devices, local(): lax.all_to_all(listed.reshape(state_count, channels, section_count, halo_...  7.04 us
  transfers between devices with their start and end apart: 3, of which 3 were waited for; matrix products, arithmetic and copies ran while one was open for 3% of the time, Pallas kernels for 0%

profile of v4, /device:TPU:1, one launch (start us, length us, event | category | flops | bytes accessed | tf_op | source)
XLA Modules:
  0.0 139.4 jit_solution(1976832751429390836)
XLA Ops:
  0.7 0.8 compare_and_fusion
  1.4 0.8 reshape_squeeze.6
  2.3 1.4 %copy.82 = bf16[32,4096]{0,1:T(8,128)(2,1)S(1)} copy(bf16[32,4096]{1,0:T(8,128)(2,1)} %bitcast.94) | data formatting | bytes 524288 | tf_op jit(solution)/shard_map/reshape | solution.py:72
  3.7 3.2 %gather_fusion = bf16[1536,32]{1,0:T(8,128)(2,1)S(1)} fusion(bf16[32,4096]{0,1:T(8,128)(2,1)S(1)} %copy.82, s32[2048]{0:T(1024)S(1)} %pad_clamp_fusion), kind=kCustom, calls=%fused_computation | custom fusion | bytes 202752 | tf_op jit(solution)/shard_map/jit(_take)/gather | solution.py:72
  6.9 0.2 copy.83
  7.1 0.2 gather.15
  7.3 0.8 reshape.310
  8.1 16.7 %all-to-all-start = ((bf16[24,2,1024]{2,1,0:T(2,128)(2,1)}), bf16[24,2,1024]{2,1,0:T(2,128)(2,1)S(1)}, u32[]{:S(2)}, u32[]{:S(2)}) async-start(bf16[24,2,1024]{2,1,0:T(2,128)(2,1)} %reshape.310), calls=%async_computation | async-start | bytes 196608 | tf_op jit(solution)/shard_map/all_to_all | solution.py:73
  25.4 0.7 compare_select_fusion.4
  26.1 1.1 fusion.16
  27.2 0.9 convert_bitcast_fusion
  28.1 0.7 compare_and_fusion.2
  28.8 7.0 %all-to-all-done = bf16[24,2,1024]{2,1,0:T(2,128)(2,1)S(1)} async-done(((bf16[24,2,1024]{2,1,0:T(2,128)(2,1)}), bf16[24,2,1024]{2,1,0:T(2,128)(2,1)S(1)}, u32[]{:S(2)}, u32[]{:S(2)}) %all-to-all-start) | async-done | bytes 98336 | tf_op jit(solution)/shard_map/all_to_all | solution.py:73
  35.8 0.2 reshape.311
  36.0 0.8 fusion.24
  36.9 0.1 convert_element_type.77
  37.0 0.8 gather_fusion.1
  37.8 7.8 %fusion.4 = bf16[8,256,128]{2,0,1:T(8,128)(2,1)S(1)} fusion(bf16[1,256,128,128]{3,2,1,0:T(8,128)(2,1)} %param.12, bf16[256,8,128]{2,1,0:T(8,128)(2,1)S(1)} %gather_fusion.1, pred[256]{0:T(512)(128)(4,1)S(1)} %compare_and_fusion.2), kind=kOutput, calls=%fused_computation.8 | convolution fusion | flops 67371008 | bytes 9437440 | tf_op jit(solution)/shard_map/dtc,trc->dtr/dot_general | solution.py:11
  45.6 0.2 fusion.11
  46.0 0.2 copy.87
  46.2 23.3 %all_to_all.27 = f32[32,8,257]{2,1,0:T(8,128)S(1)} all-to-all(f32[32,8,257]{2,1,0:T(8,128)S(1)} %copy.87), channel_id=1, replica_groups=mesh['vert'=24,'feat'=32] {'feat'}, dimensions={0} | all-to-all | bytes 526336 | tf_op jit(solution)/shard_map/all_to_all | solution.py:93
  69.5 0.1 slice_reduce_fusion.2
  69.6 0.1 copy.103
  69.7 0.3 convert_reduce_fusion
  70.0 0.2 convolution_bitcast_fusion
  70.2 0.2 fusion.13
  70.4 0.2 reshape.300
  70.7 0.1 copy.90
  70.8 0.9 pad_maximum_fusion
  71.7 5.0 %all-to-all-start.2 = ((f32[32,8,513]{2,1,0:T(8,128)}), f32[32,8,513]{2,1,0:T(8,128)S(1)}, u32[]{:S(2)}, u32[]{:S(2)}) async-start(f32[32,8,513]{2,1,0:T(8,128)} %pad_maximum_fusion), calls=%async_computation.2 | async-start | bytes 1310720 | tf_op jit(solution)/shard_map/all_to_all | solution.py:121
  76.7 17.5 %all-to-all-done.2 = f32[32,8,513]{2,1,0:T(8,128)S(1)} async-done(((f32[32,8,513]{2,1,0:T(8,128)}), f32[32,8,513]{2,1,0:T(8,128)S(1)}, u32[]{:S(2)}, u32[]{:S(2)}) %all-to-all-start.2) | async-done | bytes 525344 | tf_op jit(solution)/shard_map/all_to_all | solution.py:121
  94.2 0.6 slice_bitcast_fusion
  94.9 0.8 gather_fusion.2
  95.7 5.7 %fusion.7 = bf16[8,256,128]{2,0,1:T(8,128)(2,1)S(1)} fusion(bf16[1,256,128,128]{3,2,1,0:T(8,128)(2,1)} %param.12, bf16[256,8,128]{2,1,0:T(8,128)(2,1)S(1)} %gather_fusion.2, pred[256]{0:T(512)(128)(4,1)S(1)} %compare_and_fusion.1), kind=kOutput, calls=%fused_computation.9 | convolution fusion | flops 67371008 | bytes 9437440 | tf_op jit(solution)/shard_map/dtr,trc->dtc/dot_general | solution.py:20
  101.4 0.2 convolution_bitcast_fusion.1
  101.9 0.2 fusion.17
  102.1 0.1 fusion.25
  102.5 0.9 all_to_all.20
  103.4 7.3 %all-to-all-start.3 = ((f32[24,1,2600]{2,1,0:T(1,128)}), f32[24,1,2600]{2,1,0:T(1,128)S(1)}, u32[]{:S(2)}, u32[]{:S(2)}) async-start(f32[24,1,2600]{2,1,0:T(1,128)} %all_to_all.20), calls=%async_computation.3 | async-start | bytes 516096 | tf_op jit(solution)/shard_map/all_to_all | solution.py:149
  110.8 0.6 copy.104
  111.4 14.6 %all-to-all-done.3 = f32[24,1,2600]{2,1,0:T(1,128)S(1)} async-done(((f32[24,1,2600]{2,1,0:T(1,128)}), f32[24,1,2600]{2,1,0:T(1,128)S(1)}, u32[]{:S(2)}, u32[]{:S(2)}) %all-to-all-start.3) | async-done | bytes 249632 | tf_op jit(solution)/shard_map/all_to_all | solution.py:149
  126.2 0.6 fusion.41
  126.9 0.6 slice_multiply_fusion
  127.5 0.7 mul.96
  128.2 0.3 copy.100
  128.5 9.5 %scatter_fusion = f32[8,4096]{0,1:T(8,128)S(1)} fusion(f32[8,4096]{0,1:T(8,128)S(1)} %copy.104, s32[1536]{0:T(1024)S(1)} %reshape.291, f32[1536,8]{1,0:T(8,128)S(1)} %bitcast.101), kind=kCustom, calls=%fused_computation.3 | custom fusion | flops 12288 | bytes 153600 | tf_op jit(solution)/shard_map/scatter-add | solution.py:156
  138.0 0.6 copy.99
  138.6 0.8 multiply_convert_fusion
  (51 shorter events, 1.4 us)
Async XLA Ops:
  0.6 69.1 %copy-start = (bf16[256,256]{1,0:T(8,128)(2,1)S(1)}, bf16[256,256]{1,0:T(8,128)(2,1)}, u32[]{:S(2)}) copy-start(bf16[256,256]{1,0:T(8,128)(2,1)} %param.17) | copy-start | bytes 393220
  0.6 45.0 %copy-start.4 = (s32[1,256]{1,0:T(1,128)S(1)}, s32[1,256]{1,0:T(1,128)}, u32[]{:S(2)}) copy-start(s32[1,256]{1,0:T(1,128)} %param.13) | copy-start | bytes 3076
  2.2 43.6 %copy-start.6 = (f32[8]{0:T(128)S(1)}, f32[8]{0:T(128)}, u32[]{:S(2)}) copy-start(f32[8]{0:T(128)} %param.18) | copy-start | bytes 100
  8.1 27.8 %all-to-all-start = ((bf16[24,2,1024]{2,1,0:T(2,128)(2,1)}), bf16[24,2,1024]{2,1,0:T(2,128)(2,1)S(1)}, u32[]{:S(2)}, u32[]{:S(2)}) async-start(bf16[24,2,1024]{2,1,0:T(2,128)(2,1)} %reshape.310), calls=%async_computation | async-start | bytes 196608 | tf_op jit(solution)/shard_map/all_to_all | solution.py:73
  69.7 31.7 %copy-start.5 = (s32[1,256]{1,0:T(1,128)S(1)}, s32[1,256]{1,0:T(1,128)}, u32[]{:S(2)}) copy-start(s32[1,256]{1,0:T(1,128)} %param.14) | copy-start | bytes 3076
  70.6 31.3 %copy-start.1 = (bf16[4,8,4096]{2,1,0:T(8,128)(2,1)S(1)}, bf16[4,8,4096]{2,1,0:T(8,128)(2,1)}, u32[]{:S(2)}) copy-start(bf16[4,8,4096]{2,1,0:T(8,128)(2,1)} %param.10) | copy-start | bytes 786436
  71.7 22.5 %all-to-all-start.2 = ((f32[32,8,513]{2,1,0:T(8,128)}), f32[32,8,513]{2,1,0:T(8,128)S(1)}, u32[]{:S(2)}, u32[]{:S(2)}) async-start(f32[32,8,513]{2,1,0:T(8,128)} %pad_maximum_fusion), calls=%async_computation.2 | async-start | bytes 1310720 | tf_op jit(solution)/shard_map/all_to_all | solution.py:121
  76.7 34.0 %copy-start.2 = (s32[1,24,64]{2,1,0:T(8,128)S(1)}, s32[1,24,64]{2,1,0:T(8,128)}, u32[]{:S(2)}) copy-start(s32[1,24,64]{2,1,0:T(8,128)} %param.16) | copy-start | bytes 18436
  101.4 37.2 %copy-start.3 = (f32[4,8]{1,0:T(4,128)S(1)}, f32[4,8]{1,0:T(4,128)}, u32[]{:S(2)}) copy-start(f32[4,8]{1,0:T(4,128)} %param.11) | copy-start | bytes 388
  103.4 22.6 %all-to-all-start.3 = ((f32[24,1,2600]{2,1,0:T(1,128)}), f32[24,1,2600]{2,1,0:T(1,128)S(1)}, u32[]{:S(2)}, u32[]{:S(2)}) async-start(f32[24,1,2600]{2,1,0:T(1,128)} %all_to_all.20), calls=%async_computation.3 | async-start | bytes 516096 | tf_op jit(solution)/shard_map/all_to_all | solution.py:149

commit v5 on v4

--- a/solution.py
+++ b/solution.py
@@ -153,7 +153,16 @@
         .transpose(1, 0, 2)
     )
     totals = jnp.sum(last_recv[:, channels * halo_width :], axis=0)
-    grad_mixed = own_grad.at[:, my_send].add(returned)
+    hot = (
+        my_send.reshape(-1)[None, :] == jnp.arange(row_count, dtype=jnp.int32)[:, None]
+    ).astype(bf16)
+    added = lax.dot_general(
+        hot,
+        returned.reshape(channels, -1).astype(bf16),
+        (((1,), (1,)), ((), ())),
+        preferred_element_type=f32,
+    )
+    grad_mixed = own_grad + added.T
     grad_states = (depth_weight[:, :, None] * grad_mixed[None]).astype(bf16)
     panel_sum = totals[: panel_terms.size].reshape(panel_terms.shape)
     depth_sum = totals[panel_terms.size :].reshape(depth_terms.shape)

time: 140 us -> 134 us (0.957)
  other arithmetic: 18 us -> 8.47 us
  matrix products: 14.6 us -> 18.8 us
    scatter-add x1 -> x0, other arithmetic: 9.52 us -> none  [local(): grad_mixed = own_grad.at[:, my_send].add(returned)]
    dot_general x0 -> x1, matrix products: none -> 4.22 us  [local(): lax.dot_general(hot, returned.reshape(channels, -1).astype(bf16), (((1,),...]
where the time goes in v5:
time: 134 us; the launch traced here: 133 us
  waiting for transfers between devices  39.8 us (30%)
  starting transfers between devices  29 us (22%)
  blocking collectives  23.3 us (17%)
  matrix products  18.8 us (14%)
  local copies, waits for them, and re-layouts  12.5 us (9%)
  other arithmetic  8.47 us (6%)
  between operations  1.71 us (1%)
    all_to_all x1, blocking collectives, local(): lax.all_to_all(first_send, 'feat', split_axis=0, concat_axis=0, tiled=True)  23.3 us
    all_to_all x1, waiting for transfers between devices, local(): lax.all_to_all(second_send, 'feat', split_axis=0, concat_axis=0, tiled=True)  17.5 us
    all_to_all x1, starting transfers between devices, local(): lax.all_to_all(listed.reshape(state_count, channels, section_count, halo_...  16.7 us
    all_to_all x1, waiting for transfers between devices, local(): lax.all_to_all(last_send, 'vert', split_axis=0, concat_axis=0, tiled=True)  15.2 us
    dot_general x1, matrix products, tile_forward(): jnp.einsum('dtc,trc->dtr', picked, tile_grp, preferred_element_type=jnp.f...  7.83 us
    all_to_all x1, starting transfers between devices, local(): lax.all_to_all(last_send, 'vert', split_axis=0, concat_axis=0, tiled=True)  7.28 us
    all_to_all x1, waiting for transfers between devices, local(): lax.all_to_all(listed.reshape(state_count, channels, section_count, halo_...  7.04 us
    dot_general x1, matrix products, tile_backward(): jnp.einsum('dtr,trc->dtc', picked, tile_grp, preferred_element_type=jnp.f...  5.71 us
  transfers between devices with their start and end apart: 3, of which 3 were waited for; matrix products, arithmetic and copies ran while one was open for 3% of the time, Pallas kernels for 0%

profile of v5, /device:TPU:1, one launch (start us, length us, event | category | flops | bytes accessed | tf_op | source)
XLA Modules:
  0.0 133.4 jit_solution(3155590194324584181)
XLA Ops:
  0.7 0.8 compare_and_fusion
  1.4 0.8 reshape_squeeze.8
  2.3 1.4 %copy.64 = bf16[32,4096]{0,1:T(8,128)(2,1)S(1)} copy(bf16[32,4096]{1,0:T(8,128)(2,1)} %bitcast.90) | data formatting | bytes 524288 | tf_op jit(solution)/shard_map/reshape | solution.py:72
  3.7 3.2 %gather_fusion = bf16[1536,32]{1,0:T(8,128)(2,1)S(1)} fusion(bf16[32,4096]{0,1:T(8,128)(2,1)S(1)} %copy.64, s32[2048]{0:T(1024)S(1)} %pad_clamp_fusion), kind=kCustom, calls=%fused_computation | custom fusion | bytes 202752 | tf_op jit(solution)/shard_map/jit(_take)/gather | solution.py:72
  6.9 0.2 copy.65
  7.1 0.2 gather.15
  7.3 0.8 reshape.274
  8.1 16.7 %all-to-all-start = ((bf16[24,2,1024]{2,1,0:T(2,128)(2,1)}), bf16[24,2,1024]{2,1,0:T(2,128)(2,1)S(1)}, u32[]{:S(2)}, u32[]{:S(2)}) async-start(bf16[24,2,1024]{2,1,0:T(2,128)(2,1)} %reshape.274), calls=%async_computation | async-start | bytes 196608 | tf_op jit(solution)/shard_map/all_to_all | solution.py:73
  25.4 0.7 compare_select_fusion.3
  26.1 1.1 fusion.19
  27.2 0.9 convert_bitcast_fusion
  28.1 0.7 compare_and_fusion.2
  28.8 7.0 %all-to-all-done = bf16[24,2,1024]{2,1,0:T(2,128)(2,1)S(1)} async-done(((bf16[24,2,1024]{2,1,0:T(2,128)(2,1)}), bf16[24,2,1024]{2,1,0:T(2,128)(2,1)S(1)}, u32[]{:S(2)}, u32[]{:S(2)}) %all-to-all-start) | async-done | bytes 98336 | tf_op jit(solution)/shard_map/all_to_all | solution.py:73
  35.8 0.2 reshape.275
  36.0 0.8 fusion.27
  36.9 0.1 convert_element_type.88
  37.0 0.8 gather_fusion.1
  37.8 7.8 %fusion.7 = bf16[8,256,128]{2,0,1:T(8,128)(2,1)S(1)} fusion(bf16[1,256,128,128]{3,2,1,0:T(8,128)(2,1)} %param.12, bf16[256,8,128]{2,1,0:T(8,128)(2,1)S(1)} %gather_fusion.1, pred[256]{0:T(512)(128)(4,1)S(1)} %compare_and_fusion.2), kind=kOutput, calls=%fused_computation.11 | convolution fusion | flops 67371008 | bytes 9437440 | tf_op jit(solution)/shard_map/dtc,trc->dtr/dot_general | solution.py:11
  45.6 0.2 fusion.14
  46.0 0.2 copy.69
  46.2 23.3 %all_to_all.27 = f32[32,8,257]{2,1,0:T(8,128)S(1)} all-to-all(f32[32,8,257]{2,1,0:T(8,128)S(1)} %copy.69), channel_id=1, replica_groups=mesh['vert'=24,'feat'=32] {'feat'}, dimensions={0} | all-to-all | bytes 526336 | tf_op jit(solution)/shard_map/all_to_all | solution.py:93
  69.5 0.1 slice_reduce_fusion.2
  69.6 0.1 copy.79
  69.7 0.3 convert_reduce_fusion
  70.0 0.2 convolution_bitcast_fusion
  70.2 0.2 fusion.16
  70.4 0.2 reshape.264
  70.6 0.1 copy.70
  70.7 0.1 copy.72
  70.8 0.9 pad_maximum_fusion
  71.7 5.0 %all-to-all-start.2 = ((f32[32,8,513]{2,1,0:T(8,128)}), f32[32,8,513]{2,1,0:T(8,128)S(1)}, u32[]{:S(2)}, u32[]{:S(2)}) async-start(f32[32,8,513]{2,1,0:T(8,128)} %pad_maximum_fusion), calls=%async_computation.2 | async-start | bytes 1310720 | tf_op jit(solution)/shard_map/all_to_all | solution.py:121
  76.7 17.5 %all-to-all-done.2 = f32[32,8,513]{2,1,0:T(8,128)S(1)} async-done(((f32[32,8,513]{2,1,0:T(8,128)}), f32[32,8,513]{2,1,0:T(8,128)S(1)}, u32[]{:S(2)}, u32[]{:S(2)}) %all-to-all-start.2) | async-done | bytes 525344 | tf_op jit(solution)/shard_map/all_to_all | solution.py:121
  94.2 0.6 slice_bitcast_fusion
  94.9 0.8 gather_fusion.2
  95.7 5.7 %fusion.10 = bf16[8,256,128]{2,0,1:T(8,128)(2,1)S(1)} fusion(bf16[1,256,128,128]{3,2,1,0:T(8,128)(2,1)} %param.12, bf16[256,8,128]{2,1,0:T(8,128)(2,1)S(1)} %gather_fusion.2, pred[256]{0:T(512)(128)(4,1)S(1)} %compare_and_fusion.1), kind=kOutput, calls=%fused_computation.12 | convolution fusion | flops 67371008 | bytes 9437440 | tf_op jit(solution)/shard_map/dtr,trc->dtc/dot_general | solution.py:20
  101.4 0.2 convolution_bitcast_fusion.1
  102.0 0.1 fusion.28
  102.2 0.2 fusion.20
  102.6 0.9 all_to_all.20
  103.4 7.3 %all-to-all-start.3 = ((f32[24,1,2600]{2,1,0:T(1,128)}), f32[24,1,2600]{2,1,0:T(1,128)S(1)}, u32[]{:S(2)}, u32[]{:S(2)}) async-start(f32[24,1,2600]{2,1,0:T(1,128)} %all_to_all.20), calls=%async_computation.3 | async-start | bytes 516096 | tf_op jit(solution)/shard_map/all_to_all | solution.py:149
  110.8 15.2 %all-to-all-done.3 = f32[24,1,2600]{2,1,0:T(1,128)S(1)} async-done(((f32[24,1,2600]{2,1,0:T(1,128)}), f32[24,1,2600]{2,1,0:T(1,128)S(1)}, u32[]{:S(2)}, u32[]{:S(2)}) %all-to-all-start.3) | async-done | bytes 249632 | tf_op jit(solution)/shard_map/all_to_all | solution.py:149
  126.3 0.6 fusion.44
  126.9 0.6 slice_multiply_fusion
  127.5 0.7 mul.96
  128.2 0.1 convert_element_type.102
  128.3 0.1 convert_element_type.104
  128.4 4.2 %fusion.6 = f32[8,4096]{1,0:T(8,128)S(1)} fusion(bf16[8,1536]{1,0:T(8,128)(2,1)S(1)} %convert_element_type.104, s32[1536]{0:T(1024)S(1)} %reshape_squeeze.9, f32[8,5632]{1,0:T(8,128)S(1)} %bitcast.101), kind=kOutput, calls=%fused_computation.10 | convolution fusion | flops 106987520 | bytes 292864 | tf_op jit(solution)/shard_map/dot_general | solution.py:159
  132.6 0.8 multiply_convert_fusion
  (49 shorter events, 1.2 us)
Async XLA Ops:
  0.6 69.1 %copy-start = (bf16[256,256]{1,0:T(8,128)(2,1)S(1)}, bf16[256,256]{1,0:T(8,128)(2,1)}, u32[]{:S(2)}) copy-start(bf16[256,256]{1,0:T(8,128)(2,1)} %param.17) | copy-start | bytes 393220
  0.6 45.0 %copy-start.4 = (s32[1,256]{1,0:T(1,128)S(1)}, s32[1,256]{1,0:T(1,128)}, u32[]{:S(2)}) copy-start(s32[1,256]{1,0:T(1,128)} %param.13) | copy-start | bytes 3076
  2.2 43.6 %copy-start.6 = (f32[8]{0:T(128)S(1)}, f32[8]{0:T(128)}, u32[]{:S(2)}) copy-start(f32[8]{0:T(128)} %param.18) | copy-start | bytes 100
  8.1 27.8 %all-to-all-start = ((bf16[24,2,1024]{2,1,0:T(2,128)(2,1)}), bf16[24,2,1024]{2,1,0:T(2,128)(2,1)S(1)}, u32[]{:S(2)}, u32[]{:S(2)}) async-start(bf16[24,2,1024]{2,1,0:T(2,128)(2,1)} %reshape.274), calls=%async_computation | async-start | bytes 196608 | tf_op jit(solution)/shard_map/all_to_all | solution.py:73
  69.7 31.7 %copy-start.5 = (s32[1,256]{1,0:T(1,128)S(1)}, s32[1,256]{1,0:T(1,128)}, u32[]{:S(2)}) copy-start(s32[1,256]{1,0:T(1,128)} %param.14) | copy-start | bytes 3076
  70.8 31.4 %copy-start.1 = (bf16[4,8,4096]{2,1,0:T(8,128)(2,1)S(1)}, bf16[4,8,4096]{2,1,0:T(8,128)(2,1)}, u32[]{:S(2)}) copy-start(bf16[4,8,4096]{2,1,0:T(8,128)(2,1)} %param.10) | copy-start | bytes 786436
  71.7 22.5 %all-to-all-start.2 = ((f32[32,8,513]{2,1,0:T(8,128)}), f32[32,8,513]{2,1,0:T(8,128)S(1)}, u32[]{:S(2)}, u32[]{:S(2)}) async-start(f32[32,8,513]{2,1,0:T(8,128)} %pad_maximum_fusion), calls=%async_computation.2 | async-start | bytes 1310720 | tf_op jit(solution)/shard_map/all_to_all | solution.py:121
  76.7 34.1 %copy-start.2 = (s32[1,24,64]{2,1,0:T(8,128)S(1)}, s32[1,24,64]{2,1,0:T(8,128)}, u32[]{:S(2)}) copy-start(s32[1,24,64]{2,1,0:T(8,128)} %param.16) | copy-start | bytes 18436
  95.7 36.9 %copy-start.3 = (f32[4,8]{1,0:T(4,128)S(1)}, f32[4,8]{1,0:T(4,128)}, u32[]{:S(2)}) copy-start(f32[4,8]{1,0:T(4,128)} %param.11) | copy-start | bytes 388
  103.4 22.6 %all-to-all-start.3 = ((f32[24,1,2600]{2,1,0:T(1,128)}), f32[24,1,2600]{2,1,0:T(1,128)S(1)}, u32[]{:S(2)}, u32[]{:S(2)}) async-start(f32[24,1,2600]{2,1,0:T(1,128)} %all_to_all.20), calls=%async_computation.3 | async-start | bytes 516096 | tf_op jit(solution)/shard_map/all_to_all | solution.py:149

commit v6 on v5

--- a/solution.py
+++ b/solution.py
@@ -28,6 +28,24 @@
     capacity = tile_values.shape[0]
     live_mask = jnp.arange(capacity, dtype=jnp.int32) < tile_total
     return kernel(source, tile_values, tile_dst, tile_src, live_mask, out_blocks)
+
+
+def bf16_parts(x, count):
+    parts = []
+    rest = x
+    for _ in range(count - 1):
+        head = lax.reduce_precision(rest, exponent_bits=8, mantissa_bits=7)
+        parts.append(head.astype(jnp.bfloat16))
+        rest = rest - head
+    parts.append(rest.astype(jnp.bfloat16))
+    return parts
+
+
+def parts_sum(parts):
+    total = parts[0].astype(jnp.float32)
+    for part in parts[1:]:
+        total = total + part.astype(jnp.float32)
+    return total
 
 
 def local(
@@ -86,15 +104,15 @@
     )
     aggregated = aggregated.reshape(channels, row_count).astype(bf16)
 
-    bias_cols = jnp.broadcast_to(bias_vec[None, :, None], (feat_count, channels, 1))
-    first_send = jnp.concatenate(
-        [to_blocks(aggregated).astype(f32), to_blocks(cotangent).astype(f32), bias_cols], axis=2
-    )
+    bias_cols = jnp.broadcast_to(
+        jnp.stack(bf16_parts(bias_vec, 3), axis=1)[None], (feat_count, channels, 3)
+    )
+    first_send = jnp.concatenate([to_blocks(aggregated), to_blocks(cotangent), bias_cols], axis=2)
     first_recv = lax.all_to_all(first_send, "feat", split_axis=0, concat_axis=0, tiled=True)
     first_recv = first_recv.reshape(feat_count * channels, -1)
-    agg_block = first_recv[:, :col_width].astype(bf16)
-    cot_block = first_recv[:, col_width : 2 * col_width]
-    bias_full = first_recv[:, 2 * col_width]
+    agg_block = first_recv[:, :col_width]
+    cot_block = first_recv[:, col_width : 2 * col_width].astype(f32)
+    bias_full = parts_sum([first_recv[:, 2 * col_width + n] for n in range(3)])
 
     pre_act = lax.dot_general(
         weight, agg_block, (((0,), (0,)), ((), ())), preferred_element_type=f32
@@ -109,19 +127,35 @@
     )
     bias_terms = jnp.sum(grad_pre.astype(f32), axis=1)
 
-    second_send = jnp.concatenate(
+    grad_terms = jnp.concatenate(
         [
-            out_block.astype(f32).reshape(feat_count, channels, col_width),
-            grad_agg_block.astype(f32).reshape(feat_count, channels, col_width),
             weight_terms.reshape(feat_count, channels, width),
             bias_terms.reshape(feat_count, channels, 1),
         ],
         axis=2,
     )
+    second_send = jnp.concatenate(
+        [
+            out_block.reshape(feat_count, channels, col_width),
+            grad_agg_block.reshape(feat_count, channels, col_width),
+        ]
+        + bf16_parts(grad_terms, 2),
+        axis=2,
+    )
     second_recv = lax.all_to_all(second_send, "feat", split_axis=0, concat_axis=0, tiled=True)
-    layer_out = from_blocks(second_recv[:, :, :col_width]).astype(bf16)
-    grad_agg = from_blocks(second_recv[:, :, col_width : 2 * col_width]).astype(bf16)
-    panel_terms = jnp.sum(second_recv[:, :, 2 * col_width :], axis=0)
+    layer_out = from_blocks(second_recv[:, :, :col_width])
+    grad_agg = from_blocks(second_recv[:, :, col_width : 2 * col_width])
+    terms_width = width + 1
+    start = 2 * col_width
+    panel_terms = jnp.sum(
+        parts_sum(
+            [
+                second_recv[:, :, start : start + terms_width],
+                second_recv[:, :, start + terms_width :],
+            ]
+        ),
+        axis=0,
+    )
 
     grad_blocks = grad_agg.reshape(channels, row_blocks, block_size)
     spread_out = over_tiles(
@@ -129,20 +163,17 @@
     )
     spread_out = spread_out.reshape(channels, src_blocks * block_size)
     own_grad = spread_out[:, :row_count]
-    halo_terms = (
-        spread_out[:, row_count:]
-        .astype(bf16)
-        .astype(f32)
-        .reshape(channels, section_count, halo_width)
-    )
+    halo_part = spread_out[:, row_count:].reshape(channels, section_count, halo_width)
+    halo_terms = lax.reduce_precision(halo_part, exponent_bits=8, mantissa_bits=7)
     depth_terms = jnp.sum(states * own_grad[None], axis=2) + jnp.sum(
         halo_states * halo_terms[None], axis=(2, 3)
     )
     totals = jnp.concatenate([panel_terms.reshape(-1), depth_terms.reshape(-1)])
     last_send = jnp.concatenate(
-        [
-            halo_terms.transpose(1, 0, 2).reshape(section_count, channels * halo_width),
-            jnp.broadcast_to(totals[None, :], (vert_count, totals.shape[0])),
+        [halo_part.astype(bf16).transpose(1, 0, 2).reshape(section_count, channels * halo_width)]
+        + [
+            jnp.broadcast_to(part[None, :], (vert_count, totals.shape[0]))
+            for part in bf16_parts(totals, 2)
         ],
         axis=1,
     )
@@ -152,13 +183,16 @@
         .reshape(section_count, channels, halo_width)
         .transpose(1, 0, 2)
     )
-    totals = jnp.sum(last_recv[:, channels * halo_width :], axis=0)
+    tail = last_recv[:, channels * halo_width :]
+    totals = jnp.sum(
+        parts_sum([tail[:, : totals.shape[0]], tail[:, totals.shape[0] :]]), axis=0
+    )
     hot = (
         my_send.reshape(-1)[None, :] == jnp.arange(row_count, dtype=jnp.int32)[:, None]
     ).astype(bf16)
     added = lax.dot_general(
         hot,
-        returned.reshape(channels, -1).astype(bf16),
+        returned.reshape(channels, -1),
         (((1,), (1,)), ((), ())),
         preferred_element_type=f32,
     )

time: 134 us -> 128 us (0.955)
  waiting for transfers between devices: 39.8 us -> 34.7 us
  blocking collectives: 23.3 us -> 19.4 us
  local copies, waits for them, and re-layouts: 12.5 us -> 14.3 us
    all_to_all x1, blocking collectives: 23.3 us -> 19.4 us  [local(): lax.all_to_all(first_send, 'feat', split_axis=0, concat_axis=0, tiled=True)]
    all_to_all x1, waiting for transfers between devices: 17.5 us -> 13.8 us  [local(): lax.all_to_all(second_send, 'feat', split_axis=0, concat_axis=0, tiled=True)]
    unnamed x20, local copies, waits for them, and re-layouts: 1.23 us -> 3.32 us
where the time goes in v6:
time: 128 us; the launch traced here: 127 us
  waiting for transfers between devices  34.7 us (27%)
  starting transfers between devices  28.8 us (22%)
  blocking collectives  19.4 us (15%)
  matrix products  18.8 us (15%)
  local copies, waits for them, and re-layouts  14.3 us (11%)
  other arithmetic  9.38 us (7%)
  between operations  1.71 us (1%)
    all_to_all x1, blocking collectives, local(): lax.all_to_all(first_send, 'feat', split_axis=0, concat_axis=0, tiled=True)  19.4 us
    all_to_all x1, starting transfers between devices, local(): lax.all_to_all(listed.reshape(state_count, channels, section_count, halo_...  16.7 us
    all_to_all x1, waiting for transfers between devices, local(): lax.all_to_all(last_send, 'vert', split_axis=0, concat_axis=0, tiled=True)  14.6 us
    all_to_all x1, waiting for transfers between devices, local(): lax.all_to_all(second_send, 'feat', split_axis=0, concat_axis=0, tiled=True)  13.8 us
    dot_general x1, matrix products, tile_forward(): jnp.einsum('dtc,trc->dtr', picked, tile_grp, preferred_element_type=jnp.f...  7.83 us
    all_to_all x1, starting transfers between devices, local(): lax.all_to_all(last_send, 'vert', split_axis=0, concat_axis=0, tiled=True)  7.38 us
    all_to_all x1, waiting for transfers between devices, local(): lax.all_to_all(listed.reshape(state_count, channels, section_count, halo_...  6.31 us
    dot_general x1, matrix products, tile_backward(): jnp.einsum('dtr,trc->dtc', picked, tile_grp, preferred_element_type=jnp.f...  5.71 us
  transfers between devices with their start and end apart: 3, of which 3 were waited for; matrix products, arithmetic and copies ran while one was open for 3% of the time, Pallas kernels for 0%

profile of v6, /device:TPU:1, one launch (start us, length us, event | category | flops | bytes accessed | tf_op | source)
XLA Modules:
  0.0 127.0 jit_solution(17875169970820566269)
XLA Ops:
  0.7 0.8 compare_and_fusion
  1.4 0.8 reshape_squeeze.8
  2.2 1.4 %copy.85 = bf16[32,4096]{0,1:T(8,128)(2,1)S(1)} copy(bf16[32,4096]{1,0:T(8,128)(2,1)} %bitcast.97) | data formatting | bytes 524288 | tf_op jit(solution)/shard_map/reshape | solution.py:90
  3.7 3.2 %gather_fusion = bf16[1536,32]{1,0:T(8,128)(2,1)S(1)} fusion(bf16[32,4096]{0,1:T(8,128)(2,1)S(1)} %copy.85, s32[2048]{0:T(1024)S(1)} %pad_clamp_fusion), kind=kCustom, calls=%fused_computation | custom fusion | bytes 202752 | tf_op jit(solution)/shard_map/jit(_take)/gather | solution.py:90
  6.9 0.2 copy.86
  7.0 0.2 gather.15
  7.3 0.8 reshape.293
  8.1 16.7 %all-to-all-start = ((bf16[24,2,1024]{2,1,0:T(2,128)(2,1)}), bf16[24,2,1024]{2,1,0:T(2,128)(2,1)S(1)}, u32[]{:S(2)}, u32[]{:S(2)}) async-start(bf16[24,2,1024]{2,1,0:T(2,128)(2,1)} %reshape.293), calls=%async_computation | async-start | bytes 196608 | tf_op jit(solution)/shard_map/all_to_all | solution.py:91
  25.4 0.7 compare_select_fusion.3
  26.1 0.7 fusion.45
  26.9 0.8 copy.116
  27.7 1.1 fusion.17
  28.8 0.7 compare_and_fusion.2
  29.5 6.3 %all-to-all-done = bf16[24,2,1024]{2,1,0:T(2,128)(2,1)S(1)} async-done(((bf16[24,2,1024]{2,1,0:T(2,128)(2,1)}), bf16[24,2,1024]{2,1,0:T(2,128)(2,1)S(1)}, u32[]{:S(2)}, u32[]{:S(2)}) %all-to-all-start) | async-done | bytes 98336 | tf_op jit(solution)/shard_map/all_to_all | solution.py:91
  35.8 0.2 reshape.294
  36.0 0.8 fusion.25
  37.0 0.8 gather_fusion.1
  37.8 7.8 %fusion.7 = bf16[8,256,128]{2,0,1:T(8,128)(2,1)S(1)} fusion(bf16[1,256,128,128]{3,2,1,0:T(8,128)(2,1)} %param.12, bf16[256,8,128]{2,1,0:T(8,128)(2,1)S(1)} %gather_fusion.1, pred[256]{0:T(512)(128)(4,1)S(1)} %compare_and_fusion.2), kind=kOutput, calls=%fused_computation.11 | convolution fusion | flops 67371008 | bytes 9437440 | tf_op jit(solution)/shard_map/dtc,trc->dtr/dot_general | solution.py:11
  45.6 0.2 convolution_convert_fusion
  46.0 19.4 %all_to_all.27 = bf16[32,8,259]{2,1,0:T(8,128)(2,1)S(1)} all-to-all(bf16[32,8,259]{2,1,0:T(8,128)(2,1)S(1)} %copy.91), channel_id=1, replica_groups=mesh['vert'=24,'feat'=32] {'feat'}, dimensions={0} | all-to-all | bytes 265216 | tf_op jit(solution)/shard_map/all_to_all | solution.py:111
  65.4 0.2 add_reduce_fusion.2
  65.7 0.3 convert_reduce_fusion
  66.0 0.2 convolution_bitcast_fusion
  66.1 0.2 fusion.14
  66.5 0.1 copy.94
  66.6 0.2 reshape.289
  66.9 0.9 pad_maximum_fusion
  67.8 4.7 %all-to-all-start.2 = ((bf16[32,8,770]{2,1,0:T(8,128)(2,1)}), bf16[32,8,770]{2,1,0:T(8,128)(2,1)S(1)}, u32[]{:S(2)}, u32[]{:S(2)}) async-start(bf16[32,8,770]{2,1,0:T(8,128)(2,1)} %pad_maximum_fusion), calls=%async_computation.2 | async-start | bytes 917504 | tf_op jit(solution)/shard_map/all_to_all | solution.py:145
  72.5 13.8 %all-to-all-done.2 = bf16[32,8,770]{2,1,0:T(8,128)(2,1)S(1)} async-done(((bf16[32,8,770]{2,1,0:T(8,128)(2,1)}), bf16[32,8,770]{2,1,0:T(8,128)(2,1)S(1)}, u32[]{:S(2)}, u32[]{:S(2)}) %all-to-all-start.2) | async-done | bytes 394272 | tf_op jit(solution)/shard_map/all_to_all | solution.py:145
  86.3 0.6 slice_bitcast_fusion
  87.0 0.8 gather_fusion.2
  87.8 5.7 %fusion.10 = bf16[8,256,128]{2,0,1:T(8,128)(2,1)S(1)} fusion(bf16[1,256,128,128]{3,2,1,0:T(8,128)(2,1)} %param.12, bf16[256,8,128]{2,1,0:T(8,128)(2,1)S(1)} %gather_fusion.2, pred[256]{0:T(512)(128)(4,1)S(1)} %compare_and_fusion.1), kind=kOutput, calls=%fused_computation.12 | convolution fusion | flops 67371008 | bytes 9437440 | tf_op jit(solution)/shard_map/dtr,trc->dtc/dot_general | solution.py:20
  93.5 0.2 convolution_bitcast_fusion.1
  93.8 0.1 add_reduce_fusion
  94.4 0.1 fusion.26
  94.5 0.2 fusion.18
  94.9 0.1 concatenate.36
  95.0 0.5 broadcast.143
  95.5 0.7 reduce.6
  96.2 1.0 reshape.295
  97.2 7.4 %all-to-all-start.3 = ((bf16[24,2,2344]{2,1,0:T(2,128)(2,1)}), bf16[24,2,2344]{2,1,0:T(2,128)(2,1)S(1)}, u32[]{:S(2)}, u32[]{:S(2)}) async-start(bf16[24,2,2344]{2,1,0:T(2,128)(2,1)} %reshape.295), calls=%async_computation.3 | async-start | bytes 466944 | tf_op jit(solution)/shard_map/all_to_all | solution.py:180
  104.7 14.6 %all-to-all-done.3 = bf16[24,2,2344]{2,1,0:T(2,128)(2,1)S(1)} async-done(((bf16[24,2,2344]{2,1,0:T(2,128)(2,1)}), bf16[24,2,2344]{2,1,0:T(2,128)(2,1)S(1)}, u32[]{:S(2)}, u32[]{:S(2)}) %all-to-all-start.3) | async-done | bytes 225056 | tf_op jit(solution)/shard_map/all_to_all | solution.py:180
  119.3 0.3 reshape.296
  119.9 0.6 fusion.44
  120.5 0.6 slice_multiply_fusion
  121.1 0.7 mul.96
  122.0 4.2 %fusion.6 = f32[8,4096]{1,0:T(8,128)S(1)} fusion(bf16[8,1536]{1,0:T(8,128)(2,1)S(1)} %reshape.261, s32[1536]{0:T(1024)S(1)} %reshape_squeeze.9, f32[8,5632]{1,0:T(8,128)S(1)} %bitcast.108), kind=kOutput, calls=%fused_computation.10 | convolution fusion | flops 106987520 | bytes 292864 | tf_op jit(solution)/shard_map/dot_general | solution.py:193
  126.2 0.8 multiply_convert_fusion
  (57 shorter events, 2.0 us)
Async XLA Ops:
  0.6 65.1 %copy-start = (bf16[256,256]{1,0:T(8,128)(2,1)S(1)}, bf16[256,256]{1,0:T(8,128)(2,1)}, u32[]{:S(2)}) copy-start(bf16[256,256]{1,0:T(8,128)(2,1)} %param.17) | copy-start | bytes 393220
  0.6 45.0 %copy-start.4 = (s32[1,256]{1,0:T(1,128)S(1)}, s32[1,256]{1,0:T(1,128)}, u32[]{:S(2)}) copy-start(s32[1,256]{1,0:T(1,128)} %param.13) | copy-start | bytes 3076
  8.1 27.8 %all-to-all-start = ((bf16[24,2,1024]{2,1,0:T(2,128)(2,1)}), bf16[24,2,1024]{2,1,0:T(2,128)(2,1)S(1)}, u32[]{:S(2)}, u32[]{:S(2)}) async-start(bf16[24,2,1024]{2,1,0:T(2,128)(2,1)} %reshape.293), calls=%async_computation | async-start | bytes 196608 | tf_op jit(solution)/shard_map/all_to_all | solution.py:91
  45.9 47.6 %copy-start.5 = (s32[1,256]{1,0:T(1,128)S(1)}, s32[1,256]{1,0:T(1,128)}, u32[]{:S(2)}) copy-start(s32[1,256]{1,0:T(1,128)} %param.14) | copy-start | bytes 3076
  66.3 28.2 %copy-start.1 = (bf16[4,8,4096]{2,1,0:T(8,128)(2,1)S(1)}, bf16[4,8,4096]{2,1,0:T(8,128)(2,1)}, u32[]{:S(2)}) copy-start(bf16[4,8,4096]{2,1,0:T(8,128)(2,1)} %param.10) | copy-start | bytes 786436
  67.8 36.8 %copy-start.2 = (s32[1,24,64]{2,1,0:T(8,128)S(1)}, s32[1,24,64]{2,1,0:T(8,128)}, u32[]{:S(2)}) copy-start(s32[1,24,64]{2,1,0:T(8,128)} %param.16) | copy-start | bytes 18436
  67.8 18.6 %all-to-all-start.2 = ((bf16[32,8,770]{2,1,0:T(8,128)(2,1)}), bf16[32,8,770]{2,1,0:T(8,128)(2,1)S(1)}, u32[]{:S(2)}, u32[]{:S(2)}) async-start(bf16[32,8,770]{2,1,0:T(8,128)(2,1)} %pad_maximum_fusion), calls=%async_computation.2 | async-start | bytes 917504 | tf_op jit(solution)/shard_map/all_to_all | solution.py:145
  93.5 32.7 %copy-start.3 = (f32[4,8]{1,0:T(4,128)S(1)}, f32[4,8]{1,0:T(4,128)}, u32[]{:S(2)}) copy-start(f32[4,8]{1,0:T(4,128)} %param.11) | copy-start | bytes 388
  97.2 22.1 %all-to-all-start.3 = ((bf16[24,2,2344]{2,1,0:T(2,128)(2,1)}), bf16[24,2,2344]{2,1,0:T(2,128)(2,1)S(1)}, u32[]{:S(2)}, u32[]{:S(2)}) async-start(bf16[24,2,2344]{2,1,0:T(2,128)(2,1)} %reshape.295), calls=%async_computation.3 | async-start | bytes 466944 | tf_op jit(solution)/shard_map/all_to_all | solution.py:180

commit v7 on v6

--- a/solution.py
+++ b/solution.py
@@ -7,7 +7,7 @@
 
 
 def tile_forward(extended, tile_grp, dst_grp, src_grp, live_mask, row_blocks):
-    picked = jnp.take(extended, src_grp, axis=1)
+    picked = extended.at[:, src_grp].get(mode="promise_in_bounds")
     products = jnp.einsum("dtc,trc->dtr", picked, tile_grp, preferred_element_type=jnp.float32)
     onehot = (
         (dst_grp[:, None] == jnp.arange(row_blocks, dtype=jnp.int32)[None, :]) & live_mask[:, None]
@@ -16,7 +16,7 @@
 
 
 def tile_backward(grad_blocks, tile_grp, dst_grp, src_grp, live_mask, src_blocks):
-    picked = jnp.take(grad_blocks, dst_grp, axis=1)
+    picked = grad_blocks.at[:, dst_grp].get(mode="promise_in_bounds")
     products = jnp.einsum("dtr,trc->dtc", picked, tile_grp, preferred_element_type=jnp.float32)
     onehot = (
         (src_grp[:, None] == jnp.arange(src_blocks, dtype=jnp.int32)[None, :]) & live_mask[:, None]
@@ -87,7 +87,11 @@
         return x.transpose(1, 0, 2).reshape(channels, row_count)
 
     state_count = states.shape[0]
-    listed = jnp.take(states.reshape(state_count * channels, row_count), my_send.reshape(-1), axis=1)
+    listed = (
+        states.reshape(state_count * channels, row_count)
+        .at[:, my_send.reshape(-1)]
+        .get(mode="promise_in_bounds")
+    )
     halo_states = lax.all_to_all(
         listed.reshape(state_count, channels, section_count, halo_width),
         "vert",
@@ -168,7 +172,7 @@
     depth_terms = jnp.sum(states * own_grad[None], axis=2) + jnp.sum(
         halo_states * halo_terms[None], axis=(2, 3)
     )
-    totals = jnp.concatenate([panel_terms.reshape(-1), depth_terms.reshape(-1)])
+    totals = jnp.concatenate([panel_terms.reshape(-1), depth_terms.reshape(-1)]) * norm_scale
     last_send = jnp.concatenate(
         [halo_part.astype(bf16).transpose(1, 0, 2).reshape(section_count, channels * halo_width)]
         + [
@@ -203,9 +207,9 @@
     return (
         layer_out,
         grad_states,
-        panel_sum[:, :width] * norm_scale,
-        panel_sum[:, width] * norm_scale,
-        depth_sum * norm_scale,
+        panel_sum[:, :width],
+        panel_sum[:, width],
+        depth_sum,
     )
 
 

time: 128 us -> 127 us (level)
  other arithmetic: 9.38 us -> 6.61 us
  local copies, waits for them, and re-layouts: 14.3 us -> 15.6 us
    and x3 -> x0, other arithmetic: 1.45 us -> none  [the longest x1 0.76 us: local(): jnp.take(states.reshape(state_count * channels, row_count), my_send.resha...]
    mul x3 -> x0, other arithmetic: 1.3 us -> none  [the longest x1 0.63 us: local(): panel_sum[:, width] * norm_scale]
    slice x0 -> x3, local copies, waits for them, and re-layouts: none -> 1.3 us  [the longest x1 0.63 us: local(): panel_sum[:, width]]
    gather x5 -> x4, local copies, waits for them, and re-layouts: 5.16 us -> 4.99 us  [the longest x2 3.36 us: local(): listed = states.reshape(state_count * channels, row_count).at[:, my_send....]
where the time goes in v7:
time: 127 us; the launch traced here: 126 us
  waiting for transfers between devices  35.4 us (28%)
  starting transfers between devices  28.8 us (23%)
  blocking collectives  19.4 us (15%)
  matrix products  18.7 us (15%)
  local copies, waits for them, and re-layouts  15.6 us (12%)
  other arithmetic  6.61 us (5%)
  between operations  1.7 us (1%)
    all_to_all x1, blocking collectives, local(): lax.all_to_all(first_send, 'feat', split_axis=0, concat_axis=0, tiled=True)  19.4 us
    all_to_all x1, starting transfers between devices, local(): lax.all_to_all(listed.reshape(state_count, channels, section_count, halo_...  16.7 us
    all_to_all x1, waiting for transfers between devices, local(): lax.all_to_all(last_send, 'vert', split_axis=0, concat_axis=0, tiled=True)  14.6 us
    all_to_all x1, waiting for transfers between devices, local(): lax.all_to_all(second_send, 'feat', split_axis=0, concat_axis=0, tiled=True)  13.8 us
    dot_general x1, matrix products, tile_forward(): jnp.einsum('dtc,trc->dtr', picked, tile_grp, preferred_element_type=jnp.f...  7.8 us
    all_to_all x1, starting transfers between devices, local(): lax.all_to_all(last_send, 'vert', split_axis=0, concat_axis=0, tiled=True)  7.37 us
    all_to_all x1, waiting for transfers between devices, local(): lax.all_to_all(listed.reshape(state_count, channels, section_count, halo_...  6.99 us
    dot_general x1, matrix products, tile_backward(): jnp.einsum('dtr,trc->dtc', picked, tile_grp, preferred_element_type=jnp.f...  5.65 us
  transfers between devices with their start and end apart: 3, of which 3 were waited for; matrix products, arithmetic and copies ran while one was open for 3% of the time, Pallas kernels for 0%

profile of v7, /device:TPU:1, one launch (start us, length us, event | category | flops | bytes accessed | tf_op | source)
XLA Modules:
  0.0 126.2 jit_solution(8281938841250997180)
XLA Ops:
  0.7 0.8 reshape_squeeze.3
  1.5 1.4 %copy.85 = bf16[32,4096]{0,1:T(8,128)(2,1)S(1)} copy(bf16[32,4096]{1,0:T(8,128)(2,1)} %bitcast.93) | data formatting | bytes 524288 | tf_op jit(solution)/shard_map/reshape | solution.py:91
  3.0 3.2 %gather_fusion = bf16[1536,32]{1,0:T(8,128)(2,1)S(1)} fusion(bf16[32,4096]{0,1:T(8,128)(2,1)S(1)} %copy.85, s32[2048]{0:T(1024)S(1)} %pad_clamp_fusion), kind=kCustom, calls=%fused_computation | custom fusion | bytes 202752 | tf_op jit(solution)/shard_map/gather | solution.py:93
  6.2 0.2 copy.86
  6.3 0.2 reshape.215
  6.5 0.8 reshape.260
  7.3 16.7 %all-to-all-start = ((bf16[24,2,1024]{2,1,0:T(2,128)(2,1)}), bf16[24,2,1024]{2,1,0:T(2,128)(2,1)S(1)}, u32[]{:S(2)}, u32[]{:S(2)}) async-start(bf16[24,2,1024]{2,1,0:T(2,128)(2,1)} %reshape.260), calls=%async_computation | async-start | bytes 196608 | tf_op jit(solution)/shard_map/all_to_all | solution.py:95
  24.7 0.7 compare_select_fusion.2
  25.4 0.7 fusion.38
  26.2 0.8 copy.116
  27.0 1.1 fusion.17
  28.1 7.0 %all-to-all-done = bf16[24,2,1024]{2,1,0:T(2,128)(2,1)S(1)} async-done(((bf16[24,2,1024]{2,1,0:T(2,128)(2,1)}), bf16[24,2,1024]{2,1,0:T(2,128)(2,1)S(1)}, u32[]{:S(2)}, u32[]{:S(2)}) %all-to-all-start) | async-done | bytes 98336 | tf_op jit(solution)/shard_map/all_to_all | solution.py:95
  35.1 0.2 reshape.261
  35.3 0.8 fusion.21
  36.2 0.8 gather_fusion.1
  37.0 7.8 %fusion.7 = bf16[8,256,128]{2,0,1:T(8,128)(2,1)S(1)} fusion(bf16[1,256,128,128]{3,2,1,0:T(8,128)(2,1)} %param.12, bf16[256,8,128]{2,1,0:T(8,128)(2,1)S(1)} %gather_fusion.1), kind=kOutput, calls=%fused_computation.11 | convolution fusion | flops 67108864 | bytes 9437184 | tf_op jit(solution)/shard_map/dtc,trc->dtr/dot_general | solution.py:11
  44.8 0.2 convolution_convert_fusion
  45.2 19.4 %all_to_all.27 = bf16[32,8,259]{2,1,0:T(8,128)(2,1)S(1)} all-to-all(bf16[32,8,259]{2,1,0:T(8,128)(2,1)S(1)} %copy.91), channel_id=1, replica_groups=mesh['vert'=24,'feat'=32] {'feat'}, dimensions={0} | all-to-all | bytes 265216 | tf_op jit(solution)/shard_map/all_to_all | solution.py:115
  64.6 0.2 add_reduce_fusion.2
  64.9 0.3 convert_reduce_fusion
  65.2 0.2 convolution_bitcast_fusion
  65.4 0.2 fusion.14
  65.6 0.1 copy.92
  65.7 0.1 copy.94
  65.8 0.2 reshape.256
  66.1 0.9 pad_maximum_fusion
  67.0 4.7 %all-to-all-start.2 = ((bf16[32,8,770]{2,1,0:T(8,128)(2,1)}), bf16[32,8,770]{2,1,0:T(8,128)(2,1)S(1)}, u32[]{:S(2)}, u32[]{:S(2)}) async-start(bf16[32,8,770]{2,1,0:T(8,128)(2,1)} %pad_maximum_fusion), calls=%async_computation.2 | async-start | bytes 917504 | tf_op jit(solution)/shard_map/all_to_all | solution.py:149
  71.7 13.8 %all-to-all-done.2 = bf16[32,8,770]{2,1,0:T(8,128)(2,1)S(1)} async-done(((bf16[32,8,770]{2,1,0:T(8,128)(2,1)}), bf16[32,8,770]{2,1,0:T(8,128)(2,1)S(1)}, u32[]{:S(2)}, u32[]{:S(2)}) %all-to-all-start.2) | async-done | bytes 394272 | tf_op jit(solution)/shard_map/all_to_all | solution.py:149
  85.5 0.6 slice_bitcast_fusion
  86.2 0.8 gather_fusion.2
  87.0 5.7 %fusion.10 = bf16[8,256,128]{2,0,1:T(8,128)(2,1)S(1)} fusion(bf16[1,256,128,128]{3,2,1,0:T(8,128)(2,1)} %param.12, bf16[256,8,128]{2,1,0:T(8,128)(2,1)S(1)} %gather_fusion.2), kind=kOutput, calls=%fused_computation.12 | convolution fusion | flops 67108864 | bytes 9437184 | tf_op jit(solution)/shard_map/dtr,trc->dtc/dot_general | solution.py:20
  92.7 0.2 convolution_bitcast_fusion.1
  93.0 0.1 add_reduce_fusion
  93.5 0.1 fusion.22
  93.7 0.2 fusion.18
  94.0 0.1 concatenate.33
  94.2 0.5 broadcast.87
  94.7 0.7 reduce.6
  95.4 1.0 reshape.262
  96.4 7.4 %all-to-all-start.3 = ((bf16[24,2,2344]{2,1,0:T(2,128)(2,1)}), bf16[24,2,2344]{2,1,0:T(2,128)(2,1)S(1)}, u32[]{:S(2)}, u32[]{:S(2)}) async-start(bf16[24,2,2344]{2,1,0:T(2,128)(2,1)} %reshape.262), calls=%async_computation.3 | async-start | bytes 466944 | tf_op jit(solution)/shard_map/all_to_all | solution.py:184
  103.8 14.6 %all-to-all-done.3 = bf16[24,2,2344]{2,1,0:T(2,128)(2,1)S(1)} async-done(((bf16[24,2,2344]{2,1,0:T(2,128)(2,1)}), bf16[24,2,2344]{2,1,0:T(2,128)(2,1)S(1)}, u32[]{:S(2)}, u32[]{:S(2)}) %all-to-all-start.3) | async-done | bytes 225056 | tf_op jit(solution)/shard_map/all_to_all | solution.py:184
  118.4 0.3 reshape.263
  118.8 0.1 add_reduce_fusion.1
  119.1 0.6 slice_reduce_fusion
  119.7 0.6 slice.104
  120.3 0.7 reshape.229
  121.2 4.2 %fusion.6 = f32[8,4096]{1,0:T(8,128)S(1)} fusion(bf16[8,1536]{1,0:T(8,128)(2,1)S(1)} %reshape.227, s32[1536]{0:T(1024)S(1)} %eq.53, f32[8,5632]{1,0:T(8,128)S(1)} %bitcast.104), kind=kOutput, calls=%fused_computation.10 | convolution fusion | flops 106987520 | bytes 292864 | tf_op jit(solution)/shard_map/dot_general | solution.py:197
  125.4 0.8 multiply_convert_fusion
  (53 shorter events, 1.8 us)
Async XLA Ops:
  0.6 64.3 %copy-start = (bf16[256,256]{1,0:T(8,128)(2,1)S(1)}, bf16[256,256]{1,0:T(8,128)(2,1)}, u32[]{:S(2)}) copy-start(bf16[256,256]{1,0:T(8,128)(2,1)} %param.17) | copy-start | bytes 393220
  0.6 44.2 %copy-start.4 = (s32[1,256]{1,0:T(1,128)S(1)}, s32[1,256]{1,0:T(1,128)}, u32[]{:S(2)}) copy-start(s32[1,256]{1,0:T(1,128)} %param.13) | copy-start | bytes 3076
  7.3 27.8 %all-to-all-start = ((bf16[24,2,1024]{2,1,0:T(2,128)(2,1)}), bf16[24,2,1024]{2,1,0:T(2,128)(2,1)S(1)}, u32[]{:S(2)}, u32[]{:S(2)}) async-start(bf16[24,2,1024]{2,1,0:T(2,128)(2,1)} %reshape.260), calls=%async_computation | async-start | bytes 196608 | tf_op jit(solution)/shard_map/all_to_all | solution.py:95
  45.1 47.5 %copy-start.5 = (s32[1,256]{1,0:T(1,128)S(1)}, s32[1,256]{1,0:T(1,128)}, u32[]{:S(2)}) copy-start(s32[1,256]{1,0:T(1,128)} %param.14) | copy-start | bytes 3076
  65.6 28.1 %copy-start.1 = (bf16[4,8,4096]{2,1,0:T(8,128)(2,1)S(1)}, bf16[4,8,4096]{2,1,0:T(8,128)(2,1)}, u32[]{:S(2)}) copy-start(bf16[4,8,4096]{2,1,0:T(8,128)(2,1)} %param.10) | copy-start | bytes 786436
  67.0 36.8 %copy-start.2 = (s32[1,24,64]{2,1,0:T(8,128)S(1)}, s32[1,24,64]{2,1,0:T(8,128)}, u32[]{:S(2)}) copy-start(s32[1,24,64]{2,1,0:T(8,128)} %param.16) | copy-start | bytes 18436
  67.0 18.6 %all-to-all-start.2 = ((bf16[32,8,770]{2,1,0:T(8,128)(2,1)}), bf16[32,8,770]{2,1,0:T(8,128)(2,1)S(1)}, u32[]{:S(2)}, u32[]{:S(2)}) async-start(bf16[32,8,770]{2,1,0:T(8,128)(2,1)} %pad_maximum_fusion), calls=%async_computation.2 | async-start | bytes 917504 | tf_op jit(solution)/shard_map/all_to_all | solution.py:149
  92.7 32.7 %copy-start.3 = (f32[4,8]{1,0:T(4,128)S(1)}, f32[4,8]{1,0:T(4,128)}, u32[]{:S(2)}) copy-start(f32[4,8]{1,0:T(4,128)} %param.11) | copy-start | bytes 388
  96.4 22.1 %all-to-all-start.3 = ((bf16[24,2,2344]{2,1,0:T(2,128)(2,1)}), bf16[24,2,2344]{2,1,0:T(2,128)(2,1)S(1)}, u32[]{:S(2)}, u32[]{:S(2)}) async-start(bf16[24,2,2344]{2,1,0:T(2,128)(2,1)} %reshape.262), calls=%async_computation.3 | async-start | bytes 466944 | tf_op jit(solution)/shard_map/all_to_all | solution.py:184

commit v8 on v7

--- a/solution.py
+++ b/solution.py
@@ -143,7 +143,7 @@
             out_block.reshape(feat_count, channels, col_width),
             grad_agg_block.reshape(feat_count, channels, col_width),
         ]
-        + bf16_parts(grad_terms, 2),
+        + bf16_parts(grad_terms, 1),
         axis=2,
     )
     second_recv = lax.all_to_all(second_send, "feat", split_axis=0, concat_axis=0, tiled=True)
@@ -151,15 +151,7 @@
     grad_agg = from_blocks(second_recv[:, :, col_width : 2 * col_width])
     terms_width = width + 1
     start = 2 * col_width
-    panel_terms = jnp.sum(
-        parts_sum(
-            [
-                second_recv[:, :, start : start + terms_width],
-                second_recv[:, :, start + terms_width :],
-            ]
-        ),
-        axis=0,
-    )
+    panel_terms = jnp.sum(second_recv[:, :, start : start + terms_width].astype(f32), axis=0)
 
     grad_blocks = grad_agg.reshape(channels, row_blocks, block_size)
     spread_out = over_tiles(
@@ -177,7 +169,7 @@
         [halo_part.astype(bf16).transpose(1, 0, 2).reshape(section_count, channels * halo_width)]
         + [
             jnp.broadcast_to(part[None, :], (vert_count, totals.shape[0]))
-            for part in bf16_parts(totals, 2)
+            for part in bf16_parts(totals, 1)
         ],
         axis=1,
     )
@@ -188,9 +180,7 @@
         .transpose(1, 0, 2)
     )
     tail = last_recv[:, channels * halo_width :]
-    totals = jnp.sum(
-        parts_sum([tail[:, : totals.shape[0]], tail[:, totals.shape[0] :]]), axis=0
-    )
+    totals = jnp.sum(tail.astype(f32), axis=0)
     hot = (
         my_send.reshape(-1)[None, :] == jnp.arange(row_count, dtype=jnp.int32)[:, None]
     ).astype(bf16)

time: 127 us -> 121 us (0.953)
  waiting for transfers between devices: 35.4 us -> 29.6 us
    all_to_all x1, waiting for transfers between devices: 13.8 us -> 10.7 us  [local(): lax.all_to_all(second_send, 'feat', split_axis=0, concat_axis=0, tiled=True)]
    all_to_all x1, waiting for transfers between devices: 14.6 us -> 11.9 us  [local(): lax.all_to_all(last_send, 'vert', split_axis=0, concat_axis=0, tiled=True)]
where the time goes in v8:
time: 121 us; the launch traced here: 120 us
  waiting for transfers between devices  29.6 us (24%)
  starting transfers between devices  29.3 us (24%)
  blocking collectives  19.5 us (16%)
  matrix products  18.7 us (15%)
  local copies, waits for them, and re-layouts  15.3 us (13%)
  other arithmetic  6.26 us (5%)
  between operations  1.7 us (1%)
    all_to_all x1, blocking collectives, local(): lax.all_to_all(first_send, 'feat', split_axis=0, concat_axis=0, tiled=True)  19.5 us
    all_to_all x1, starting transfers between devices, local(): lax.all_to_all(listed.reshape(state_count, channels, section_count, halo_...  16.7 us
    all_to_all x1, waiting for transfers between devices, local(): lax.all_to_all(last_send, 'vert', split_axis=0, concat_axis=0, tiled=True)  11.9 us
    all_to_all x1, waiting for transfers between devices, local(): lax.all_to_all(second_send, 'feat', split_axis=0, concat_axis=0, tiled=True)  10.7 us
    all_to_all x1, starting transfers between devices, local(): lax.all_to_all(last_send, 'vert', split_axis=0, concat_axis=0, tiled=True)  8.04 us
    dot_general x1, matrix products, tile_forward(): jnp.einsum('dtc,trc->dtr', picked, tile_grp, preferred_element_type=jnp.f...  7.8 us
    all_to_all x1, waiting for transfers between devices, local(): lax.all_to_all(listed.reshape(state_count, channels, section_count, halo_...  6.98 us
    dot_general x1, matrix products, tile_backward(): jnp.einsum('dtr,trc->dtc', picked, tile_grp, preferred_element_type=jnp.f...  5.66 us
  transfers between devices with their start and end apart: 3, of which 3 were waited for; matrix products, arithmetic and copies ran while one was open for 3% of the time, Pallas kernels for 0%

profile of v8, /device:TPU:1, one launch (start us, length us, event | category | flops | bytes accessed | tf_op | source)
XLA Modules:
  0.0 120.4 jit_solution(12875889312692823429)
XLA Ops:
  0.7 1.5 %copy.85 = bf16[32,4096]{0,1:T(8,128)(2,1)S(1)} copy(bf16[32,4096]{1,0:T(8,128)(2,1)} %bitcast.94) | data formatting | bytes 524288 | tf_op jit(solution)/shard_map/reshape | solution.py:91
  2.1 0.8 reshape_squeeze.3
  3.0 3.2 %gather_fusion = bf16[1536,32]{1,0:T(8,128)(2,1)S(1)} fusion(bf16[32,4096]{0,1:T(8,128)(2,1)S(1)} %copy.85, s32[2048]{0:T(1024)S(1)} %pad_clamp_fusion), kind=kCustom, calls=%fused_computation | custom fusion | bytes 202752 | tf_op jit(solution)/shard_map/gather | solution.py:93
  6.2 0.2 copy.86
  6.3 0.2 reshape.204
  6.5 0.8 reshape.250
  7.3 16.7 %all-to-all-start = ((bf16[24,2,1024]{2,1,0:T(2,128)(2,1)}), bf16[24,2,1024]{2,1,0:T(2,128)(2,1)S(1)}, u32[]{:S(2)}, u32[]{:S(2)}) async-start(bf16[24,2,1024]{2,1,0:T(2,128)(2,1)} %reshape.250), calls=%async_computation | async-start | bytes 196608 | tf_op jit(solution)/shard_map/all_to_all | solution.py:95
  24.0 0.7 fusion.38
  24.7 0.7 compare_select_fusion.2
  26.2 0.8 copy.116
  27.0 1.1 fusion.18
  28.1 7.0 %all-to-all-done = bf16[24,2,1024]{2,1,0:T(2,128)(2,1)S(1)} async-done(((bf16[24,2,1024]{2,1,0:T(2,128)(2,1)}), bf16[24,2,1024]{2,1,0:T(2,128)(2,1)S(1)}, u32[]{:S(2)}, u32[]{:S(2)}) %all-to-all-start) | async-done | bytes 98336 | tf_op jit(solution)/shard_map/all_to_all | solution.py:95
  35.1 0.2 reshape.251
  35.3 0.8 fusion.22
  36.1 0.1 convert_element_type.92
  36.2 0.8 gather_fusion.1
  37.0 7.8 %fusion.7 = bf16[8,256,128]{2,0,1:T(8,128)(2,1)S(1)} fusion(bf16[1,256,128,128]{3,2,1,0:T(8,128)(2,1)} %param.12, bf16[256,8,128]{2,1,0:T(8,128)(2,1)S(1)} %gather_fusion.1), kind=kOutput, calls=%fused_computation.11 | convolution fusion | flops 67108864 | bytes 9437184 | tf_op jit(solution)/shard_map/dtc,trc->dtr/dot_general | solution.py:11
  44.8 0.2 convolution_convert_fusion.1
  45.2 19.5 %all_to_all.27 = bf16[32,8,259]{2,1,0:T(8,128)(2,1)S(1)} all-to-all(bf16[32,8,259]{2,1,0:T(8,128)(2,1)S(1)} %copy.91), channel_id=1, replica_groups=mesh['vert'=24,'feat'=32] {'feat'}, dimensions={0} | all-to-all | bytes 265216 | tf_op jit(solution)/shard_map/all_to_all | solution.py:115
  64.7 0.2 add_reduce_fusion
  64.9 0.1 copy.102
  65.0 0.3 fusion.42
  65.3 0.2 fusion.13
  65.5 0.2 fusion.15
  65.7 0.2 reshape.245
  65.9 0.1 copy.94
  66.1 0.1 copy.92
  66.2 0.7 pad_maximum_fusion
  67.0 4.6 %all-to-all-start.2 = ((bf16[32,8,513]{2,1,0:T(8,128)(2,1)}), bf16[32,8,513]{2,1,0:T(8,128)(2,1)S(1)}, u32[]{:S(2)}, u32[]{:S(2)}) async-start(bf16[32,8,513]{2,1,0:T(8,128)(2,1)} %pad_maximum_fusion), calls=%async_computation.2 | async-start | bytes 655360 | tf_op jit(solution)/shard_map/all_to_all | solution.py:149
  71.6 10.7 %all-to-all-done.2 = bf16[32,8,513]{2,1,0:T(8,128)(2,1)S(1)} async-done(((bf16[32,8,513]{2,1,0:T(8,128)(2,1)}), bf16[32,8,513]{2,1,0:T(8,128)(2,1)S(1)}, u32[]{:S(2)}, u32[]{:S(2)}) %all-to-all-start.2) | async-done | bytes 262688 | tf_op jit(solution)/shard_map/all_to_all | solution.py:149
  82.3 0.6 slice_bitcast_fusion
  83.0 0.8 gather_fusion.2
  83.8 5.7 %fusion.10 = bf16[8,256,128]{2,0,1:T(8,128)(2,1)S(1)} fusion(bf16[1,256,128,128]{3,2,1,0:T(8,128)(2,1)} %param.12, bf16[256,8,128]{2,1,0:T(8,128)(2,1)S(1)} %gather_fusion.2), kind=kOutput, calls=%fused_computation.12 | convolution fusion | flops 67108864 | bytes 9437184 | tf_op jit(solution)/shard_map/dtr,trc->dtc/dot_general | solution.py:20
  89.5 0.2 convolution_bitcast_fusion
  89.9 0.1 reshape.214
  90.0 0.2 fusion.19
  90.3 0.1 fusion.23
  90.8 0.5 broadcast.86
  91.3 0.7 reduce.8
  92.0 0.8 reshape.252
  92.8 8.0 %all-to-all-start.3 = ((bf16[24,2,1300]{2,1,0:T(2,128)(2,1)}), bf16[24,2,1300]{2,1,0:T(2,128)(2,1)S(1)}, u32[]{:S(2)}, u32[]{:S(2)}) async-start(bf16[24,2,1300]{2,1,0:T(2,128)(2,1)} %reshape.252), calls=%async_computation.3 | async-start | bytes 270336 | tf_op jit(solution)/shard_map/all_to_all | solution.py:176
  100.9 11.9 %all-to-all-done.3 = bf16[24,2,1300]{2,1,0:T(2,128)(2,1)S(1)} async-done(((bf16[24,2,1300]{2,1,0:T(2,128)(2,1)}), bf16[24,2,1300]{2,1,0:T(2,128)(2,1)S(1)}, u32[]{:S(2)}, u32[]{:S(2)}) %all-to-all-start.3) | async-done | bytes 124832 | tf_op jit(solution)/shard_map/all_to_all | solution.py:176
  112.8 0.2 reshape.253
  113.2 0.6 slice.91
  113.8 0.6 slice_reduce_fusion
  114.7 4.2 %fusion.6 = f32[8,4096]{1,0:T(8,128)S(1)} fusion(bf16[8,1536]{1,0:T(8,128)(2,1)S(1)} %reshape.216, s32[1536]{0:T(1024)S(1)} %eq.53, f32[8,5632]{1,0:T(8,128)S(1)} %bitcast.102), kind=kOutput, calls=%fused_computation.10 | convolution fusion | flops 106987520 | bytes 292864 | tf_op jit(solution)/shard_map/dot_general | solution.py:187
  118.9 0.8 multiply_convert_fusion
  119.7 0.7 reshape.218
  (52 shorter events, 1.5 us)
Async XLA Ops:
  0.6 64.4 %copy-start = (bf16[256,256]{1,0:T(8,128)(2,1)S(1)}, bf16[256,256]{1,0:T(8,128)(2,1)}, u32[]{:S(2)}) copy-start(bf16[256,256]{1,0:T(8,128)(2,1)} %param.17) | copy-start | bytes 393220
  0.6 44.2 %copy-start.4 = (s32[1,256]{1,0:T(1,128)S(1)}, s32[1,256]{1,0:T(1,128)}, u32[]{:S(2)}) copy-start(s32[1,256]{1,0:T(1,128)} %param.13) | copy-start | bytes 3076
  7.3 27.8 %all-to-all-start = ((bf16[24,2,1024]{2,1,0:T(2,128)(2,1)}), bf16[24,2,1024]{2,1,0:T(2,128)(2,1)S(1)}, u32[]{:S(2)}, u32[]{:S(2)}) async-start(bf16[24,2,1024]{2,1,0:T(2,128)(2,1)} %reshape.250), calls=%async_computation | async-start | bytes 196608 | tf_op jit(solution)/shard_map/all_to_all | solution.py:95
  44.8 44.6 %copy-start.5 = (s32[1,256]{1,0:T(1,128)S(1)}, s32[1,256]{1,0:T(1,128)}, u32[]{:S(2)}) copy-start(s32[1,256]{1,0:T(1,128)} %param.14) | copy-start | bytes 3076
  45.2 44.8 %copy-start.1 = (bf16[4,8,4096]{2,1,0:T(8,128)(2,1)S(1)}, bf16[4,8,4096]{2,1,0:T(8,128)(2,1)}, u32[]{:S(2)}) copy-start(bf16[4,8,4096]{2,1,0:T(8,128)(2,1)} %param.10) | copy-start | bytes 786436
  65.5 35.4 %copy-start.2 = (s32[1,24,64]{2,1,0:T(8,128)S(1)}, s32[1,24,64]{2,1,0:T(8,128)}, u32[]{:S(2)}) copy-start(s32[1,24,64]{2,1,0:T(8,128)} %param.16) | copy-start | bytes 18436
  67.0 15.4 %all-to-all-start.2 = ((bf16[32,8,513]{2,1,0:T(8,128)(2,1)}), bf16[32,8,513]{2,1,0:T(8,128)(2,1)S(1)}, u32[]{:S(2)}, u32[]{:S(2)}) async-start(bf16[32,8,513]{2,1,0:T(8,128)(2,1)} %pad_maximum_fusion), calls=%async_computation.2 | async-start | bytes 655360 | tf_op jit(solution)/shard_map/all_to_all | solution.py:149
  83.8 35.1 %copy-start.3 = (f32[4,8]{1,0:T(4,128)S(1)}, f32[4,8]{1,0:T(4,128)}, u32[]{:S(2)}) copy-start(f32[4,8]{1,0:T(4,128)} %param.11) | copy-start | bytes 388
  92.8 20.0 %all-to-all-start.3 = ((bf16[24,2,1300]{2,1,0:T(2,128)(2,1)}), bf16[24,2,1300]{2,1,0:T(2,128)(2,1)S(1)}, u32[]{:S(2)}, u32[]{:S(2)}) async-start(bf16[24,2,1300]{2,1,0:T(2,128)(2,1)} %reshape.252), calls=%async_computation.3 | async-start | bytes 270336 | tf_op jit(solution)/shard_map/all_to_all | solution.py:176

commit v9 on v8

--- a/solution.py
+++ b/solution.py
@@ -131,27 +131,24 @@
     )
     bias_terms = jnp.sum(grad_pre.astype(f32), axis=1)
 
-    grad_terms = jnp.concatenate(
-        [
-            weight_terms.reshape(feat_count, channels, width),
-            bias_terms.reshape(feat_count, channels, 1),
-        ],
-        axis=2,
-    )
     second_send = jnp.concatenate(
         [
             out_block.reshape(feat_count, channels, col_width),
             grad_agg_block.reshape(feat_count, channels, col_width),
+            weight_terms.reshape(feat_count, channels, width).astype(bf16),
         ]
-        + bf16_parts(grad_terms, 1),
+        + bf16_parts(bias_terms.reshape(feat_count, channels, 1), 2),
         axis=2,
     )
     second_recv = lax.all_to_all(second_send, "feat", split_axis=0, concat_axis=0, tiled=True)
     layer_out = from_blocks(second_recv[:, :, :col_width])
     grad_agg = from_blocks(second_recv[:, :, col_width : 2 * col_width])
-    terms_width = width + 1
     start = 2 * col_width
-    panel_terms = jnp.sum(second_recv[:, :, start : start + terms_width].astype(f32), axis=0)
+    weight_part = second_recv[:, :, start : start + width].astype(f32)
+    bias_part = parts_sum(
+        [second_recv[:, :, start + width : start + width + 1], second_recv[:, :, start + width + 1 :]]
+    )
+    panel_terms = jnp.sum(jnp.concatenate([weight_part, bias_part], axis=2), axis=0)
 
     grad_blocks = grad_agg.reshape(channels, row_blocks, block_size)
     spread_out = over_tiles(
@@ -164,12 +161,15 @@
     depth_terms = jnp.sum(states * own_grad[None], axis=2) + jnp.sum(
         halo_states * halo_terms[None], axis=(2, 3)
     )
-    totals = jnp.concatenate([panel_terms.reshape(-1), depth_terms.reshape(-1)]) * norm_scale
+    weight_total = panel_terms[:, :width].reshape(-1) * norm_scale
+    small_total = (
+        jnp.concatenate([panel_terms[:, width], depth_terms.reshape(-1)]) * norm_scale
+    )
     last_send = jnp.concatenate(
         [halo_part.astype(bf16).transpose(1, 0, 2).reshape(section_count, channels * halo_width)]
         + [
-            jnp.broadcast_to(part[None, :], (vert_count, totals.shape[0]))
-            for part in bf16_parts(totals, 1)
+            jnp.broadcast_to(part[None, :], (vert_count, part.shape[0]))
+            for part in [weight_total.astype(bf16)] + bf16_parts(small_total, 2)
         ],
         axis=1,
     )
@@ -180,7 +180,18 @@
         .transpose(1, 0, 2)
     )
     tail = last_recv[:, channels * halo_width :]
-    totals = jnp.sum(tail.astype(f32), axis=0)
+    weight_count = weight_total.shape[0]
+    small_count = small_total.shape[0]
+    weight_sum = jnp.sum(tail[:, :weight_count].astype(f32), axis=0)
+    small_sum = jnp.sum(
+        parts_sum(
+            [
+                tail[:, weight_count : weight_count + small_count],
+                tail[:, weight_count + small_count :],
+            ]
+        ),
+        axis=0,
+    )
     hot = (
         my_send.reshape(-1)[None, :] == jnp.arange(row_count, dtype=jnp.int32)[:, None]
     ).astype(bf16)
@@ -192,14 +203,12 @@
     )
     grad_mixed = own_grad + added.T
     grad_states = (depth_weight[:, :, None] * grad_mixed[None]).astype(bf16)
-    panel_sum = totals[: panel_terms.size].reshape(panel_terms.shape)
-    depth_sum = totals[panel_terms.size :].reshape(depth_terms.shape)
     return (
         layer_out,
         grad_states,
-        panel_sum[:, :width],
-        panel_sum[:, width],
-        depth_sum,
+        weight_sum.reshape(channels, width),
+        small_sum[:channels],
+        small_sum[channels:].reshape(depth_terms.shape),
     )
 
 

time: 121 us -> 121 us (level)
    unnamed x20 -> x23, local copies, waits for them, and re-layouts: 3.07 us -> 3.07 us
where the time goes in v9:
time: 121 us; the launch traced here: 120 us
  waiting for transfers between devices  29.6 us (24%)
  starting transfers between devices  29.5 us (24%)
  blocking collectives  19.4 us (16%)
  matrix products  18.7 us (15%)
  local copies, waits for them, and re-layouts  15.8 us (13%)
  other arithmetic  5.67 us (5%)
  between operations  1.72 us (1%)
    all_to_all x1, blocking collectives, local(): lax.all_to_all(first_send, 'feat', split_axis=0, concat_axis=0, tiled=True)  19.4 us
    all_to_all x1, starting transfers between devices, local(): lax.all_to_all(listed.reshape(state_count, channels, section_count, halo_...  16.7 us
    all_to_all x1, waiting for transfers between devices, local(): lax.all_to_all(last_send, 'vert', split_axis=0, concat_axis=0, tiled=True)  11.9 us
    all_to_all x1, waiting for transfers between devices, local(): lax.all_to_all(second_send, 'feat', split_axis=0, concat_axis=0, tiled=True)  10.7 us
    all_to_all x1, starting transfers between devices, local(): lax.all_to_all(last_send, 'vert', split_axis=0, concat_axis=0, tiled=True)  8.05 us
    dot_general x1, matrix products, tile_forward(): jnp.einsum('dtc,trc->dtr', picked, tile_grp, preferred_element_type=jnp.f...  7.8 us
    all_to_all x1, waiting for transfers between devices, local(): lax.all_to_all(listed.reshape(state_count, channels, section_count, halo_...  6.98 us
    dot_general x1, matrix products, tile_backward(): jnp.einsum('dtr,trc->dtc', picked, tile_grp, preferred_element_type=jnp.f...  5.65 us
  transfers between devices with their start and end apart: 3, of which 3 were waited for; matrix products, arithmetic and copies ran while one was open for 3% of the time, Pallas kernels for 0%

profile of v9, /device:TPU:1, one launch (start us, length us, event | category | flops | bytes accessed | tf_op | source)
XLA Modules:
  0.0 120.3 jit_solution(5783066647038179495)
XLA Ops:
  0.7 1.5 %copy.109 = bf16[32,4096]{0,1:T(8,128)(2,1)S(1)} copy(bf16[32,4096]{1,0:T(8,128)(2,1)} %bitcast.96) | data formatting | bytes 524288 | tf_op jit(solution)/shard_map/reshape | solution.py:91
  2.1 0.8 reshape_squeeze.3
  3.0 3.2 %gather_fusion = bf16[1536,32]{1,0:T(8,128)(2,1)S(1)} fusion(bf16[32,4096]{0,1:T(8,128)(2,1)S(1)} %copy.109, s32[2048]{0:T(1024)S(1)} %pad_clamp_fusion), kind=kCustom, calls=%fused_computation | custom fusion | bytes 202752 | tf_op jit(solution)/shard_map/gather | solution.py:93
  6.2 0.2 copy.110
  6.3 0.2 reshape.259
  6.5 0.8 reshape.302
  7.3 16.7 %all-to-all-start = ((bf16[24,2,1024]{2,1,0:T(2,128)(2,1)}), bf16[24,2,1024]{2,1,0:T(2,128)(2,1)S(1)}, u32[]{:S(2)}, u32[]{:S(2)}) async-start(bf16[24,2,1024]{2,1,0:T(2,128)(2,1)} %reshape.302), calls=%async_computation | async-start | bytes 196608 | tf_op jit(solution)/shard_map/all_to_all | solution.py:95
  24.0 0.7 fusion.40
  24.7 0.7 compare_select_fusion.2
  26.2 0.8 copy.144
  27.0 1.1 fusion.18
  28.1 7.0 %all-to-all-done = bf16[24,2,1024]{2,1,0:T(2,128)(2,1)S(1)} async-done(((bf16[24,2,1024]{2,1,0:T(2,128)(2,1)}), bf16[24,2,1024]{2,1,0:T(2,128)(2,1)S(1)}, u32[]{:S(2)}, u32[]{:S(2)}) %all-to-all-start) | async-done | bytes 98336 | tf_op jit(solution)/shard_map/all_to_all | solution.py:95
  35.1 0.2 reshape.303
  35.3 0.8 fusion.22
  36.2 0.8 gather_fusion.1
  37.0 7.8 %fusion.7 = bf16[8,256,128]{2,0,1:T(8,128)(2,1)S(1)} fusion(bf16[1,256,128,128]{3,2,1,0:T(8,128)(2,1)} %param.12, bf16[256,8,128]{2,1,0:T(8,128)(2,1)S(1)} %gather_fusion.1), kind=kOutput, calls=%fused_computation.11 | convolution fusion | flops 67108864 | bytes 9437184 | tf_op jit(solution)/shard_map/dtc,trc->dtr/dot_general | solution.py:11
  44.8 0.2 convolution_convert_fusion.1
  45.2 19.4 %all_to_all.27 = bf16[32,8,259]{2,1,0:T(8,128)(2,1)S(1)} all-to-all(bf16[32,8,259]{2,1,0:T(8,128)(2,1)S(1)} %copy.115), channel_id=1, replica_groups=mesh['vert'=24,'feat'=32] {'feat'}, dimensions={0} | all-to-all | bytes 265216 | tf_op jit(solution)/shard_map/all_to_all | solution.py:115
  64.6 0.2 add_reduce_fusion
  64.8 0.1 copy.129
  64.9 0.3 convert_reduce_fusion.1
  65.2 0.2 fusion.15
  65.4 0.2 fusion.13
  65.6 0.1 copy.116
  65.7 0.1 copy.118
  66.0 0.2 copy.121
  66.1 0.2 copy.122
  66.3 0.8 concatenate.29
  67.1 4.7 %all-to-all-start.2 = ((bf16[32,8,514]{2,1,0:T(8,128)(2,1)}), bf16[32,8,514]{2,1,0:T(8,128)(2,1)S(1)}, u32[]{:S(2)}, u32[]{:S(2)}) async-start(bf16[32,8,514]{2,1,0:T(8,128)(2,1)} %concatenate.29), calls=%async_computation.2 | async-start | bytes 655360 | tf_op jit(solution)/shard_map/all_to_all | solution.py:143
  71.9 10.7 %all-to-all-done.2 = bf16[32,8,514]{2,1,0:T(8,128)(2,1)S(1)} async-done(((bf16[32,8,514]{2,1,0:T(8,128)(2,1)}), bf16[32,8,514]{2,1,0:T(8,128)(2,1)S(1)}, u32[]{:S(2)}, u32[]{:S(2)}) %all-to-all-start.2) | async-done | bytes 263200 | tf_op jit(solution)/shard_map/all_to_all | solution.py:143
  82.6 0.6 slice_bitcast_fusion
  83.2 0.8 gather_fusion.2
  84.1 5.7 %fusion.10 = bf16[8,256,128]{2,0,1:T(8,128)(2,1)S(1)} fusion(bf16[1,256,128,128]{3,2,1,0:T(8,128)(2,1)} %param.12, bf16[256,8,128]{2,1,0:T(8,128)(2,1)S(1)} %gather_fusion.2), kind=kOutput, calls=%fused_computation.12 | convolution fusion | flops 67108864 | bytes 9437184 | tf_op jit(solution)/shard_map/dtr,trc->dtc/dot_general | solution.py:20
  89.7 0.2 convolution_bitcast_fusion
  90.2 0.1 slice_reduce_fusion
  90.5 0.1 reshape.268
  90.6 0.2 fusion.19
  90.8 0.1 fusion.23
  91.3 0.5 broadcast.93
  91.8 0.7 reduce.6
  92.5 0.8 reshape.304
  93.3 8.0 %all-to-all-start.3 = ((bf16[24,2,1320]{2,1,0:T(2,128)(2,1)}), bf16[24,2,1320]{2,1,0:T(2,128)(2,1)S(1)}, u32[]{:S(2)}, u32[]{:S(2)}) async-start(bf16[24,2,1320]{2,1,0:T(2,128)(2,1)} %reshape.304), calls=%async_computation.3 | async-start | bytes 270336 | tf_op jit(solution)/shard_map/all_to_all | solution.py:176
  101.5 11.9 %all-to-all-done.3 = bf16[24,2,1320]{2,1,0:T(2,128)(2,1)S(1)} async-done(((bf16[24,2,1320]{2,1,0:T(2,128)(2,1)}), bf16[24,2,1320]{2,1,0:T(2,128)(2,1)S(1)}, u32[]{:S(2)}, u32[]{:S(2)}) %all-to-all-start.3) | async-done | bytes 126752 | tf_op jit(solution)/shard_map/all_to_all | solution.py:176
  113.4 0.2 reshape.305
  114.0 4.2 %fusion.6 = f32[8,4096]{1,0:T(8,128)S(1)} fusion(bf16[8,1536]{1,0:T(8,128)(2,1)S(1)} %reshape.270, s32[1536]{0:T(1024)S(1)} %eq.53, f32[8,5632]{1,0:T(8,128)S(1)} %bitcast.104), kind=kOutput, calls=%fused_computation.10 | convolution fusion | flops 106987520 | bytes 292864 | tf_op jit(solution)/shard_map/dot_general | solution.py:198
  118.2 0.8 multiply_convert_fusion
  119.0 0.6 reshape.271
  119.7 0.7 reshape.272
  (63 shorter events, 1.9 us)
Async XLA Ops:
  0.6 64.3 %copy-start = (bf16[256,256]{1,0:T(8,128)(2,1)S(1)}, bf16[256,256]{1,0:T(8,128)(2,1)}, u32[]{:S(2)}) copy-start(bf16[256,256]{1,0:T(8,128)(2,1)} %param.17) | copy-start | bytes 393220
  0.6 44.2 %copy-start.4 = (s32[1,256]{1,0:T(1,128)S(1)}, s32[1,256]{1,0:T(1,128)}, u32[]{:S(2)}) copy-start(s32[1,256]{1,0:T(1,128)} %param.13) | copy-start | bytes 3076
  7.3 27.8 %all-to-all-start = ((bf16[24,2,1024]{2,1,0:T(2,128)(2,1)}), bf16[24,2,1024]{2,1,0:T(2,128)(2,1)S(1)}, u32[]{:S(2)}, u32[]{:S(2)}) async-start(bf16[24,2,1024]{2,1,0:T(2,128)(2,1)} %reshape.302), calls=%async_computation | async-start | bytes 196608 | tf_op jit(solution)/shard_map/all_to_all | solution.py:95
  44.8 44.9 %copy-start.5 = (s32[1,256]{1,0:T(1,128)S(1)}, s32[1,256]{1,0:T(1,128)}, u32[]{:S(2)}) copy-start(s32[1,256]{1,0:T(1,128)} %param.14) | copy-start | bytes 3076
  64.9 25.7 %copy-start.1 = (bf16[4,8,4096]{2,1,0:T(8,128)(2,1)S(1)}, bf16[4,8,4096]{2,1,0:T(8,128)(2,1)}, u32[]{:S(2)}) copy-start(bf16[4,8,4096]{2,1,0:T(8,128)(2,1)} %param.10) | copy-start | bytes 786436
  67.1 34.3 %copy-start.2 = (s32[1,24,64]{2,1,0:T(8,128)S(1)}, s32[1,24,64]{2,1,0:T(8,128)}, u32[]{:S(2)}) copy-start(s32[1,24,64]{2,1,0:T(8,128)} %param.16) | copy-start | bytes 18436
  67.1 15.5 %all-to-all-start.2 = ((bf16[32,8,514]{2,1,0:T(8,128)(2,1)}), bf16[32,8,514]{2,1,0:T(8,128)(2,1)S(1)}, u32[]{:S(2)}, u32[]{:S(2)}) async-start(bf16[32,8,514]{2,1,0:T(8,128)(2,1)} %concatenate.29), calls=%async_computation.2 | async-start | bytes 655360 | tf_op jit(solution)/shard_map/all_to_all | solution.py:143
  89.7 28.5 %copy-start.3 = (f32[4,8]{1,0:T(4,128)S(1)}, f32[4,8]{1,0:T(4,128)}, u32[]{:S(2)}) copy-start(f32[4,8]{1,0:T(4,128)} %param.11) | copy-start | bytes 388
  93.3 20.0 %all-to-all-start.3 = ((bf16[24,2,1320]{2,1,0:T(2,128)(2,1)}), bf16[24,2,1320]{2,1,0:T(2,128)(2,1)S(1)}, u32[]{:S(2)}, u32[]{:S(2)}) async-start(bf16[24,2,1320]{2,1,0:T(2,128)(2,1)} %reshape.304), calls=%async_computation.3 | async-start | bytes 270336 | tf_op jit(solution)/shard_map/all_to_all | solution.py:176
  113.7 6.6 %copy-start.6 = (f32[40]{0:T(128)}, f32[40]{0:T(128)S(1)}, u32[]{:S(2)}) copy-start(f32[40]{0:T(128)S(1)} %add_reduce_fusion.1) | copy-start | bytes 484

commit v10 on v9

--- a/solution.py
+++ b/solution.py
@@ -87,10 +87,18 @@
         return x.transpose(1, 0, 2).reshape(channels, row_count)
 
     state_count = states.shape[0]
+    pick = (
+        my_send.reshape(-1)[:, None] == jnp.arange(row_count, dtype=jnp.int32)[None, :]
+    ).astype(bf16)
     listed = (
-        states.reshape(state_count * channels, row_count)
-        .at[:, my_send.reshape(-1)]
-        .get(mode="promise_in_bounds")
+        lax.dot_general(
+            pick,
+            states.reshape(state_count * channels, row_count),
+            (((1,), (1,)), ((), ())),
+            preferred_element_type=f32,
+        )
+        .astype(bf16)
+        .T
     )
     halo_states = lax.all_to_all(
         listed.reshape(state_count, channels, section_count, halo_width),

time: 121 us -> 120 us (level)
  blocking collectives: 19.4 us -> 38.8 us
  waiting for transfers between devices: 29.6 us -> 20.8 us
  starting transfers between devices: 29.5 us -> 21.3 us
  local copies, waits for them, and re-layouts: 15.8 us -> 9.45 us
  matrix products: 18.7 us -> 24.9 us
  other arithmetic: 5.67 us -> 2.67 us
    all_to_all x0 -> x1, blocking collectives: none -> 19.4 us  [local(): lax.all_to_all(last_send, 'vert', split_axis=0, concat_axis=0, tiled=True)]
    all_to_all x1 -> x0, waiting for transfers between devices: 11.9 us -> none  [local(): lax.all_to_all(last_send, 'vert', split_axis=0, concat_axis=0, tiled=True)]
    all_to_all x1 -> x0, starting transfers between devices: 8.05 us -> none  [local(): lax.all_to_all(last_send, 'vert', split_axis=0, concat_axis=0, tiled=True)]
    dot_general x0 -> x1, matrix products: none -> 6.19 us  [local(): lax.dot_general(pick, states.reshape(state_count * channels, row_count),...]
    gather x2 -> x0, local copies, waits for them, and re-layouts: 3.36 us -> none  [local(): listed = states.reshape(state_count * channels, row_count).at[:, my_send....]
    all_to_all x1, waiting for transfers between devices: 6.98 us -> 10.1 us  [local(): lax.all_to_all(listed.reshape(state_count, channels, section_count, halo_...]
    unnamed x23 -> x25, local copies, waits for them, and re-layouts: 3.07 us -> 1.58 us
    reshape x1 -> x0, local copies, waits for them, and re-layouts: 1.46 us -> none  [local(): states.reshape(state_count * channels, row_count).at[:, my_send.reshape(-1)]]
  transfers between devices with their start and end apart: 3 -> 2, of which waited for: 3 -> 2; matrix products, arithmetic and copies ran while one was open for 3% -> 0% of each run, Pallas kernels for 0% -> 0%
where the time goes in v10:
time: 120 us
  blocking collectives  38.8 us (32%)
  matrix products  24.9 us (21%)
  starting transfers between devices  21.3 us (18%)
  waiting for transfers between devices  20.8 us (17%)
  local copies, waits for them, and re-layouts  9.45 us (8%)
  other arithmetic  2.67 us (2%)
  between operations  1.73 us (1%)
    all_to_all x1, blocking collectives, local(): lax.all_to_all(last_send, 'vert', split_axis=0, concat_axis=0, tiled=True)  19.4 us
    all_to_all x1, blocking collectives, local(): lax.all_to_all(first_send, 'feat', split_axis=0, concat_axis=0, tiled=True)  19.4 us
    all_to_all x1, starting transfers between devices, local(): lax.all_to_all(listed.reshape(state_count, channels, section_count, halo_...  16.7 us
    all_to_all x1, waiting for transfers between devices, local(): lax.all_to_all(second_send, 'feat', split_axis=0, concat_axis=0, tiled=True)  10.7 us
    all_to_all x1, waiting for transfers between devices, local(): lax.all_to_all(listed.reshape(state_count, channels, section_count, halo_...  10.1 us
    dot_general x1, matrix products, tile_forward(): jnp.einsum('dtc,trc->dtr', picked, tile_grp, preferred_element_type=jnp.f...  7.8 us
    dot_general x1, matrix products, local(): lax.dot_general(pick, states.reshape(state_count * channels, row_count),...  6.19 us
    dot_general x1, matrix products, tile_backward(): jnp.einsum('dtr,trc->dtc', picked, tile_grp, preferred_element_type=jnp.f...  5.65 us
  transfers between devices with their start and end apart: 2, of which 2 were waited for; matrix products, arithmetic and copies ran while one was open for 0% of the time, Pallas kernels for 0%

profile of v10, /device:TPU:1, one launch (start us, length us, event | category | flops | bytes accessed | tf_op | source)
XLA Modules:
  0.0 119.6 jit_solution(3518117817963110549)
XLA Ops:
  0.7 0.9 eq.62
  1.6 6.2 %fusion.10 = bf16[32,1536]{1,0:T(8,128)(2,1)S(1)} fusion(s32[1536]{0:T(1024)S(1)} %eq.62, bf16[4,8,4096]{2,1,0:T(8,128)(2,1)} %param.10), kind=kOutput, calls=%fused_computation.14 | convolution fusion | flops 408993792 | bytes 366592 | tf_op jit(solution)/shard_map/dot_general | solution.py:94
  7.8 0.2 reshape.232
  8.0 0.8 reshape.266
  8.8 16.7 %all-to-all-start = ((bf16[24,2,1024]{2,1,0:T(2,128)(2,1)}), bf16[24,2,1024]{2,1,0:T(2,128)(2,1)S(1)}, u32[]{:S(2)}, u32[]{:S(2)}) async-start(bf16[24,2,1024]{2,1,0:T(2,128)(2,1)} %reshape.266), calls=%async_computation | async-start | bytes 196608 | tf_op jit(solution)/shard_map/all_to_all | solution.py:103
  26.2 0.1 copy.98
  26.4 0.1 fusion.22
  26.5 10.1 %all-to-all-done = bf16[24,2,1024]{2,1,0:T(2,128)(2,1)S(1)} async-done(((bf16[24,2,1024]{2,1,0:T(2,128)(2,1)}), bf16[24,2,1024]{2,1,0:T(2,128)(2,1)S(1)}, u32[]{:S(2)}, u32[]{:S(2)}) %all-to-all-start) | async-done | bytes 98336 | tf_op jit(solution)/shard_map/all_to_all | solution.py:103
  36.5 0.2 reshape.267
  36.7 0.1 fusion.26
  36.8 0.1 convert_element_type.158
  37.0 0.8 gather_fusion
  37.8 7.8 %fusion.11 = bf16[8,256,128]{2,0,1:T(8,128)(2,1)S(1)} fusion(bf16[1,256,128,128]{3,2,1,0:T(8,128)(2,1)} %param.12, bf16[256,8,128]{2,1,0:T(8,128)(2,1)S(1)} %gather_fusion), kind=kOutput, calls=%fused_computation.15 | convolution fusion | flops 67108864 | bytes 9437184 | tf_op jit(solution)/shard_map/dtc,trc->dtr/dot_general | solution.py:11
  45.6 0.2 convolution_convert_fusion.1
  45.9 19.4 %all_to_all.27 = bf16[32,8,259]{2,1,0:T(8,128)(2,1)S(1)} all-to-all(bf16[32,8,259]{2,1,0:T(8,128)(2,1)S(1)} %copy.99), channel_id=1, replica_groups=mesh['vert'=24,'feat'=32] {'feat'}, dimensions={0} | all-to-all | bytes 265216 | tf_op jit(solution)/shard_map/all_to_all | solution.py:123
  65.3 0.2 add_reduce_fusion
  65.5 0.1 copy.113
  65.7 0.3 convert_reduce_fusion.1
  65.9 0.2 fusion.17
  66.1 0.2 fusion.19
  66.5 0.2 copy.106
  66.6 0.2 copy.105
  66.8 0.1 copy.100
  66.9 0.1 copy.102
  67.0 0.8 concatenate.29
  67.9 4.6 %all-to-all-start.2 = ((bf16[32,8,514]{2,1,0:T(8,128)(2,1)}), bf16[32,8,514]{2,1,0:T(8,128)(2,1)S(1)}, u32[]{:S(2)}, u32[]{:S(2)}) async-start(bf16[32,8,514]{2,1,0:T(8,128)(2,1)} %concatenate.29), calls=%async_computation.2 | async-start | bytes 655360 | tf_op jit(solution)/shard_map/all_to_all | solution.py:151
  72.5 10.7 %all-to-all-done.2 = bf16[32,8,514]{2,1,0:T(8,128)(2,1)S(1)} async-done(((bf16[32,8,514]{2,1,0:T(8,128)(2,1)}), bf16[32,8,514]{2,1,0:T(8,128)(2,1)S(1)}, u32[]{:S(2)}, u32[]{:S(2)}) %all-to-all-start.2) | async-done | bytes 263200 | tf_op jit(solution)/shard_map/all_to_all | solution.py:151
  83.4 0.1 slice_reduce_fusion
  83.5 0.6 slice_bitcast_fusion
  84.1 0.8 gather_fusion.1
  85.0 5.7 %fusion.14 = bf16[8,256,128]{2,0,1:T(8,128)(2,1)S(1)} fusion(bf16[1,256,128,128]{3,2,1,0:T(8,128)(2,1)} %param.12, bf16[256,8,128]{2,1,0:T(8,128)(2,1)S(1)} %gather_fusion.1), kind=kOutput, calls=%fused_computation.16 | convolution fusion | flops 67108864 | bytes 9437184 | tf_op jit(solution)/shard_map/dtr,trc->dtc/dot_general | solution.py:20
  90.6 0.2 convolution_bitcast_fusion
  90.9 0.1 convert_element_type.177
  91.1 0.1 reshape.241
  91.3 0.2 fusion.27
  91.4 0.2 fusion.23
  91.8 0.1 concatenate.33
  91.9 0.5 broadcast.74
  92.4 0.7 reduce.4
  93.1 0.2 reshape.268
  93.3 19.4 %all_to_all.28 = bf16[24,2,1320]{2,1,0:T(2,128)(2,1)S(1)} all-to-all(bf16[24,2,1320]{2,1,0:T(2,128)(2,1)S(1)} %reshape.268), channel_id=1, replica_groups=mesh['vert'=24,'feat'=32] {'vert'}, dimensions={0} | all-to-all | bytes 253440 | tf_op jit(solution)/shard_map/all_to_all | solution.py:184
  112.7 0.2 reshape.269
  113.1 0.7 reshape.245
  113.8 0.6 reshape.244
  114.4 0.1 reshape.242
  114.5 0.1 reshape.243
  114.6 4.2 %fusion.8 = f32[8,4096]{1,0:T(8,128)S(1)} fusion(bf16[8,1536]{1,0:T(8,128)(2,1)S(1)} %reshape.243, s32[1536]{0:T(1024)S(1)} %eq.62, f32[8,5632]{1,0:T(8,128)S(1)} %bitcast.106), kind=kOutput, calls=%fused_computation.12 | convolution fusion | flops 106987520 | bytes 292864 | tf_op jit(solution)/shard_map/dot_general | solution.py:206
  118.8 0.8 multiply_convert_fusion
  (59 shorter events, 1.2 us)
Async XLA Ops:
  0.6 65.0 %copy-start = (bf16[256,256]{1,0:T(8,128)(2,1)S(1)}, bf16[256,256]{1,0:T(8,128)(2,1)}, u32[]{:S(2)}) copy-start(bf16[256,256]{1,0:T(8,128)(2,1)} %param.17) | copy-start | bytes 393220
  0.6 25.7 %copy-start.1 = (bf16[4,8,4096]{2,1,0:T(8,128)(2,1)S(1)}, bf16[4,8,4096]{2,1,0:T(8,128)(2,1)}, u32[]{:S(2)}) copy-start(bf16[4,8,4096]{2,1,0:T(8,128)(2,1)} %param.10) | copy-start | bytes 786436
  0.7 25.5 %copy-start.5 = (s32[1,256]{1,0:T(1,128)S(1)}, s32[1,256]{1,0:T(1,128)}, u32[]{:S(2)}) copy-start(s32[1,256]{1,0:T(1,128)} %param.14) | copy-start | bytes 3076
  0.7 25.5 %copy-start.7 = (f32[8]{0:T(128)S(1)}, f32[8]{0:T(128)}, u32[]{:S(2)}) copy-start(f32[8]{0:T(128)} %param.18) | copy-start | bytes 100
  0.7 25.6 %copy-start.2 = (bf16[8,4096]{1,0:T(8,128)(2,1)S(1)}, bf16[8,4096]{1,0:T(8,128)(2,1)}, u32[]{:S(2)}) copy-start(bf16[8,4096]{1,0:T(8,128)(2,1)} %param.19) | copy-start | bytes 196612
  0.7 25.7 %copy-start.3 = (f32[4,8]{1,0:T(4,128)S(1)}, f32[4,8]{1,0:T(4,128)}, u32[]{:S(2)}) copy-start(f32[4,8]{1,0:T(4,128)} %param.11) | copy-start | bytes 388
  7.8 37.8 %copy-start.4 = (s32[1,256]{1,0:T(1,128)S(1)}, s32[1,256]{1,0:T(1,128)}, u32[]{:S(2)}) copy-start(s32[1,256]{1,0:T(1,128)} %param.13) | copy-start | bytes 3076
  8.8 27.7 %all-to-all-start = ((bf16[24,2,1024]{2,1,0:T(2,128)(2,1)}), bf16[24,2,1024]{2,1,0:T(2,128)(2,1)S(1)}, u32[]{:S(2)}, u32[]{:S(2)}) async-start(bf16[24,2,1024]{2,1,0:T(2,128)(2,1)} %reshape.266), calls=%async_computation | async-start | bytes 196608 | tf_op jit(solution)/shard_map/all_to_all | solution.py:103
  67.9 15.4 %all-to-all-start.2 = ((bf16[32,8,514]{2,1,0:T(8,128)(2,1)}), bf16[32,8,514]{2,1,0:T(8,128)(2,1)S(1)}, u32[]{:S(2)}, u32[]{:S(2)}) async-start(bf16[32,8,514]{2,1,0:T(8,128)(2,1)} %concatenate.29), calls=%async_computation.2 | async-start | bytes 655360 | tf_op jit(solution)/shard_map/all_to_all | solution.py:151
  113.0 6.6 %copy-start.6 = (f32[40]{0:T(128)}, f32[40]{0:T(128)S(1)}, u32[]{:S(2)}) copy-start(f32[40]{0:T(128)S(1)} %add_reduce_fusion.1) | copy-start | bytes 484

commit v11 on v9

--- a/solution.py
+++ b/solution.py
@@ -87,11 +87,12 @@
         return x.transpose(1, 0, 2).reshape(channels, row_count)
 
     state_count = states.shape[0]
-    listed = (
-        states.reshape(state_count * channels, row_count)
-        .at[:, my_send.reshape(-1)]
-        .get(mode="promise_in_bounds")
-    )
+    pick = (
+        jnp.arange(row_count, dtype=jnp.int32)[:, None] == my_send.reshape(-1)[None, :]
+    ).astype(bf16)
+    listed = jnp.dot(
+        states.reshape(state_count * channels, row_count), pick, preferred_element_type=f32
+    ).astype(bf16)
     halo_states = lax.all_to_all(
         listed.reshape(state_count, channels, section_count, halo_width),
         "vert",

time: 121 us -> 119 us (0.983)
  blocking collectives: 19.4 us -> 38.9 us
  waiting for transfers between devices: 29.6 us -> 20.8 us
  starting transfers between devices: 29.5 us -> 21.3 us
  local copies, waits for them, and re-layouts: 15.8 us -> 9.45 us
  matrix products: 18.7 us -> 23.6 us
  other arithmetic: 5.67 us -> 2.67 us
    all_to_all x0 -> x1, blocking collectives: none -> 19.5 us  [local(): lax.all_to_all(last_send, 'vert', split_axis=0, concat_axis=0, tiled=True)]
    all_to_all x1 -> x0, waiting for transfers between devices: 11.9 us -> none  [local(): lax.all_to_all(last_send, 'vert', split_axis=0, concat_axis=0, tiled=True)]
    all_to_all x1 -> x0, starting transfers between devices: 8.05 us -> none  [local(): lax.all_to_all(last_send, 'vert', split_axis=0, concat_axis=0, tiled=True)]
    dot_general x0 -> x1, matrix products: none -> 4.95 us  [local(): jnp.dot(states.reshape(state_count * channels, row_count), pick, preferre...]
    gather x2 -> x0, local copies, waits for them, and re-layouts: 3.36 us -> none  [local(): listed = states.reshape(state_count * channels, row_count).at[:, my_send....]
    all_to_all x1, waiting for transfers between devices: 6.98 us -> 10.1 us  [local(): lax.all_to_all(listed.reshape(state_count, channels, section_count, halo_...]
    unnamed x23 -> x25, local copies, waits for them, and re-layouts: 3.07 us -> 1.58 us
    reshape x1 -> x0, local copies, waits for them, and re-layouts: 1.46 us -> none  [local(): states.reshape(state_count * channels, row_count).at[:, my_send.reshape(-1)]]
  transfers between devices with their start and end apart: 3 -> 2, of which waited for: 3 -> 2; matrix products, arithmetic and copies ran while one was open for 3% -> 0% of each run, Pallas kernels for 0% -> 0%
where the time goes in v11:
time: 119 us; the launch traced here: 118 us
  blocking collectives  38.9 us (33%)
  matrix products  23.6 us (20%)
  starting transfers between devices  21.3 us (18%)
  waiting for transfers between devices  20.8 us (17%)
  local copies, waits for them, and re-layouts  9.45 us (8%)
  other arithmetic  2.67 us (2%)
  between operations  1.74 us (1%)
    all_to_all x1, blocking collectives, local(): lax.all_to_all(last_send, 'vert', split_axis=0, concat_axis=0, tiled=True)  19.5 us
    all_to_all x1, blocking collectives, local(): lax.all_to_all(first_send, 'feat', split_axis=0, concat_axis=0, tiled=True)  19.4 us
    all_to_all x1, starting transfers between devices, local(): lax.all_to_all(listed.reshape(state_count, channels, section_count, halo_...  16.7 us
    all_to_all x1, waiting for transfers between devices, local(): lax.all_to_all(second_send, 'feat', split_axis=0, concat_axis=0, tiled=True)  10.7 us
    all_to_all x1, waiting for transfers between devices, local(): lax.all_to_all(listed.reshape(state_count, channels, section_count, halo_...  10.1 us
    dot_general x1, matrix products, tile_forward(): jnp.einsum('dtc,trc->dtr', picked, tile_grp, preferred_element_type=jnp.f...  7.8 us
    dot_general x1, matrix products, tile_backward(): jnp.einsum('dtr,trc->dtc', picked, tile_grp, preferred_element_type=jnp.f...  5.65 us
    dot_general x1, matrix products, local(): jnp.dot(states.reshape(state_count * channels, row_count), pick, preferre...  4.95 us
  transfers between devices with their start and end apart: 2, of which 2 were waited for; matrix products, arithmetic and copies ran while one was open for 0% of the time, Pallas kernels for 0%

profile of v11, /device:TPU:1, one launch (start us, length us, event | category | flops | bytes accessed | tf_op | source)
XLA Modules:
  0.0 118.5 jit_solution(6738877628974667375)
XLA Ops:
  0.7 0.9 eq.61
  1.6 4.9 %fusion.10 = bf16[32,1536]{1,0:T(8,128)(2,1)S(1)} fusion(s32[1536]{0:T(1024)S(1)} %eq.61, bf16[4,8,4096]{2,1,0:T(8,128)(2,1)} %param.10), kind=kOutput, calls=%fused_computation.14 | convolution fusion | flops 408993792 | bytes 366592 | tf_op jit(solution)/shard_map/dot_general | solution.py:93
  6.5 0.2 reshape.231
  6.7 0.8 reshape.265
  7.5 16.7 %all-to-all-start = ((bf16[24,2,1024]{2,1,0:T(2,128)(2,1)}), bf16[24,2,1024]{2,1,0:T(2,128)(2,1)S(1)}, u32[]{:S(2)}, u32[]{:S(2)}) async-start(bf16[24,2,1024]{2,1,0:T(2,128)(2,1)} %reshape.265), calls=%async_computation | async-start | bytes 196608 | tf_op jit(solution)/shard_map/all_to_all | solution.py:96
  25.0 0.1 copy.98
  25.1 0.1 fusion.22
  25.2 10.1 %all-to-all-done = bf16[24,2,1024]{2,1,0:T(2,128)(2,1)S(1)} async-done(((bf16[24,2,1024]{2,1,0:T(2,128)(2,1)}), bf16[24,2,1024]{2,1,0:T(2,128)(2,1)S(1)}, u32[]{:S(2)}, u32[]{:S(2)}) %all-to-all-start) | async-done | bytes 98336 | tf_op jit(solution)/shard_map/all_to_all | solution.py:96
  35.3 0.2 reshape.266
  35.5 0.1 fusion.26
  35.6 0.1 convert_element_type.157
  35.7 0.8 gather_fusion
  36.6 7.8 %fusion.11 = bf16[8,256,128]{2,0,1:T(8,128)(2,1)S(1)} fusion(bf16[1,256,128,128]{3,2,1,0:T(8,128)(2,1)} %param.12, bf16[256,8,128]{2,1,0:T(8,128)(2,1)S(1)} %gather_fusion), kind=kOutput, calls=%fused_computation.15 | convolution fusion | flops 67108864 | bytes 9437184 | tf_op jit(solution)/shard_map/dtc,trc->dtr/dot_general | solution.py:11
  44.4 0.2 convolution_convert_fusion.1
  44.7 19.4 %all_to_all.27 = bf16[32,8,259]{2,1,0:T(8,128)(2,1)S(1)} all-to-all(bf16[32,8,259]{2,1,0:T(8,128)(2,1)S(1)} %copy.99), channel_id=1, replica_groups=mesh['vert'=24,'feat'=32] {'feat'}, dimensions={0} | all-to-all | bytes 265216 | tf_op jit(solution)/shard_map/all_to_all | solution.py:116
  64.1 0.2 add_reduce_fusion
  64.3 0.1 copy.113
  64.4 0.3 convert_reduce_fusion.1
  64.7 0.2 fusion.17
  64.9 0.2 fusion.19
  65.2 0.2 copy.106
  65.4 0.2 copy.105
  65.6 0.1 copy.100
  65.7 0.1 copy.102
  65.8 0.8 concatenate.29
  66.6 4.6 %all-to-all-start.2 = ((bf16[32,8,514]{2,1,0:T(8,128)(2,1)}), bf16[32,8,514]{2,1,0:T(8,128)(2,1)S(1)}, u32[]{:S(2)}, u32[]{:S(2)}) async-start(bf16[32,8,514]{2,1,0:T(8,128)(2,1)} %concatenate.29), calls=%async_computation.2 | async-start | bytes 655360 | tf_op jit(solution)/shard_map/all_to_all | solution.py:144
  71.3 10.7 %all-to-all-done.2 = bf16[32,8,514]{2,1,0:T(8,128)(2,1)S(1)} async-done(((bf16[32,8,514]{2,1,0:T(8,128)(2,1)}), bf16[32,8,514]{2,1,0:T(8,128)(2,1)S(1)}, u32[]{:S(2)}, u32[]{:S(2)}) %all-to-all-start.2) | async-done | bytes 263200 | tf_op jit(solution)/shard_map/all_to_all | solution.py:144
  82.2 0.1 slice_reduce_fusion
  82.3 0.6 slice_bitcast_fusion
  82.9 0.8 gather_fusion.1
  83.7 5.7 %fusion.14 = bf16[8,256,128]{2,0,1:T(8,128)(2,1)S(1)} fusion(bf16[1,256,128,128]{3,2,1,0:T(8,128)(2,1)} %param.12, bf16[256,8,128]{2,1,0:T(8,128)(2,1)S(1)} %gather_fusion.1), kind=kOutput, calls=%fused_computation.16 | convolution fusion | flops 67108864 | bytes 9437184 | tf_op jit(solution)/shard_map/dtr,trc->dtc/dot_general | solution.py:20
  89.4 0.2 convolution_bitcast_fusion
  89.7 0.1 convert_element_type.176
  89.8 0.1 reshape.240
  90.0 0.2 fusion.27
  90.2 0.2 fusion.23
  90.6 0.1 concatenate.33
  90.7 0.5 broadcast.74
  91.2 0.7 reduce.4
  91.9 0.2 reshape.267
  92.0 19.5 %all_to_all.28 = bf16[24,2,1320]{2,1,0:T(2,128)(2,1)S(1)} all-to-all(bf16[24,2,1320]{2,1,0:T(2,128)(2,1)S(1)} %reshape.267), channel_id=1, replica_groups=mesh['vert'=24,'feat'=32] {'vert'}, dimensions={0} | all-to-all | bytes 253440 | tf_op jit(solution)/shard_map/all_to_all | solution.py:177
  111.5 0.2 reshape.268
  111.9 0.7 reshape.244
  112.6 0.6 reshape.243
  113.2 0.1 reshape.241
  113.3 0.1 reshape.242
  113.4 4.2 %fusion.8 = f32[8,4096]{1,0:T(8,128)S(1)} fusion(bf16[8,1536]{1,0:T(8,128)(2,1)S(1)} %reshape.242, s32[1536]{0:T(1024)S(1)} %eq.61, f32[8,5632]{1,0:T(8,128)S(1)} %bitcast.106), kind=kOutput, calls=%fused_computation.12 | convolution fusion | flops 106987520 | bytes 292864 | tf_op jit(solution)/shard_map/dot_general | solution.py:199
  117.6 0.8 multiply_convert_fusion
  (59 shorter events, 1.2 us)
Async XLA Ops:
  0.6 63.8 %copy-start = (bf16[256,256]{1,0:T(8,128)(2,1)S(1)}, bf16[256,256]{1,0:T(8,128)(2,1)}, u32[]{:S(2)}) copy-start(bf16[256,256]{1,0:T(8,128)(2,1)} %param.17) | copy-start | bytes 393220
  0.6 24.4 %copy-start.1 = (bf16[4,8,4096]{2,1,0:T(8,128)(2,1)S(1)}, bf16[4,8,4096]{2,1,0:T(8,128)(2,1)}, u32[]{:S(2)}) copy-start(bf16[4,8,4096]{2,1,0:T(8,128)(2,1)} %param.10) | copy-start | bytes 786436
  0.7 24.2 %copy-start.5 = (s32[1,256]{1,0:T(1,128)S(1)}, s32[1,256]{1,0:T(1,128)}, u32[]{:S(2)}) copy-start(s32[1,256]{1,0:T(1,128)} %param.14) | copy-start | bytes 3076
  0.7 24.2 %copy-start.7 = (f32[8]{0:T(128)S(1)}, f32[8]{0:T(128)}, u32[]{:S(2)}) copy-start(f32[8]{0:T(128)} %param.18) | copy-start | bytes 100
  0.7 24.4 %copy-start.2 = (bf16[8,4096]{1,0:T(8,128)(2,1)S(1)}, bf16[8,4096]{1,0:T(8,128)(2,1)}, u32[]{:S(2)}) copy-start(bf16[8,4096]{1,0:T(8,128)(2,1)} %param.19) | copy-start | bytes 196612
  0.7 24.4 %copy-start.3 = (f32[4,8]{1,0:T(4,128)S(1)}, f32[4,8]{1,0:T(4,128)}, u32[]{:S(2)}) copy-start(f32[4,8]{1,0:T(4,128)} %param.11) | copy-start | bytes 388
  6.5 37.8 %copy-start.4 = (s32[1,256]{1,0:T(1,128)S(1)}, s32[1,256]{1,0:T(1,128)}, u32[]{:S(2)}) copy-start(s32[1,256]{1,0:T(1,128)} %param.13) | copy-start | bytes 3076
  7.5 27.8 %all-to-all-start = ((bf16[24,2,1024]{2,1,0:T(2,128)(2,1)}), bf16[24,2,1024]{2,1,0:T(2,128)(2,1)S(1)}, u32[]{:S(2)}, u32[]{:S(2)}) async-start(bf16[24,2,1024]{2,1,0:T(2,128)(2,1)} %reshape.265), calls=%async_computation | async-start | bytes 196608 | tf_op jit(solution)/shard_map/all_to_all | solution.py:96
  66.6 15.4 %all-to-all-start.2 = ((bf16[32,8,514]{2,1,0:T(8,128)(2,1)}), bf16[32,8,514]{2,1,0:T(8,128)(2,1)S(1)}, u32[]{:S(2)}, u32[]{:S(2)}) async-start(bf16[32,8,514]{2,1,0:T(8,128)(2,1)} %concatenate.29), calls=%async_computation.2 | async-start | bytes 655360 | tf_op jit(solution)/shard_map/all_to_all | solution.py:144
  111.8 6.6 %copy-start.6 = (f32[40]{0:T(128)}, f32[40]{0:T(128)S(1)}, u32[]{:S(2)}) copy-start(f32[40]{0:T(128)S(1)} %add_reduce_fusion.1) | copy-start | bytes 484

commit v12 on v11

--- a/solution.py
+++ b/solution.py
@@ -194,15 +194,10 @@
         axis=0,
     )
     hot = (
-        my_send.reshape(-1)[None, :] == jnp.arange(row_count, dtype=jnp.int32)[:, None]
+        my_send.reshape(-1)[:, None] == jnp.arange(row_count, dtype=jnp.int32)[None, :]
     ).astype(bf16)
-    added = lax.dot_general(
-        hot,
-        returned.reshape(channels, -1),
-        (((1,), (1,)), ((), ())),
-        preferred_element_type=f32,
-    )
-    grad_mixed = own_grad + added.T
+    added = jnp.dot(returned.reshape(channels, -1), hot, preferred_element_type=f32)
+    grad_mixed = own_grad + added
     grad_states = (depth_weight[:, :, None] * grad_mixed[None]).astype(bf16)
     return (
         layer_out,

time: 119 us -> 119 us (level)
  no operation moved by 1% of the time
where the time goes in v12:
time: 119 us
  blocking collectives  38.9 us (33%)
  matrix products  24 us (20%)
  starting transfers between devices  21.3 us (18%)
  waiting for transfers between devices  20.8 us (17%)
  local copies, waits for them, and re-layouts  9.45 us (8%)
  other arithmetic  2.67 us (2%)
  between operations  1.74 us (1%)
    all_to_all x1, blocking collectives, local(): lax.all_to_all(last_send, 'vert', split_axis=0, concat_axis=0, tiled=True)  19.5 us
    all_to_all x1, blocking collectives, local(): lax.all_to_all(first_send, 'feat', split_axis=0, concat_axis=0, tiled=True)  19.4 us
    all_to_all x1, starting transfers between devices, local(): lax.all_to_all(listed.reshape(state_count, channels, section_count, halo_...  16.7 us
    all_to_all x1, waiting for transfers between devices, local(): lax.all_to_all(second_send, 'feat', split_axis=0, concat_axis=0, tiled=True)  10.7 us
    all_to_all x1, waiting for transfers between devices, local(): lax.all_to_all(listed.reshape(state_count, channels, section_count, halo_...  10.1 us
    dot_general x1, matrix products, tile_forward(): jnp.einsum('dtc,trc->dtr', picked, tile_grp, preferred_element_type=jnp.f...  7.8 us
    dot_general x1, matrix products, tile_backward(): jnp.einsum('dtr,trc->dtc', picked, tile_grp, preferred_element_type=jnp.f...  5.65 us
    dot_general x1, matrix products, local(): jnp.dot(states.reshape(state_count * channels, row_count), pick, preferre...  4.95 us
  transfers between devices with their start and end apart: 2, of which 2 were waited for; matrix products, arithmetic and copies ran while one was open for 0% of the time, Pallas kernels for 0%

profile of v12, /device:TPU:1, one launch (start us, length us, event | category | flops | bytes accessed | tf_op | source)
XLA Modules:
  0.0 118.8 jit_solution(2097934224378207883)
XLA Ops:
  0.7 0.9 eq.63
  1.6 4.9 %fusion.10 = bf16[32,1536]{1,0:T(8,128)(2,1)S(1)} fusion(s32[1536]{0:T(1024)S(1)} %eq.63, bf16[4,8,4096]{2,1,0:T(8,128)(2,1)} %param.10), kind=kOutput, calls=%fused_computation.14 | convolution fusion | flops 408993792 | bytes 366592 | tf_op jit(solution)/shard_map/dot_general | solution.py:93
  6.5 0.2 reshape.232
  6.7 0.8 reshape.266
  7.5 16.7 %all-to-all-start = ((bf16[24,2,1024]{2,1,0:T(2,128)(2,1)}), bf16[24,2,1024]{2,1,0:T(2,128)(2,1)S(1)}, u32[]{:S(2)}, u32[]{:S(2)}) async-start(bf16[24,2,1024]{2,1,0:T(2,128)(2,1)} %reshape.266), calls=%async_computation | async-start | bytes 196608 | tf_op jit(solution)/shard_map/all_to_all | solution.py:96
  25.0 0.1 copy.98
  25.1 0.1 fusion.22
  25.2 10.1 %all-to-all-done = bf16[24,2,1024]{2,1,0:T(2,128)(2,1)S(1)} async-done(((bf16[24,2,1024]{2,1,0:T(2,128)(2,1)}), bf16[24,2,1024]{2,1,0:T(2,128)(2,1)S(1)}, u32[]{:S(2)}, u32[]{:S(2)}) %all-to-all-start) | async-done | bytes 98336 | tf_op jit(solution)/shard_map/all_to_all | solution.py:96
  35.3 0.2 reshape.267
  35.5 0.1 fusion.26
  35.6 0.1 convert_element_type.157
  35.7 0.8 gather_fusion
  36.6 7.8 %fusion.11 = bf16[8,256,128]{2,0,1:T(8,128)(2,1)S(1)} fusion(bf16[1,256,128,128]{3,2,1,0:T(8,128)(2,1)} %param.12, bf16[256,8,128]{2,1,0:T(8,128)(2,1)S(1)} %gather_fusion), kind=kOutput, calls=%fused_computation.15 | convolution fusion | flops 67108864 | bytes 9437184 | tf_op jit(solution)/shard_map/dtc,trc->dtr/dot_general | solution.py:11
  44.4 0.2 convolution_convert_fusion.1
  44.7 19.4 %all_to_all.27 = bf16[32,8,259]{2,1,0:T(8,128)(2,1)S(1)} all-to-all(bf16[32,8,259]{2,1,0:T(8,128)(2,1)S(1)} %copy.99), channel_id=1, replica_groups=mesh['vert'=24,'feat'=32] {'feat'}, dimensions={0} | all-to-all | bytes 265216 | tf_op jit(solution)/shard_map/all_to_all | solution.py:116
  64.1 0.2 add_reduce_fusion
  64.3 0.1 copy.113
  64.4 0.3 convert_reduce_fusion.1
  64.7 0.2 fusion.17
  64.9 0.2 fusion.19
  65.2 0.2 copy.106
  65.4 0.2 copy.105
  65.6 0.1 copy.100
  65.7 0.1 copy.102
  65.8 0.8 concatenate.29
  66.6 4.6 %all-to-all-start.2 = ((bf16[32,8,514]{2,1,0:T(8,128)(2,1)}), bf16[32,8,514]{2,1,0:T(8,128)(2,1)S(1)}, u32[]{:S(2)}, u32[]{:S(2)}) async-start(bf16[32,8,514]{2,1,0:T(8,128)(2,1)} %concatenate.29), calls=%async_computation.2 | async-start | bytes 655360 | tf_op jit(solution)/shard_map/all_to_all | solution.py:144
  71.3 10.7 %all-to-all-done.2 = bf16[32,8,514]{2,1,0:T(8,128)(2,1)S(1)} async-done(((bf16[32,8,514]{2,1,0:T(8,128)(2,1)}), bf16[32,8,514]{2,1,0:T(8,128)(2,1)S(1)}, u32[]{:S(2)}, u32[]{:S(2)}) %all-to-all-start.2) | async-done | bytes 263200 | tf_op jit(solution)/shard_map/all_to_all | solution.py:144
  82.2 0.1 slice_reduce_fusion
  82.3 0.6 slice_bitcast_fusion
  82.9 0.8 gather_fusion.1
  83.7 5.7 %fusion.14 = bf16[8,256,128]{2,0,1:T(8,128)(2,1)S(1)} fusion(bf16[1,256,128,128]{3,2,1,0:T(8,128)(2,1)} %param.12, bf16[256,8,128]{2,1,0:T(8,128)(2,1)S(1)} %gather_fusion.1), kind=kOutput, calls=%fused_computation.16 | convolution fusion | flops 67108864 | bytes 9437184 | tf_op jit(solution)/shard_map/dtr,trc->dtc/dot_general | solution.py:20
  89.4 0.2 convolution_bitcast_fusion
  89.7 0.1 convert_element_type.176
  89.8 0.1 reshape.241
  90.0 0.2 fusion.27
  90.2 0.2 fusion.23
  90.6 0.1 concatenate.33
  90.7 0.5 broadcast.74
  91.2 0.7 reduce.4
  91.9 0.2 reshape.268
  92.0 19.5 %all_to_all.28 = bf16[24,2,1320]{2,1,0:T(2,128)(2,1)S(1)} all-to-all(bf16[24,2,1320]{2,1,0:T(2,128)(2,1)S(1)} %reshape.268), channel_id=1, replica_groups=mesh['vert'=24,'feat'=32] {'vert'}, dimensions={0} | all-to-all | bytes 253440 | tf_op jit(solution)/shard_map/all_to_all | solution.py:177
  111.5 0.2 reshape.269
  111.9 0.7 reshape.245
  112.6 0.6 reshape.244
  113.2 0.1 reshape.242
  113.3 0.1 reshape.243
  113.4 4.6 %fusion.8 = f32[8,4096]{1,0:T(8,128)S(1)} fusion(bf16[8,1536]{1,0:T(8,128)(2,1)S(1)} %reshape.243, s32[1536]{0:T(1024)S(1)} %eq.63, f32[8,5632]{1,0:T(8,128)S(1)} %bitcast.106), kind=kOutput, calls=%fused_computation.12 | convolution fusion | flops 106987520 | bytes 292864 | tf_op jit(solution)/shard_map/dot_general | solution.py:199
  118.0 0.8 multiply_convert_fusion
  (59 shorter events, 1.2 us)
Async XLA Ops:
  0.6 63.8 %copy-start = (bf16[256,256]{1,0:T(8,128)(2,1)S(1)}, bf16[256,256]{1,0:T(8,128)(2,1)}, u32[]{:S(2)}) copy-start(bf16[256,256]{1,0:T(8,128)(2,1)} %param.17) | copy-start | bytes 393220
  0.6 24.4 %copy-start.1 = (bf16[4,8,4096]{2,1,0:T(8,128)(2,1)S(1)}, bf16[4,8,4096]{2,1,0:T(8,128)(2,1)}, u32[]{:S(2)}) copy-start(bf16[4,8,4096]{2,1,0:T(8,128)(2,1)} %param.10) | copy-start | bytes 786436
  0.7 24.2 %copy-start.5 = (s32[1,256]{1,0:T(1,128)S(1)}, s32[1,256]{1,0:T(1,128)}, u32[]{:S(2)}) copy-start(s32[1,256]{1,0:T(1,128)} %param.14) | copy-start | bytes 3076
  0.7 24.2 %copy-start.7 = (f32[8]{0:T(128)S(1)}, f32[8]{0:T(128)}, u32[]{:S(2)}) copy-start(f32[8]{0:T(128)} %param.18) | copy-start | bytes 100
  0.7 24.4 %copy-start.2 = (bf16[8,4096]{1,0:T(8,128)(2,1)S(1)}, bf16[8,4096]{1,0:T(8,128)(2,1)}, u32[]{:S(2)}) copy-start(bf16[8,4096]{1,0:T(8,128)(2,1)} %param.19) | copy-start | bytes 196612
  0.7 24.4 %copy-start.3 = (f32[4,8]{1,0:T(4,128)S(1)}, f32[4,8]{1,0:T(4,128)}, u32[]{:S(2)}) copy-start(f32[4,8]{1,0:T(4,128)} %param.11) | copy-start | bytes 388
  6.5 37.8 %copy-start.4 = (s32[1,256]{1,0:T(1,128)S(1)}, s32[1,256]{1,0:T(1,128)}, u32[]{:S(2)}) copy-start(s32[1,256]{1,0:T(1,128)} %param.13) | copy-start | bytes 3076
  7.5 27.8 %all-to-all-start = ((bf16[24,2,1024]{2,1,0:T(2,128)(2,1)}), bf16[24,2,1024]{2,1,0:T(2,128)(2,1)S(1)}, u32[]{:S(2)}, u32[]{:S(2)}) async-start(bf16[24,2,1024]{2,1,0:T(2,128)(2,1)} %reshape.266), calls=%async_computation | async-start | bytes 196608 | tf_op jit(solution)/shard_map/all_to_all | solution.py:96
  66.6 15.4 %all-to-all-start.2 = ((bf16[32,8,514]{2,1,0:T(8,128)(2,1)}), bf16[32,8,514]{2,1,0:T(8,128)(2,1)S(1)}, u32[]{:S(2)}, u32[]{:S(2)}) async-start(bf16[32,8,514]{2,1,0:T(8,128)(2,1)} %concatenate.29), calls=%async_computation.2 | async-start | bytes 655360 | tf_op jit(solution)/shard_map/all_to_all | solution.py:144
  111.8 7.0 %copy-start.6 = (f32[40]{0:T(128)}, f32[40]{0:T(128)S(1)}, u32[]{:S(2)}) copy-start(f32[40]{0:T(128)S(1)} %add_reduce_fusion.1) | copy-start | bytes 484

commit v13 on v11

--- a/solution.py
+++ b/solution.py
@@ -109,15 +109,21 @@
     )
     aggregated = aggregated.reshape(channels, row_count).astype(bf16)
 
-    bias_cols = jnp.broadcast_to(
-        jnp.stack(bf16_parts(bias_vec, 3), axis=1)[None], (feat_count, channels, 3)
-    )
-    first_send = jnp.concatenate([to_blocks(aggregated), to_blocks(cotangent), bias_cols], axis=2)
+    bias_row = jnp.stack(bf16_parts(bias_vec, 3), axis=1).reshape(-1)
+    bias_row = jnp.pad(bias_row, (0, 2 * col_width - bias_row.shape[0]))
+    first_send = jnp.concatenate(
+        [
+            jnp.concatenate([to_blocks(aggregated), to_blocks(cotangent)], axis=2),
+            jnp.broadcast_to(bias_row[None, None, :], (feat_count, 1, 2 * col_width)),
+        ],
+        axis=1,
+    )
     first_recv = lax.all_to_all(first_send, "feat", split_axis=0, concat_axis=0, tiled=True)
-    first_recv = first_recv.reshape(feat_count * channels, -1)
-    agg_block = first_recv[:, :col_width]
-    cot_block = first_recv[:, col_width : 2 * col_width].astype(f32)
-    bias_full = parts_sum([first_recv[:, 2 * col_width + n] for n in range(3)])
+    block_rows = first_recv[:, :channels, :].reshape(feat_count * channels, -1)
+    agg_block = block_rows[:, :col_width]
+    cot_block = block_rows[:, col_width:].astype(f32)
+    bias_parts = first_recv[:, channels, : channels * 3].reshape(feat_count * channels, 3)
+    bias_full = parts_sum([bias_parts[:, n] for n in range(3)])
 
     pre_act = lax.dot_general(
         weight, agg_block, (((0,), (0,)), ((), ())), preferred_element_type=f32

time: 119 us -> 121 us (1.017)
    all_to_all x1, blocking collectives: 19.4 us -> 20.7 us  [local(): lax.all_to_all(first_send, 'feat', split_axis=0, concat_axis=0, tiled=True)]
where the time goes in v13:
time: 121 us; the launch traced here: 120 us
  blocking collectives  39.7 us (33%)
  matrix products  23.6 us (20%)
  starting transfers between devices  21.6 us (18%)
  waiting for transfers between devices  20.9 us (17%)
  local copies, waits for them, and re-layouts  9.73 us (8%)
  other arithmetic  2.66 us (2%)
  between operations  1.77 us (1%)
    all_to_all x1, blocking collectives, local(): lax.all_to_all(first_send, 'feat', split_axis=0, concat_axis=0, tiled=True)  20.7 us
    all_to_all x1, blocking collectives, local(): lax.all_to_all(last_send, 'vert', split_axis=0, concat_axis=0, tiled=True)  19.1 us
    all_to_all x1, starting transfers between devices, local(): lax.all_to_all(listed.reshape(state_count, channels, section_count, halo_...  16.7 us
    all_to_all x1, waiting for transfers between devices, local(): lax.all_to_all(second_send, 'feat', split_axis=0, concat_axis=0, tiled=True)  11 us
    all_to_all x1, waiting for transfers between devices, local(): lax.all_to_all(listed.reshape(state_count, channels, section_count, halo_...  9.95 us
    dot_general x1, matrix products, tile_forward(): jnp.einsum('dtc,trc->dtr', picked, tile_grp, preferred_element_type=jnp.f...  7.8 us
    dot_general x1, matrix products, tile_backward(): jnp.einsum('dtr,trc->dtc', picked, tile_grp, preferred_element_type=jnp.f...  5.65 us
    dot_general x1, matrix products, local(): jnp.dot(states.reshape(state_count * channels, row_count), pick, preferre...  4.95 us
  transfers between devices with their start and end apart: 2, of which 2 were waited for; matrix products, arithmetic and copies ran while one was open for 0% of the time, Pallas kernels for 0%

profile of v13, /device:TPU:1, one launch (start us, length us, event | category | flops | bytes accessed | tf_op | source)
XLA Modules:
  0.0 120.1 jit_solution(10736219867646737403)
XLA Ops:
  0.7 0.9 eq.61
  1.6 4.9 %fusion.10 = bf16[32,1536]{1,0:T(8,128)(2,1)S(1)} fusion(s32[1536]{0:T(1024)S(1)} %eq.61, bf16[4,8,4096]{2,1,0:T(8,128)(2,1)} %param.10), kind=kOutput, calls=%fused_computation.14 | convolution fusion | flops 408993792 | bytes 366592 | tf_op jit(solution)/shard_map/dot_general | solution.py:93
  6.5 0.2 reshape.236
  6.7 0.8 reshape.272
  7.5 16.7 %all-to-all-start = ((bf16[24,2,1024]{2,1,0:T(2,128)(2,1)}), bf16[24,2,1024]{2,1,0:T(2,128)(2,1)S(1)}, u32[]{:S(2)}, u32[]{:S(2)}) async-start(bf16[24,2,1024]{2,1,0:T(2,128)(2,1)} %reshape.272), calls=%async_computation | async-start | bytes 196608 | tf_op jit(solution)/shard_map/all_to_all | solution.py:96
  25.0 0.1 copy.98
  25.2 0.1 fusion.22
  25.3 10.0 %all-to-all-done = bf16[24,2,1024]{2,1,0:T(2,128)(2,1)S(1)} async-done(((bf16[24,2,1024]{2,1,0:T(2,128)(2,1)}), bf16[24,2,1024]{2,1,0:T(2,128)(2,1)S(1)}, u32[]{:S(2)}, u32[]{:S(2)}) %all-to-all-start) | async-done | bytes 98336 | tf_op jit(solution)/shard_map/all_to_all | solution.py:96
  35.3 0.2 reshape.273
  35.5 0.1 fusion.26
  35.6 0.1 convert_element_type.159
  35.7 0.8 gather_fusion
  36.6 7.8 %fusion.11 = bf16[8,256,128]{2,0,1:T(8,128)(2,1)S(1)} fusion(bf16[1,256,128,128]{3,2,1,0:T(8,128)(2,1)} %param.12, bf16[256,8,128]{2,1,0:T(8,128)(2,1)S(1)} %gather_fusion), kind=kOutput, calls=%fused_computation.15 | convolution fusion | flops 67108864 | bytes 9437184 | tf_op jit(solution)/shard_map/dtc,trc->dtr/dot_general | solution.py:11
  44.4 0.2 convolution_convert_fusion.1
  44.7 20.7 %all_to_all.27 = bf16[32,9,256]{2,1,0:T(8,128)(2,1)S(1)} all-to-all(bf16[32,9,256]{2,1,0:T(8,128)(2,1)S(1)} %copy.99), channel_id=1, replica_groups=mesh['vert'=24,'feat'=32] {'feat'}, dimensions={0} | all-to-all | bytes 294912 | tf_op jit(solution)/shard_map/all_to_all | solution.py:121
  65.4 0.1 reshape_squeeze.3
  65.5 0.2 add_reduce_fusion
  65.8 0.1 copy.113
  65.9 0.3 convert_reduce_fusion.1
  66.1 0.2 fusion.17
  66.3 0.2 fusion.19
  66.7 0.2 copy.106
  66.9 0.2 copy.105
  67.0 0.1 copy.100
  67.1 0.1 copy.102
  67.2 0.8 concatenate.33
  68.1 4.9 %all-to-all-start.2 = ((bf16[32,8,514]{2,1,0:T(8,128)(2,1)}), bf16[32,8,514]{2,1,0:T(8,128)(2,1)S(1)}, u32[]{:S(2)}, u32[]{:S(2)}) async-start(bf16[32,8,514]{2,1,0:T(8,128)(2,1)} %concatenate.33), calls=%async_computation.2 | async-start | bytes 655360 | tf_op jit(solution)/shard_map/all_to_all | solution.py:150
  73.1 11.0 %all-to-all-done.2 = bf16[32,8,514]{2,1,0:T(8,128)(2,1)S(1)} async-done(((bf16[32,8,514]{2,1,0:T(8,128)(2,1)}), bf16[32,8,514]{2,1,0:T(8,128)(2,1)S(1)}, u32[]{:S(2)}, u32[]{:S(2)}) %all-to-all-start.2) | async-done | bytes 263200 | tf_op jit(solution)/shard_map/all_to_all | solution.py:150
  84.2 0.1 slice_reduce_fusion.1
  84.3 0.6 slice_bitcast_fusion.1
  85.0 0.8 gather_fusion.1
  85.8 5.7 %fusion.14 = bf16[8,256,128]{2,0,1:T(8,128)(2,1)S(1)} fusion(bf16[1,256,128,128]{3,2,1,0:T(8,128)(2,1)} %param.12, bf16[256,8,128]{2,1,0:T(8,128)(2,1)S(1)} %gather_fusion.1), kind=kOutput, calls=%fused_computation.16 | convolution fusion | flops 67108864 | bytes 9437184 | tf_op jit(solution)/shard_map/dtr,trc->dtc/dot_general | solution.py:20
  91.5 0.2 convolution_bitcast_fusion
  91.8 0.1 convert_element_type.178
  91.9 0.1 reshape.246
  92.1 0.2 fusion.27
  92.3 0.2 fusion.23
  92.7 0.5 broadcast.78
  93.2 0.7 reduce.6
  93.9 0.2 reshape.274
  94.1 19.1 %all_to_all.28 = bf16[24,2,1320]{2,1,0:T(2,128)(2,1)S(1)} all-to-all(bf16[24,2,1320]{2,1,0:T(2,128)(2,1)S(1)} %reshape.274), channel_id=1, replica_groups=mesh['vert'=24,'feat'=32] {'vert'}, dimensions={0} | all-to-all | bytes 253440 | tf_op jit(solution)/shard_map/all_to_all | solution.py:183
  113.2 0.2 reshape.275
  113.6 0.7 reshape.250
  114.3 0.6 reshape.249
  114.9 0.1 reshape.247
  115.0 0.1 reshape.248
  115.1 4.2 %fusion.8 = f32[8,4096]{1,0:T(8,128)S(1)} fusion(bf16[8,1536]{1,0:T(8,128)(2,1)S(1)} %reshape.248, s32[1536]{0:T(1024)S(1)} %eq.61, f32[8,5632]{1,0:T(8,128)S(1)} %bitcast.103), kind=kOutput, calls=%fused_computation.12 | convolution fusion | flops 106987520 | bytes 292864 | tf_op jit(solution)/shard_map/dot_general | solution.py:205
  119.3 0.8 multiply_convert_fusion
  (64 shorter events, 1.5 us)
Async XLA Ops:
  0.6 65.2 %copy-start = (bf16[256,256]{1,0:T(8,128)(2,1)S(1)}, bf16[256,256]{1,0:T(8,128)(2,1)}, u32[]{:S(2)}) copy-start(bf16[256,256]{1,0:T(8,128)(2,1)} %param.17) | copy-start | bytes 393220
  0.6 24.6 %copy-start.1 = (bf16[4,8,4096]{2,1,0:T(8,128)(2,1)S(1)}, bf16[4,8,4096]{2,1,0:T(8,128)(2,1)}, u32[]{:S(2)}) copy-start(bf16[4,8,4096]{2,1,0:T(8,128)(2,1)} %param.10) | copy-start | bytes 786436
  0.7 24.2 %copy-start.5 = (s32[1,256]{1,0:T(1,128)S(1)}, s32[1,256]{1,0:T(1,128)}, u32[]{:S(2)}) copy-start(s32[1,256]{1,0:T(1,128)} %param.14) | copy-start | bytes 3076
  0.7 24.2 %copy-start.7 = (f32[8]{0:T(128)S(1)}, f32[8]{0:T(128)}, u32[]{:S(2)}) copy-start(f32[8]{0:T(128)} %param.18) | copy-start | bytes 100
  0.7 24.5 %copy-start.2 = (bf16[8,4096]{1,0:T(8,128)(2,1)S(1)}, bf16[8,4096]{1,0:T(8,128)(2,1)}, u32[]{:S(2)}) copy-start(bf16[8,4096]{1,0:T(8,128)(2,1)} %param.19) | copy-start | bytes 196612
  0.7 24.5 %copy-start.3 = (f32[4,8]{1,0:T(4,128)S(1)}, f32[4,8]{1,0:T(4,128)}, u32[]{:S(2)}) copy-start(f32[4,8]{1,0:T(4,128)} %param.11) | copy-start | bytes 388
  6.5 37.8 %copy-start.4 = (s32[1,256]{1,0:T(1,128)S(1)}, s32[1,256]{1,0:T(1,128)}, u32[]{:S(2)}) copy-start(s32[1,256]{1,0:T(1,128)} %param.13) | copy-start | bytes 3076
  7.5 27.8 %all-to-all-start = ((bf16[24,2,1024]{2,1,0:T(2,128)(2,1)}), bf16[24,2,1024]{2,1,0:T(2,128)(2,1)S(1)}, u32[]{:S(2)}, u32[]{:S(2)}) async-start(bf16[24,2,1024]{2,1,0:T(2,128)(2,1)} %reshape.272), calls=%async_computation | async-start | bytes 196608 | tf_op jit(solution)/shard_map/all_to_all | solution.py:96
  68.1 16.0 %all-to-all-start.2 = ((bf16[32,8,514]{2,1,0:T(8,128)(2,1)}), bf16[32,8,514]{2,1,0:T(8,128)(2,1)S(1)}, u32[]{:S(2)}, u32[]{:S(2)}) async-start(bf16[32,8,514]{2,1,0:T(8,128)(2,1)} %concatenate.33), calls=%async_computation.2 | async-start | bytes 655360 | tf_op jit(solution)/shard_map/all_to_all | solution.py:150
  113.5 6.6 %copy-start.6 = (f32[40]{0:T(128)}, f32[40]{0:T(128)S(1)}, u32[]{:S(2)}) copy-start(f32[40]{0:T(128)S(1)} %add_reduce_fusion.1) | copy-start | bytes 484

commit v14 on v11

--- a/solution.py
+++ b/solution.py
@@ -132,23 +132,34 @@
     )
     bias_terms = jnp.sum(grad_pre.astype(f32), axis=1)
 
+    main_cols = 2 * col_width + width
+    bias_row = jnp.concatenate(bf16_parts(bias_terms.reshape(feat_count, channels), 2), axis=1)
+    bias_row = jnp.pad(bias_row, ((0, 0), (0, main_cols - 2 * channels)))
     second_send = jnp.concatenate(
         [
-            out_block.reshape(feat_count, channels, col_width),
-            grad_agg_block.reshape(feat_count, channels, col_width),
-            weight_terms.reshape(feat_count, channels, width).astype(bf16),
+            jnp.concatenate(
+                [
+                    out_block.reshape(feat_count, channels, col_width),
+                    grad_agg_block.reshape(feat_count, channels, col_width),
+                    weight_terms.reshape(feat_count, channels, width).astype(bf16),
+                ],
+                axis=2,
+            ),
+            bias_row[:, None, :],
+        ],
+        axis=1,
+    )
+    second_recv = lax.all_to_all(second_send, "feat", split_axis=0, concat_axis=0, tiled=True)
+    layer_out = from_blocks(second_recv[:, :channels, :col_width])
+    grad_agg = from_blocks(second_recv[:, :channels, col_width : 2 * col_width])
+    start = 2 * col_width
+    weight_part = second_recv[:, :channels, start : start + width].astype(f32)
+    bias_part = parts_sum(
+        [
+            second_recv[:, channels, :channels],
+            second_recv[:, channels, channels : 2 * channels],
         ]
-        + bf16_parts(bias_terms.reshape(feat_count, channels, 1), 2),
-        axis=2,
-    )
-    second_recv = lax.all_to_all(second_send, "feat", split_axis=0, concat_axis=0, tiled=True)
-    layer_out = from_blocks(second_recv[:, :, :col_width])
-    grad_agg = from_blocks(second_recv[:, :, col_width : 2 * col_width])
-    start = 2 * col_width
-    weight_part = second_recv[:, :, start : start + width].astype(f32)
-    bias_part = parts_sum(
-        [second_recv[:, :, start + width : start + width + 1], second_recv[:, :, start + width + 1 :]]
-    )
+    )[:, :, None]
     panel_terms = jnp.sum(jnp.concatenate([weight_part, bias_part], axis=2), axis=0)
 
     grad_blocks = grad_agg.reshape(channels, row_blocks, block_size)

time: 119 us -> 123 us (1.034)
  waiting for transfers between devices: 20.8 us -> 25 us
    all_to_all x1, waiting for transfers between devices: 10.7 us -> 14.9 us  [local(): lax.all_to_all(second_send, 'feat', split_axis=0, concat_axis=0, tiled=True)]
where the time goes in v14:
time: 123 us
  blocking collectives  38.7 us (31%)
  waiting for transfers between devices  25 us (20%)
  matrix products  23.6 us (19%)
  starting transfers between devices  21.3 us (17%)
  local copies, waits for them, and re-layouts  8.69 us (7%)
  other arithmetic  3.56 us (3%)
  between operations  1.75 us (1%)
    all_to_all x1, blocking collectives, local(): lax.all_to_all(first_send, 'feat', split_axis=0, concat_axis=0, tiled=True)  19.4 us
    all_to_all x1, blocking collectives, local(): lax.all_to_all(last_send, 'vert', split_axis=0, concat_axis=0, tiled=True)  19.3 us
    all_to_all x1, starting transfers between devices, local(): lax.all_to_all(listed.reshape(state_count, channels, section_count, halo_...  16.7 us
    all_to_all x1, waiting for transfers between devices, local(): lax.all_to_all(second_send, 'feat', split_axis=0, concat_axis=0, tiled=True)  14.9 us
    all_to_all x1, waiting for transfers between devices, local(): lax.all_to_all(listed.reshape(state_count, channels, section_count, halo_...  10.1 us
    dot_general x1, matrix products, tile_forward(): jnp.einsum('dtc,trc->dtr', picked, tile_grp, preferred_element_type=jnp.f...  7.8 us
    dot_general x1, matrix products, tile_backward(): jnp.einsum('dtr,trc->dtc', picked, tile_grp, preferred_element_type=jnp.f...  5.65 us
    dot_general x1, matrix products, local(): jnp.dot(states.reshape(state_count * channels, row_count), pick, preferre...  4.95 us
  transfers between devices with their start and end apart: 2, of which 2 were waited for; matrix products, arithmetic and copies ran while one was open for 0% of the time, Pallas kernels for 0%

profile of v14, /device:TPU:1, one launch (start us, length us, event | category | flops | bytes accessed | tf_op | source)
XLA Modules:
  0.0 122.7 jit_solution(13901358081516477272)
XLA Ops:
  0.7 0.9 eq.61
  1.6 4.9 %fusion.10 = bf16[32,1536]{1,0:T(8,128)(2,1)S(1)} fusion(s32[1536]{0:T(1024)S(1)} %eq.61, bf16[4,8,4096]{2,1,0:T(8,128)(2,1)} %param.10), kind=kOutput, calls=%fused_computation.14 | convolution fusion | flops 408993792 | bytes 366592 | tf_op jit(solution)/shard_map/dot_general | solution.py:93
  6.5 0.2 reshape.221
  6.7 0.8 reshape.255
  7.5 16.7 %all-to-all-start = ((bf16[24,2,1024]{2,1,0:T(2,128)(2,1)}), bf16[24,2,1024]{2,1,0:T(2,128)(2,1)S(1)}, u32[]{:S(2)}, u32[]{:S(2)}) async-start(bf16[24,2,1024]{2,1,0:T(2,128)(2,1)} %reshape.255), calls=%async_computation | async-start | bytes 196608 | tf_op jit(solution)/shard_map/all_to_all | solution.py:96
  25.0 0.1 copy.163
  25.1 0.1 fusion.22
  25.2 10.1 %all-to-all-done = bf16[24,2,1024]{2,1,0:T(2,128)(2,1)S(1)} async-done(((bf16[24,2,1024]{2,1,0:T(2,128)(2,1)}), bf16[24,2,1024]{2,1,0:T(2,128)(2,1)S(1)}, u32[]{:S(2)}, u32[]{:S(2)}) %all-to-all-start) | async-done | bytes 98336 | tf_op jit(solution)/shard_map/all_to_all | solution.py:96
  35.3 0.2 reshape.256
  35.5 0.1 fusion.26
  35.6 0.1 convert_element_type.159
  35.7 0.8 gather_fusion
  36.6 7.8 %fusion.11 = bf16[8,256,128]{2,0,1:T(8,128)(2,1)S(1)} fusion(bf16[1,256,128,128]{3,2,1,0:T(8,128)(2,1)} %param.12, bf16[256,8,128]{2,1,0:T(8,128)(2,1)S(1)} %gather_fusion), kind=kOutput, calls=%fused_computation.15 | convolution fusion | flops 67108864 | bytes 9437184 | tf_op jit(solution)/shard_map/dtc,trc->dtr/dot_general | solution.py:11
  44.4 0.2 convolution_convert_fusion.1
  44.7 19.4 %all_to_all.27 = bf16[32,8,259]{2,1,0:T(8,128)(2,1)S(1)} all-to-all(bf16[32,8,259]{2,1,0:T(8,128)(2,1)S(1)} %copy.164), channel_id=1, replica_groups=mesh['vert'=24,'feat'=32] {'feat'}, dimensions={0} | all-to-all | bytes 265216 | tf_op jit(solution)/shard_map/all_to_all | solution.py:116
  64.1 0.2 add_reduce_fusion
  64.3 0.1 copy.178
  64.4 0.3 convert_reduce_fusion.1
  64.7 0.2 fusion.17
  64.9 0.2 fusion.19
  65.3 0.1 copy.165
  65.4 0.1 copy.167
  65.6 0.9 pad_maximum_fusion
  66.4 4.6 %all-to-all-start.2 = ((bf16[32,9,512]{2,1,0:T(8,128)(2,1)}), bf16[32,9,512]{2,1,0:T(8,128)(2,1)S(1)}, u32[]{:S(2)}, u32[]{:S(2)}) async-start(bf16[32,9,512]{2,1,0:T(8,128)(2,1)} %pad_maximum_fusion), calls=%async_computation.2 | async-start | bytes 1048576 | tf_op jit(solution)/shard_map/all_to_all | solution.py:152
  71.1 14.9 %all-to-all-done.2 = bf16[32,9,512]{2,1,0:T(8,128)(2,1)S(1)} async-done(((bf16[32,9,512]{2,1,0:T(8,128)(2,1)}), bf16[32,9,512]{2,1,0:T(8,128)(2,1)S(1)}, u32[]{:S(2)}, u32[]{:S(2)}) %all-to-all-start.2) | async-done | bytes 294944 | tf_op jit(solution)/shard_map/all_to_all | solution.py:152
  86.3 0.1 copy.173
  86.5 0.1 slice_reduce_fusion
  86.6 0.7 slice_bitcast_fusion
  87.3 0.8 gather_fusion.1
  88.1 5.7 %fusion.14 = bf16[8,256,128]{2,0,1:T(8,128)(2,1)S(1)} fusion(bf16[1,256,128,128]{3,2,1,0:T(8,128)(2,1)} %param.12, bf16[256,8,128]{2,1,0:T(8,128)(2,1)S(1)} %gather_fusion.1), kind=kOutput, calls=%fused_computation.16 | convolution fusion | flops 67108864 | bytes 9437184 | tf_op jit(solution)/shard_map/dtr,trc->dtc/dot_general | solution.py:20
  93.8 0.2 convolution_bitcast_fusion
  94.1 0.1 convert_element_type.178
  94.2 0.1 reshape.230
  94.4 0.2 fusion.27
  94.6 0.2 fusion.23
  94.9 0.1 concatenate.41
  95.0 0.5 broadcast.82
  95.6 0.7 reduce.4
  96.2 0.2 reshape.257
  96.4 19.3 %all_to_all.28 = bf16[24,2,1320]{2,1,0:T(2,128)(2,1)S(1)} all-to-all(bf16[24,2,1320]{2,1,0:T(2,128)(2,1)S(1)} %reshape.257), channel_id=1, replica_groups=mesh['vert'=24,'feat'=32] {'vert'}, dimensions={0} | all-to-all | bytes 253440 | tf_op jit(solution)/shard_map/all_to_all | solution.py:188
  115.8 0.2 reshape.258
  116.0 0.1 add_reduce_fusion.1
  116.2 0.7 reshape.234
  116.8 0.6 reshape.233
  117.4 0.1 reshape.231
  117.6 0.1 reshape.232
  117.7 4.2 %fusion.8 = f32[8,4096]{1,0:T(8,128)S(1)} fusion(bf16[8,1536]{1,0:T(8,128)(2,1)S(1)} %reshape.232, s32[1536]{0:T(1024)S(1)} %eq.61, f32[8,5632]{1,0:T(8,128)S(1)} %bitcast.110), kind=kOutput, calls=%fused_computation.12 | convolution fusion | flops 106987520 | bytes 292864 | tf_op jit(solution)/shard_map/dot_general | solution.py:210
  121.9 0.8 multiply_convert_fusion
  (62 shorter events, 1.3 us)
Async XLA Ops:
  0.6 63.8 %copy-start = (bf16[256,256]{1,0:T(8,128)(2,1)S(1)}, bf16[256,256]{1,0:T(8,128)(2,1)}, u32[]{:S(2)}) copy-start(bf16[256,256]{1,0:T(8,128)(2,1)} %param.17) | copy-start | bytes 393220
  0.6 24.4 %copy-start.1 = (bf16[4,8,4096]{2,1,0:T(8,128)(2,1)S(1)}, bf16[4,8,4096]{2,1,0:T(8,128)(2,1)}, u32[]{:S(2)}) copy-start(bf16[4,8,4096]{2,1,0:T(8,128)(2,1)} %param.10) | copy-start | bytes 786436
  0.7 24.2 %copy-start.5 = (s32[1,256]{1,0:T(1,128)S(1)}, s32[1,256]{1,0:T(1,128)}, u32[]{:S(2)}) copy-start(s32[1,256]{1,0:T(1,128)} %param.14) | copy-start | bytes 3076
  0.7 24.2 %copy-start.7 = (f32[8]{0:T(128)S(1)}, f32[8]{0:T(128)}, u32[]{:S(2)}) copy-start(f32[8]{0:T(128)} %param.18) | copy-start | bytes 100
  0.7 24.4 %copy-start.2 = (bf16[8,4096]{1,0:T(8,128)(2,1)S(1)}, bf16[8,4096]{1,0:T(8,128)(2,1)}, u32[]{:S(2)}) copy-start(bf16[8,4096]{1,0:T(8,128)(2,1)} %param.19) | copy-start | bytes 196612
  0.7 24.4 %copy-start.3 = (f32[4,8]{1,0:T(4,128)S(1)}, f32[4,8]{1,0:T(4,128)}, u32[]{:S(2)}) copy-start(f32[4,8]{1,0:T(4,128)} %param.11) | copy-start | bytes 388
  6.5 37.8 %copy-start.4 = (s32[1,256]{1,0:T(1,128)S(1)}, s32[1,256]{1,0:T(1,128)}, u32[]{:S(2)}) copy-start(s32[1,256]{1,0:T(1,128)} %param.13) | copy-start | bytes 3076
  7.5 27.8 %all-to-all-start = ((bf16[24,2,1024]{2,1,0:T(2,128)(2,1)}), bf16[24,2,1024]{2,1,0:T(2,128)(2,1)S(1)}, u32[]{:S(2)}, u32[]{:S(2)}) async-start(bf16[24,2,1024]{2,1,0:T(2,128)(2,1)} %reshape.255), calls=%async_computation | async-start | bytes 196608 | tf_op jit(solution)/shard_map/all_to_all | solution.py:96
  66.4 19.6 %all-to-all-start.2 = ((bf16[32,9,512]{2,1,0:T(8,128)(2,1)}), bf16[32,9,512]{2,1,0:T(8,128)(2,1)S(1)}, u32[]{:S(2)}, u32[]{:S(2)}) async-start(bf16[32,9,512]{2,1,0:T(8,128)(2,1)} %pad_maximum_fusion), calls=%async_computation.2 | async-start | bytes 1048576 | tf_op jit(solution)/shard_map/all_to_all | solution.py:152
  116.1 6.6 %copy-start.6 = (f32[40]{0:T(128)}, f32[40]{0:T(128)S(1)}, u32[]{:S(2)}) copy-start(f32[40]{0:T(128)S(1)} %add_reduce_fusion.1) | copy-start | bytes 484
